TPU v7x, 1024 devices: a whole 4x8x16 slice. The times are simulated.
1024 devices in a mesh: dp: 8 (over y), seq: 16 (over z), head: 8 (over x, core).
Axes of the slice: x: 4, y: 8, z: 16, core: 2. Of those that a mesh axis runs over, the one named last changes fastest.
Arguments:
- stream: bfloat16 [16384, 2048], P(('dp', 'seq')), parts along dimension 0, may hold values from -40 to 40
- queries: bfloat16 [16384, 2048], P(('dp', 'seq'), 'head'), parts along dimension 0, may hold values from -6 to 6
- keys: bfloat16 [16384, 2048], P(('dp', 'seq'), 'head'), parts along dimension 0, may hold values from -6 to 6
- values: bfloat16 [16384, 4096], P(('dp', 'seq'), 'head'), parts along dimension 0, may hold values from -6 to 6
- out_gate: bfloat16 [16384, 4096], P(('dp', 'seq'), 'head'), parts along dimension 0, may hold values from -6 to 6
- gates: float32 [16384, 32], P(('dp', 'seq'), 'head'), parts along dimension 0, may hold values from 0.25 to 1
- betas: float32 [16384, 32], P(('dp', 'seq'), 'head'), parts along dimension 0, may hold values from 0.01 to 0.08
- init_state: float32 [256, 128, 128], P(('dp', 'head')), parts along dimension 0, may hold values from -1.5 to 1.5
- norm_gain: float32 [128], replicated, may hold values from 0.5 to 1.5
- out_proj: bfloat16 [4096, 2048], P('head'), may hold values from -0.09375 to 0.09375
- post_gain: float32 [2048], replicated, may hold values from 0.5 to 1.5
- expert_ids: int32 [16384, 10], P(('dp', 'seq')), parts along dimension 0, may hold values from 0 to 127, all different within a row; in each aligned block of 128 rows (0 to 127, 128 to 255, ...) at most 20 rows name the same one
- route_scores: float32 [16384, 10], P(('dp', 'seq')), parts along dimension 0, may hold values from 0.05 to 1
- w_gate: bfloat16 [128, 2048, 512], P(('seq', 'head')), may hold values from -0.125 to 0.125
- w_up: bfloat16 [128, 2048, 512], P(('seq', 'head')), may hold values from -0.125 to 0.125
- w_down: bfloat16 [128, 512, 2048], P(('seq', 'head')), may hold values from -0.5 to 0.5
Outputs:
- layer_out: bfloat16 [16384, 2048], P(('dp', 'seq'), 'head'), parts along dimension 0
There are 8 independent parts, one for each index of `dp`. A program takes and returns all parts, laid end to end along the dimension named above; an argument that names none is the same for every part. Nothing has to cross between parts.
Inputs may be any that keep to these rules, and one draw needn't show every extreme that they name: `expert_ids`: in each aligned block of 128 rows (the rows of one index of seq) no expert is named by more than 20 rows, a bound that some block reaches; the 10 experts of a row differ.
All inputs are finite; a program needn't handle non-finite values.
Results may differ from a plain program's by a relative error of at most 0.0095.
Values may be sent and summed in bfloat16 or wider, within the bound.
No kernel may reach another device: no remote copies, remote signals or barrier semaphores. Data moves between devices by JAX's collectives and lax.ppermute only.
A program may use at most 64 MiB of HBM per device.

v0:
```python
import jax
import jax.numpy as jnp
from jax import lax
from jax.sharding import PartitionSpec as P

VALUE_HEAD_COUNT = 32
QK_HEADS = 16
DK = 128
DV = 128


precise_variant = lax.Precision.HIGHEST


def prefix(array, axis, combine, identity):
    size, position = (lax.axis_size(axis), lax.axis_index(axis))
    everything = jax.tree.map(
        lambda part, kind: lax.all_gather(part.astype(kind), axis),
        array,
        (jnp.bfloat16, jnp.bfloat16),
    )
    start = jax.tree.map(
        lambda part, zero: jnp.broadcast_to(jnp.asarray(zero, part.dtype), part.shape),
        array,
        identity,
    )

    def lap(k, before):
        reached = k < position
        new = combine(
            before, jax.tree.map(lambda part, own: part[k].astype(own.dtype), everything, array)
        )
        return jax.tree.map(lambda a, b: jnp.where(reached, a, b), new, before)

    return lax.fori_loop(0, size, lap, start)


def unit_rows(matrix):
    return matrix * lax.rsqrt(jnp.sum(matrix * matrix, axis=-1, keepdims=True) + 1e-06)


def batch_product(left, right):
    return jnp.einsum("hij,hjk->hik", left, right, precision=precise_variant)


def on_device(
    stream,
    queries,
    keys,
    values,
    out_gate,
    gates,
    betas,
    init_state,
    norm_gain,
    out_proj,
    post_gain,
    expert_ids,
    route_scores,
    w_gate,
    w_up,
    w_down,
):
    length = stream.shape[0]
    model_width = stream.shape[1]
    head_count = values.shape[1] // DV
    group_size = VALUE_HEAD_COUNT // QK_HEADS
    scaled_q = unit_rows(queries.astype(jnp.float32).reshape(length, -1, DK)) * DK ** (-0.5)
    query_head_rows = jnp.repeat(scaled_q, group_size, axis=1).transpose(1, 0, 2)
    unit_k = unit_rows(keys.astype(jnp.float32).reshape(length, -1, DK))
    key_heads = jnp.repeat(unit_k, group_size, axis=1).transpose(1, 0, 2)
    value_heads = values.astype(jnp.float32).reshape(length, head_count, DV).transpose(1, 0, 2)
    beta_heads = betas.T
    log_decay = jnp.cumsum(jnp.log(gates), axis=0).T
    row_index = lax.broadcasted_iota(jnp.int32, (length, length), 0)
    col_index = lax.broadcasted_iota(jnp.int32, (length, length), 1)
    lower = row_index >= col_index
    strict = row_index > col_index
    gap_log = log_decay[:, :, None] - log_decay[:, None, :]
    decay = jnp.where(lower, jnp.exp(jnp.where(lower, gap_log, 0.0)), 0.0)
    key_inner = jnp.einsum("htk,hsk->hts", key_heads, key_heads, precision=precise_variant)
    tri_matrix = jnp.where(strict, decay * key_inner, 0.0) * beta_heads[:, :, None] + jnp.eye(
        length, dtype=jnp.float32
    )
    decay_factor = jnp.exp(log_decay)
    right_side = jnp.concatenate(
        [beta_heads[:, :, None] * value_heads, (beta_heads * decay_factor)[:, :, None] * key_heads],
        axis=-1,
    )
    solved = lax.linalg.triangular_solve(
        tri_matrix, right_side, left_side=True, lower=True, unit_diagonal=True
    )
    new_contribution = solved[:, :, :DV]
    carried_state = solved[:, :, DV:]
    tail_decay = jnp.exp(log_decay[:, -1:] - log_decay)
    keys_weighted = key_heads * tail_decay[:, :, None]
    eye_keys = jnp.eye(DK, dtype=jnp.float32)
    state_map = decay_factor[:, -1][:, None, None] * eye_keys - jnp.einsum(
        "htk,htj->hkj", keys_weighted, carried_state, precision=precise_variant
    )
    state_increment = jnp.einsum(
        "iys,iyn->isn", keys_weighted, new_contribution, precision=precise_variant
    )

    def compose(earlier, later):
        return (batch_product(later[0], earlier[0]), batch_product(later[0], earlier[1]) + later[1])

    identity_pair = (jnp.broadcast_to(eye_keys, state_map.shape), jnp.zeros_like(state_increment))
    prior_map, prior_add = prefix((state_map, state_increment), "seq", compose, identity_pair)
    opening_state = batch_product(prior_map, init_state) + prior_add
    written_rows = new_contribution - jnp.einsum(
        "ucx,uxj->ucj", carried_state, opening_state, precision=precise_variant
    )
    query_inner = (
        jnp.einsum("htk,hsk->hts", query_head_rows, key_heads, precision=precise_variant) * decay
    )
    core = jnp.einsum(
        "ucx,uxj->ucj",
        query_head_rows * decay_factor[:, :, None],
        opening_state,
        precision=precise_variant,
    )
    core = core + jnp.einsum("hts,hsv->htv", query_inner, written_rows, precision=precise_variant)
    core = core.transpose(1, 0, 2)
    gate_rows = out_gate.astype(jnp.float32).reshape(length, head_count, DV)
    gated = (
        core
        * lax.rsqrt(jnp.mean(core * core, axis=-1, keepdims=True) + 1e-06)
        * norm_gain
        * jax.nn.silu(gate_rows)
    )
    gated = gated.astype(jnp.bfloat16).reshape(length, head_count * DV)
    attn_part = jnp.dot(gated, out_proj, preferred_element_type=jnp.float32)
    share_width = model_width // lax.axis_size("head")
    share_start = lax.axis_index("head") * share_width
    attn = lax.psum(attn_part.astype(jnp.bfloat16), "head").astype(jnp.float32)
    resid = (stream.astype(jnp.float32) + attn).astype(jnp.bfloat16)
    resid = lax.optimization_barrier(resid)
    resid_f = resid.astype(jnp.float32)
    normed = (
        resid_f * lax.rsqrt(jnp.mean(resid_f * resid_f, axis=-1, keepdims=True) + 1e-06) * post_gain
    ).astype(jnp.bfloat16)
    resid_share = lax.dynamic_slice_in_dim(resid, share_start, share_width, 1)
    peer_count = lax.axis_size("seq")
    column_count = lax.axis_size("head")
    expert_count = peer_count * column_count
    pick_count = expert_ids.shape[1]
    slot_count = min(length, length * pick_count * 2 // expert_count)
    targets = jnp.arange(peer_count, dtype=jnp.int32) * column_count + lax.axis_index("head")
    hits = expert_ids[:, :, None] == targets[None, None, :]
    weights = (route_scores / jnp.sum(route_scores, axis=1, keepdims=True)).astype(jnp.bfloat16)
    weights = lax.optimization_barrier(weights).astype(jnp.float32)
    chosen = jnp.sum(hits.astype(jnp.int32), axis=1)
    share_weight = jnp.sum(jnp.where(hits, weights[:, :, None], 0.0), axis=1)
    rank = jnp.cumsum(chosen, axis=0) - chosen
    slot_index = jnp.arange(slot_count, dtype=jnp.int32)
    placement_map = (
        (chosen[:, :, None] == 1) & (rank[:, :, None] == slot_index[None, None, :])
    ).astype(jnp.bfloat16)
    outgoing = jnp.einsum(
        "tps,td->psd", placement_map, normed, preferred_element_type=jnp.float32
    ).astype(jnp.bfloat16)
    incoming = lax.all_to_all(outgoing, "seq", split_axis=0, concat_axis=0, tiled=True)
    item_count = incoming.shape[1]
    flat_rows = incoming.reshape(-1, model_width)
    gate_e = jnp.dot(flat_rows, w_gate[0], preferred_element_type=jnp.float32)
    up_e = jnp.dot(flat_rows, w_up[0], preferred_element_type=jnp.float32)
    hidden = (jax.nn.silu(gate_e) * up_e).astype(jnp.bfloat16)
    result = jnp.dot(hidden, w_down[0], preferred_element_type=jnp.float32).astype(jnp.bfloat16)
    returned = lax.all_to_all(
        result.reshape(peer_count, item_count, model_width),
        "seq",
        split_axis=0,
        concat_axis=0,
        tiled=True,
    )
    combine_map = (placement_map.astype(jnp.float32) * share_weight[:, :, None]).astype(
        jnp.bfloat16
    )
    moe = jnp.einsum("tps,psd->td", combine_map, returned, preferred_element_type=jnp.float32)
    moe_share = lax.psum_scatter(
        moe.astype(jnp.bfloat16), "head", scatter_dimension=1, tiled=True
    ).astype(jnp.float32)
    return (resid_share.astype(jnp.float32) + moe_share).astype(jnp.bfloat16)


def solution(mesh):
    return jax.shard_map(
        on_device,
        mesh=mesh,
        in_specs=(
            P(("dp", "seq"), None),
            P(("dp", "seq"), "head"),
            P(("dp", "seq"), "head"),
            P(("dp", "seq"), "head"),
            P(("dp", "seq"), "head"),
            P(("dp", "seq"), "head"),
            P(("dp", "seq"), "head"),
            P(("dp", "head"), None, None),
            P(),
            P("head", None),
            P(),
            P(("dp", "seq"), None),
            P(("dp", "seq"), None),
            P(("seq", "head"), None, None),
            P(("seq", "head"), None, None),
            P(("seq", "head"), None, None),
        ),
        out_specs=P(("dp", "seq"), "head"),
        check_vma=False,
    )
```

profile of v0, /device:TPU:1, one launch (start us, length us, event | category | flops | bytes accessed | tf_op | source)
XLA Modules:
  0.0 571.6 jit_solution(3328301880551756863)
XLA Ops:
  11.4 39.9 %custom-call.3 = f32[4,1,128,128]{2,3,1,0:T(8,128)} custom-call(f32[4,1,128,128]{3,2,1,0:T(8,128)S(1)} %fusion.29), custom_call_target="InvertDiagBlocksLowerTriangular" | custom-call | tf_op jit(solution)/shard_map/triangular_solve | solution.py:90
  52.5 1.6 fusion.43
  58.0 1.7 copy.128
  60.6 2.1 convolution_multiply_fusion
  62.7 69.4 %all-gather.5.cloned.1.call-done = bf16[64,128,128]{2,1,0:T(8,128)(2,1)} async-done(((bf16[4,128,128]{2,1,0:T(8,128)(2,1)}), bf16[64,128,128]{2,1,0:T(8,128)(2,1)}) %all-gather.5.cloned.1.call-update) | async-done | bytes 2097168 | tf_op jit(solution)/shard_map/all_gather | solution.py:18
  132.1 75.9 %all-gather.7.cloned.1.call-done = bf16[64,128,128]{2,1,0:T(8,128)(2,1)} async-done(((bf16[4,128,128]{2,1,0:T(8,128)(2,1)}), bf16[64,128,128]{2,1,0:T(8,128)(2,1)}) %all-gather.7.cloned.1.call-update) | async-done | bytes 2097168 | tf_op jit(solution)/shard_map/all_gather | solution.py:18
  208.0 40.7 %while.16 = (s32[]{:T(128)}, f32[4,128,128]{2,1,0:T(8,128)S(1)}, f32[4,128,128]{2,1,0:T(8,128)S(1)}, s32[]{:T(128)}, bf16[16,4,128,128]{3,2,1,0:T(8,128)(2,1)}, ...) while((s32[]{:T(128)}, f32[4,128,128]{2,1,0:T(8,128)S(1)}, ...), condition=%wide.region_4.5_spmd.clone, body=%wide.region_3.4_spmd.clone.sunk | while | flops 201719808 | bytes 3017832 | solution.py:35
  210.6 1.3 fusion.98
  213.2 1.3 fusion.98
  215.7 1.3 fusion.98
  218.3 1.3 fusion.98
  220.8 1.3 fusion.98
  223.4 1.3 fusion.98
  225.9 1.3 fusion.98
  228.5 1.3 fusion.98
  233.6 1.3 fusion.98
  236.1 1.3 fusion.98
  241.2 1.3 fusion.98
  243.7 1.3 fusion.98
  248.8 1.5 convolution_add_fusion.2
  252.2 1.3 convolution_convert_fusion.2
  254.0 87.2 %all-reduce.2.cloned.1.call-done = bf16[128,2048]{1,0:T(8,128)(2,1)} async-done(((bf16[128,2048]{1,0:T(8,128)(2,1)}), bf16[128,2048]{1,0:T(8,128)(2,1)}) %all-reduce.2.cloned.1.call-update) | async-done | bytes 524304 | tf_op jit(solution)/shard_map/psum | solution.py:136
  343.2 77.2 %all_to_all.10 = bf16[16,20,2048]{2,1,0:T(8,128)(2,1)} all-to-all(bf16[16,20,2048]{2,1,0:T(8,128)(2,1)S(1)} %convolution_convert_fusion), channel_id=1, replica_groups=mesh['dp'=8,'seq'=16,'head'=8] {'seq'}, dimensions={0} | all-to-all | bytes 2621440 | tf_op jit(solution)/shard_map/all_to_all | solution.py:163
  420.4 3.3 reshape.121
  423.7 3.7 fusion.15
  427.4 4.8 convolution_convert_fusion.1
  432.2 3.2 reshape.122
  435.4 12.7 %all-to-all-start.1 = ((bf16[16,20,2048]{2,1,0:T(8,128)(2,1)}), bf16[16,20,2048]{2,1,0:T(8,128)(2,1)}, u32[]{:S(2)}, u32[]{:S(2)}) async-start(bf16[16,20,2048]{2,1,0:T(8,128)(2,1)} %reshape.122), calls=%async_computation.1 | async-start | bytes 3145728 | tf_op jit(solution)/shard_map/all_to_all | solution.py:170
  448.3 69.1 %all-to-all-done.1 = bf16[16,20,2048]{2,1,0:T(8,128)(2,1)} async-done(((bf16[16,20,2048]{2,1,0:T(8,128)(2,1)}), bf16[16,20,2048]{2,1,0:T(8,128)(2,1)}, u32[]{:S(2)}, u32[]{:S(2)}) %all-to-all-start.1) | async-done | bytes 1310752 | tf_op jit(solution)/shard_map/all_to_all | solution.py:170
  517.3 2.7 fusion.11
  520.1 43.5 %reduce-scatter.2.cloned.1.call-done = bf16[128,256]{1,0:T(8,128)(2,1)} async-done(((bf16[128,2048]{1,0:T(8,128)(2,1)}), bf16[128,256]{1,0:T(8,128)(2,1)}) %reduce-scatter.2.cloned.1.call-update) | async-done | bytes 65552 | tf_op jit(solution)/shard_map/reduce_scatter | solution.py:181
  563.6 1.5 add_convert_fusion.1
  (139 shorter events, 39.9 us)
Async XLA Ops:
  6.5 420.8 %copy-start = (bf16[1,512,2048]{2,1,0:T(8,128)(2,1)S(1)}, bf16[1,512,2048]{2,1,0:T(8,128)(2,1)}, u32[]{:S(2)}) copy-start(bf16[1,512,2048]{2,1,0:T(8,128)(2,1)} %param.33) | copy-start | bytes 6291460
  6.5 4.1 copy-start.12
  6.5 125.5 %all-gather.5.cloned.1.call-start = ((), (), s32[]{:S(2)}) async-start(), calls=%async_computation.5 | async-start | bytes 2228224 | tf_op jit(solution)/shard_map/all_gather | solution.py:18
  7.8 43.8 %copy-start.6 = (f32[128,4]{0,1:T(4,128)}, f32[128,4]{0,1:T(4,128)S(1)}, u32[]{:S(2)}) copy-start(f32[128,4]{0,1:T(4,128)S(1)} %copy.119) | copy-start | bytes 6148
  10.7 41.9 %copy-start.9 = (f32[4,128]{1,0:T(4,128)}, f32[4,128]{1,0:T(4,128)S(1)}, u32[]{:S(2)}) copy-start(f32[4,128]{1,0:T(4,128)S(1)} %get-tuple-element.152) | copy-start | bytes 6148
  11.4 45.4 %copy-start.5 = (bf16[128,256]{1,0:T(8,128)(2,1)S(1)}, bf16[128,256]{1,0:T(8,128)(2,1)}, u32[]{:S(2)}) copy-start(bf16[128,256]{1,0:T(8,128)(2,1)} %param.19) | copy-start | bytes 196612
  55.4 152.6 %all-gather.7.cloned.1.call-start = ((), (), s32[]{:S(2)}) async-start(), calls=%async_computation.6 | async-start | bytes 2228224 | tf_op jit(solution)/shard_map/all_gather | solution.py:18
  56.7 284.5 %all-reduce.2.cloned.1.call-start = ((), (), s32[]{:S(2)}) async-start(), calls=%async_computation.3 | async-start | bytes 1048576 | tf_op jit(solution)/shard_map/psum | solution.py:136
  208.0 42.7 %copy-start.10 = (f32[4,128]{1,0:T(4,128)S(1)}, f32[4,128]{1,0:T(4,128)}, u32[]{:S(2)}) copy-start(f32[4,128]{1,0:T(4,128)} %copy-done.9) | copy-start | bytes 6148
  248.8 2.6 copy-start.3
  248.8 3.3 copy-start.2
  248.8 3.3 copy-start.13
  248.8 3.4 copy-start.1
  252.1 1.5 copy-start.7
  252.1 89.1 %copy-start.4 = (bf16[128,2048]{1,0:T(8,128)(2,1)S(1)}, bf16[128,2048]{1,0:T(8,128)(2,1)}, u32[]{:S(2)}) copy-start(bf16[128,2048]{1,0:T(8,128)(2,1)} %param.18) | copy-start | bytes 1572868
  253.5 89.0 %copy-start.11 = (f32[2048]{0:T(1024)S(1)}, f32[2048]{0:T(1024)}, u32[]{:S(2)}) copy-start(f32[2048]{0:T(1024)} %param.28) | copy-start | bytes 24580
  435.4 12.8 %copy-start.8 = (f32[128,10]{0,1:T(8,128)S(1)}, f32[128,10]{0,1:T(8,128)}, u32[]{:S(2)}) copy-start(f32[128,10]{0,1:T(8,128)} %param.30) | copy-start | bytes 15364
  435.4 82.0 %all-to-all-start.1 = ((bf16[16,20,2048]{2,1,0:T(8,128)(2,1)}), bf16[16,20,2048]{2,1,0:T(8,128)(2,1)}, u32[]{:S(2)}, u32[]{:S(2)}) async-start(bf16[16,20,2048]{2,1,0:T(8,128)(2,1)} %reshape.122), calls=%async_computation.1 | async-start | bytes 3145728 | tf_op jit(solution)/shard_map/all_to_all | solution.py:170
  448.1 115.5 %reduce-scatter.2.cloned.1.call-start = ((), (), s32[]{:S(2)}) async-start(), calls=%async_computation.4 | async-start | bytes 589824 | tf_op jit(solution)/shard_map/reduce_scatter | solution.py:181
Sparse Core Ops, SparseCore 0:
  55.5 76.5 all-gather.4
  134.7 73.2 all-gather.6
  253.7 87.4 all-reduce.1
  520.2 43.3 reduce-scatter.1
where the time goes:
time: 573 us; the launch traced here: 572 us
  waiting for transfers between devices  345 us (60%)
  blocking collectives  77.2 us (13%)
  matrix products  62.5 us (11%)
  other arithmetic  45.5 us (8%)
  local copies, waits for them, and re-layouts  14.1 us (2%)
  between operations  13.5 us (2%)
  starting transfers between devices  12.8 us (2%)
    all_gather x2, waiting for transfers between devices, prefix(): lax.all_gather(part.astype(kind), axis)  145 us
    psum x1, waiting for transfers between devices, on_device(): attn = lax.psum(attn_part.astype(jnp.bfloat16), 'head').astype(jnp.float32)  87.2 us
    all_to_all x1, blocking collectives, on_device(): lax.all_to_all(outgoing, 'seq', split_axis=0, concat_axis=0, tiled=True)  77.2 us
    all_to_all x1, waiting for transfers between devices, on_device(): lax.all_to_all(result.reshape(peer_count, item_count, model_width), 'seq'...  69.1 us
    reduce_scatter x1, waiting for transfers between devices, on_device(): lax.psum_scatter(moe.astype(jnp.bfloat16), 'head', scatter_dimension=1, t...  43.5 us
    dot_general x33, matrix products, batch_product(): return jnp.einsum('hij,hjk->hik', left, right, precision=precise_variant)  40.8 us
    another operation x4, other arithmetic, on_device(): lax.linalg.triangular_solve(tri_matrix, right_side, left_side=True, lower...  40 us
    all_to_all x1, starting transfers between devices, on_device(): lax.all_to_all(result.reshape(peer_count, item_count, model_width), 'seq'...  12.7 us
  transfers between devices with their start and end apart: 5, of which 5 were waited for; matrix products, arithmetic and copies ran while one was open for 1% of the time, Pallas kernels for 0%

commit v1 on v0

--- a/solution.py
+++ b/solution.py
@@ -10,29 +10,6 @@
 
 
 precise_variant = lax.Precision.HIGHEST
-
-
-def prefix(array, axis, combine, identity):
-    size, position = (lax.axis_size(axis), lax.axis_index(axis))
-    everything = jax.tree.map(
-        lambda part, kind: lax.all_gather(part.astype(kind), axis),
-        array,
-        (jnp.bfloat16, jnp.bfloat16),
-    )
-    start = jax.tree.map(
-        lambda part, zero: jnp.broadcast_to(jnp.asarray(zero, part.dtype), part.shape),
-        array,
-        identity,
-    )
-
-    def lap(k, before):
-        reached = k < position
-        new = combine(
-            before, jax.tree.map(lambda part, own: part[k].astype(own.dtype), everything, array)
-        )
-        return jax.tree.map(lambda a, b: jnp.where(reached, a, b), new, before)
-
-    return lax.fori_loop(0, size, lap, start)
 
 
 def unit_rows(matrix):
@@ -102,12 +79,15 @@
         "iys,iyn->isn", keys_weighted, new_contribution, precision=precise_variant
     )
 
-    def compose(earlier, later):
-        return (batch_product(later[0], earlier[0]), batch_product(later[0], earlier[1]) + later[1])
-
-    identity_pair = (jnp.broadcast_to(eye_keys, state_map.shape), jnp.zeros_like(state_increment))
-    prior_map, prior_add = prefix((state_map, state_increment), "seq", compose, identity_pair)
-    opening_state = batch_product(prior_map, init_state) + prior_add
+    pairs = lax.all_gather(
+        jnp.concatenate([state_map, state_increment], axis=0).astype(jnp.bfloat16), "seq"
+    )
+
+    def horner(k, state):
+        step_pair = pairs[k].astype(jnp.float32)
+        return batch_product(step_pair[:head_count], state) + step_pair[head_count:]
+
+    opening_state = lax.fori_loop(0, lax.axis_index("seq"), horner, init_state)
     written_rows = new_contribution - jnp.einsum(
         "ucx,uxj->ucj", carried_state, opening_state, precision=precise_variant
     )
@@ -133,14 +113,27 @@
     attn_part = jnp.dot(gated, out_proj, preferred_element_type=jnp.float32)
     share_width = model_width // lax.axis_size("head")
     share_start = lax.axis_index("head") * share_width
-    attn = lax.psum(attn_part.astype(jnp.bfloat16), "head").astype(jnp.float32)
-    resid = (stream.astype(jnp.float32) + attn).astype(jnp.bfloat16)
-    resid = lax.optimization_barrier(resid)
+    column_total = lax.axis_size("head")
+    attn_pieces = attn_part.astype(jnp.bfloat16).reshape(length, column_total, share_width)
+    attn_pieces = lax.all_to_all(
+        attn_pieces.transpose(1, 0, 2), "head", split_axis=0, concat_axis=0, tiled=True
+    )
+    attn_share = jnp.sum(attn_pieces.astype(jnp.float32), axis=0)
+    stream_share = lax.dynamic_slice_in_dim(stream, share_start, share_width, 1)
+    resid_share = (stream_share.astype(jnp.float32) + attn_share).astype(jnp.bfloat16)
+    resid_share = lax.optimization_barrier(resid_share)
+    resid_rows = lax.all_to_all(
+        jnp.broadcast_to(resid_share[None], (column_total, length, share_width)),
+        "head",
+        split_axis=0,
+        concat_axis=0,
+        tiled=True,
+    )
+    resid = resid_rows.transpose(1, 0, 2).reshape(length, model_width)
     resid_f = resid.astype(jnp.float32)
     normed = (
         resid_f * lax.rsqrt(jnp.mean(resid_f * resid_f, axis=-1, keepdims=True) + 1e-06) * post_gain
     ).astype(jnp.bfloat16)
-    resid_share = lax.dynamic_slice_in_dim(resid, share_start, share_width, 1)
     peer_count = lax.axis_size("seq")
     column_count = lax.axis_size("head")
     expert_count = peer_count * column_count
@@ -178,9 +171,11 @@
         jnp.bfloat16
     )
     moe = jnp.einsum("tps,psd->td", combine_map, returned, preferred_element_type=jnp.float32)
-    moe_share = lax.psum_scatter(
-        moe.astype(jnp.bfloat16), "head", scatter_dimension=1, tiled=True
-    ).astype(jnp.float32)
+    moe_pieces = moe.astype(jnp.bfloat16).reshape(length, column_total, share_width)
+    moe_pieces = lax.all_to_all(
+        moe_pieces.transpose(1, 0, 2), "head", split_axis=0, concat_axis=0, tiled=True
+    )
+    moe_share = jnp.sum(moe_pieces.astype(jnp.float32), axis=0)
     return (resid_share.astype(jnp.float32) + moe_share).astype(jnp.bfloat16)
 
 

time: 573 us -> 394 us (0.69)
  waiting for transfers between devices: 345 us -> 167 us
  matrix products: 62.5 us -> 18.1 us
  blocking collectives: 77.2 us -> 109 us
  starting transfers between devices: 12.8 us -> 30 us
    psum x1 -> x0, waiting for transfers between devices: 87.2 us -> none  [on_device(): attn = lax.psum(attn_part.astype(jnp.bfloat16), 'head').astype(jnp.float32)]
    all_gather x2 -> x1, waiting for transfers between devices: 145 us -> 79.1 us  [on_device(): lax.all_gather(jnp.concatenate([state_map, state_increment], axis=0).asty...]
    reduce_scatter x1 -> x0, waiting for transfers between devices: 43.5 us -> none  [on_device(): lax.psum_scatter(moe.astype(jnp.bfloat16), 'head', scatter_dimension=1, t...]
    dot_general x33 -> x0, matrix products: 40.8 us -> none  [batch_product(): return jnp.einsum('hij,hjk->hik', left, right, precision=precise_variant)]
    all_to_all x0 -> x2, waiting for transfers between devices: none -> 18.5 us  [the longest x1 9.48 us: on_device(): lax.all_to_all(attn_pieces.transpose(1, 0, 2), 'head', split_axis=0, conc...]
    all_to_all x0 -> x1, blocking collectives: none -> 18 us  [on_device(): lax.all_to_all(moe_pieces.transpose(1, 0, 2), 'head', split_axis=0, conca...]
    all_to_all x0 -> x2, starting transfers between devices: none -> 17.6 us  [the longest x1 13.4 us: on_device(): lax.all_to_all(attn_pieces.transpose(1, 0, 2), 'head', split_axis=0, conc...]
    all_to_all x1, blocking collectives: 77.2 us -> 91 us  [on_device(): lax.all_to_all(outgoing, 'seq', split_axis=0, concat_axis=0, tiled=True)]
  transfers between devices with their start and end apart: 5 -> 4, of which waited for: 5 -> 4; matrix products, arithmetic and copies ran while one was open for 1% -> 1% of each run, Pallas kernels for 0% -> 0%
where the time goes in v1:
time: 394 us; the launch traced here: 393 us
  waiting for transfers between devices  167 us (42%)
  blocking collectives  109 us (28%)
  other arithmetic  44.3 us (11%)
  starting transfers between devices  30 us (8%)
  matrix products  18.1 us (5%)
  between operations  13.8 us (4%)
  local copies, waits for them, and re-layouts  11.4 us (3%)
    all_to_all x1, blocking collectives, on_device(): lax.all_to_all(outgoing, 'seq', split_axis=0, concat_axis=0, tiled=True)  91 us
    all_gather x1, waiting for transfers between devices, on_device(): lax.all_gather(jnp.concatenate([state_map, state_increment], axis=0).asty...  79.1 us
    all_to_all x1, waiting for transfers between devices, on_device(): lax.all_to_all(result.reshape(peer_count, item_count, model_width), 'seq'...  68.9 us
    another operation x4, other arithmetic, on_device(): lax.linalg.triangular_solve(tri_matrix, right_side, left_side=True, lower...  39.4 us
    all_to_all x1, blocking collectives, on_device(): lax.all_to_all(moe_pieces.transpose(1, 0, 2), 'head', split_axis=0, conca...  18 us
    all_to_all x1, starting transfers between devices, on_device(): lax.all_to_all(attn_pieces.transpose(1, 0, 2), 'head', split_axis=0, conc...  13.4 us
    all_to_all x1, starting transfers between devices, on_device(): lax.all_to_all(result.reshape(peer_count, item_count, model_width), 'seq'...  12.3 us
    all_to_all x1, waiting for transfers between devices, on_device(): lax.all_to_all(attn_pieces.transpose(1, 0, 2), 'head', split_axis=0, conc...  9.48 us
  transfers between devices with their start and end apart: 4, of which 4 were waited for; matrix products, arithmetic and copies ran while one was open for 1% of the time, Pallas kernels for 0%

profile of v1, /device:TPU:1, one launch (start us, length us, event | category | flops | bytes accessed | tf_op | source)
XLA Modules:
  0.0 393.2 jit_solution(17241349937403730947)
XLA Ops:
  6.6 0.8 log.3
  8.0 0.9 reshape.172
  9.8 0.7 fusion.19
  10.6 39.3 %custom-call.3 = f32[4,1,128,128]{2,3,1,0:T(8,128)S(1)} custom-call(f32[4,1,128,128]{3,2,1,0:T(8,128)S(1)} %fusion.19), custom_call_target="InvertDiagBlocksLowerTriangular" | custom-call | tf_op jit(solution)/shard_map/triangular_solve | solution.py:67
  50.4 0.6 fusion.32
  51.0 0.6 fusion.21
  51.7 0.6 fusion.22
  52.3 0.7 pad_maximum_fusion
  53.6 0.8 copy.164
  54.4 2.3 convolution_multiply_fusion
  56.7 79.1 %all-gather.2.cloned.1.call-done = bf16[16,8,128,128]{3,2,1,0:T(8,128)(2,1)} async-done(((bf16[1,8,128,128]{3,2,1,0:T(8,128)(2,1)}), bf16[16,8,128,128]{3,2,1,0:T(8,128)(2,1)}) %all-gather.2.cloned.1.call-update) | async-done | bytes 4194320 | tf_op jit(solution)/shard_map/all_gather | solution.py:82
  136.5 0.7 fusion.39
  137.2 1.6 multiply_reduce_fusion.1
  138.9 0.5 convolution_convert_fusion.2
  139.4 0.8 copy.184
  140.3 13.4 %all-to-all-start = ((bf16[8,128,256]{2,1,0:T(8,128)(2,1)}), bf16[8,128,256]{2,1,0:T(8,128)(2,1)S(1)}, u32[]{:S(2)}, u32[]{:S(2)}) async-start(bf16[8,128,256]{2,1,0:T(8,128)(2,1)} %bitcast.99), calls=%async_computation | async-start | bytes 1048576 | tf_op jit(solution)/shard_map/all_to_all | solution.py:118
  153.6 9.5 %all-to-all-done = bf16[8,128,256]{2,1,0:T(8,128)(2,1)S(1)} async-done(((bf16[8,128,256]{2,1,0:T(8,128)(2,1)}), bf16[8,128,256]{2,1,0:T(8,128)(2,1)S(1)}, u32[]{:S(2)}, u32[]{:S(2)}) %all-to-all-start) | async-done | bytes 524320 | tf_op jit(solution)/shard_map/all_to_all | solution.py:118
  163.2 0.9 add_convert_fusion.1
  164.1 0.8 broadcast_in_dim.70
  164.9 4.3 %all-to-all-start.1 = ((bf16[8,128,256]{2,1,0:T(8,128)(2,1)}), bf16[8,128,256]{2,1,0:T(8,128)(2,1)S(1)}, u32[]{:S(2)}, u32[]{:S(2)}) async-start(bf16[8,128,256]{2,1,0:T(8,128)(2,1)} %broadcast_in_dim.70), calls=%async_computation.1 | async-start | bytes 1048576 | tf_op jit(solution)/shard_map/all_to_all | solution.py:125
  169.6 9.1 %all-to-all-done.1 = bf16[8,128,256]{2,1,0:T(8,128)(2,1)S(1)} async-done(((bf16[8,128,256]{2,1,0:T(8,128)(2,1)}), bf16[8,128,256]{2,1,0:T(8,128)(2,1)S(1)}, u32[]{:S(2)}, u32[]{:S(2)}) %all-to-all-start.1) | async-done | bytes 524320 | tf_op jit(solution)/shard_map/all_to_all | solution.py:125
  179.6 0.6 convolution_convert_fusion
  180.2 91.0 %all_to_all.25 = bf16[16,20,2048]{2,1,0:T(8,128)(2,1)} all-to-all(bf16[16,20,2048]{2,1,0:T(8,128)(2,1)S(1)} %convolution_convert_fusion), channel_id=1, replica_groups=mesh['dp'=8,'seq'=16,'head'=8] {'seq'}, dimensions={0} | all-to-all | bytes 2621440 | tf_op jit(solution)/shard_map/all_to_all | solution.py:156
  271.2 2.3 reshape.165
  273.4 3.3 fusion.5
  276.7 4.4 %convolution_convert_fusion.1 = bf16[320,2048]{1,0:T(8,128)(2,1)} fusion(bf16[1,512,2048]{2,1,0:T(8,128)(2,1)S(1)} %copy-done, bf16[320,2048]{1,0:T(8,128)(2,1)S(1)} %reshape.165, bf16[1,2048,512]{2,1,0:T(8,128)(2,1)} %param.32, f32[320,512]{1,0:T(8,128)} %fusion.5), kind=kOutput, calls=%fused_computation.5 | convolution fusion | flops 1343815680 | bytes 7471104 | tf_op jit(solution)/shard_map/dot_general | solution.py:162
  281.1 3.2 reshape.166
  284.3 12.3 %all-to-all-start.3 = ((bf16[16,20,2048]{2,1,0:T(8,128)(2,1)}), bf16[16,20,2048]{2,1,0:T(8,128)(2,1)}, u32[]{:S(2)}, u32[]{:S(2)}) async-start(bf16[16,20,2048]{2,1,0:T(8,128)(2,1)} %reshape.166), calls=%async_computation.3 | async-start | bytes 3145728 | tf_op jit(solution)/shard_map/all_to_all | solution.py:163
  296.8 68.9 %all-to-all-done.3 = bf16[16,20,2048]{2,1,0:T(8,128)(2,1)} async-done(((bf16[16,20,2048]{2,1,0:T(8,128)(2,1)}), bf16[16,20,2048]{2,1,0:T(8,128)(2,1)}, u32[]{:S(2)}, u32[]{:S(2)}) %all-to-all-start.3) | async-done | bytes 1310752 | tf_op jit(solution)/shard_map/all_to_all | solution.py:163
  365.7 1.9 fusion.1
  367.6 18.0 %all_to_all.26 = bf16[8,128,256]{2,1,0:T(8,128)(2,1)S(1)} all-to-all(bf16[8,128,256]{2,1,0:T(8,128)(2,1)S(1)} %bitcast.109), channel_id=1, replica_groups=mesh['dp'=8,'seq'=16,'head'=8] {'head'}, dimensions={0} | all-to-all | bytes 1048576 | tf_op jit(solution)/shard_map/all_to_all | solution.py:175
  385.7 0.6 add_convert_fusion
  (80 shorter events, 4.9 us)
Async XLA Ops:
  6.5 270.2 %copy-start = (bf16[1,512,2048]{2,1,0:T(8,128)(2,1)S(1)}, bf16[1,512,2048]{2,1,0:T(8,128)(2,1)}, u32[]{:S(2)}) copy-start(bf16[1,512,2048]{2,1,0:T(8,128)(2,1)} %param.33) | copy-start | bytes 6291460
  6.5 2.8 copy-start.6
  6.5 3.2 copy-start.14
  6.5 129.3 %all-gather.2.cloned.1.call-start = ((), (), s32[]{:S(2)}) async-start(), calls=%async_computation.5 | async-start | bytes 4456448 | tf_op jit(solution)/shard_map/all_gather | solution.py:82
  7.8 42.6 %copy-start.8 = (f32[128,4]{0,1:T(4,128)}, f32[128,4]{0,1:T(4,128)S(1)}, u32[]{:S(2)}) copy-start(f32[128,4]{0,1:T(4,128)S(1)} %copy.155) | copy-start | bytes 6148
  9.8 40.6 %copy-start.11 = (f32[4,128]{1,0:T(4,128)}, f32[4,128]{1,0:T(4,128)S(1)}, u32[]{:S(2)}) copy-start(f32[4,128]{1,0:T(4,128)S(1)} %get-tuple-element.39) | copy-start | bytes 6148
  9.8 40.2 %copy-start.3 = (f32[128,2,2,128]{3,0,2,1:T(8,128)}, f32[128,2,2,128]{3,0,2,1:T(8,128)S(1)}, u32[]{:S(2)}) copy-start(f32[128,2,2,128]{3,0,2,1:T(8,128)S(1)} %broadcast_in_dim.31) | copy-start | bytes 786436
  50.1 2.9 copy-start.7
  51.0 2.5 copy-start.5
  51.6 84.2 %copy-start.1 = (f32[4,128,128]{2,1,0:T(8,128)S(1)}, f32[4,128,128]{2,1,0:T(8,128)}, u32[]{:S(2)}) copy-start(f32[4,128,128]{2,1,0:T(8,128)} %param.25) | copy-start | bytes 786436
  135.8 0.7 copy-start.12
  135.8 2.9 copy-start.4
  135.9 3.0 copy-start.15
  135.9 3.1 copy-start.2
  139.4 29.7 %copy-start.9 = (s32[128,10]{0,1:T(8,128)S(1)}, s32[128,10]{0,1:T(8,128)}, u32[]{:S(2)}) copy-start(s32[128,10]{0,1:T(8,128)} %param.29) | copy-start | bytes 15364
  140.3 22.9 %all-to-all-start = ((bf16[8,128,256]{2,1,0:T(8,128)(2,1)}), bf16[8,128,256]{2,1,0:T(8,128)(2,1)S(1)}, u32[]{:S(2)}, u32[]{:S(2)}) async-start(bf16[8,128,256]{2,1,0:T(8,128)(2,1)} %bitcast.99), calls=%async_computation | async-start | bytes 1048576 | tf_op jit(solution)/shard_map/all_to_all | solution.py:118
  163.2 16.0 %copy-start.13 = (f32[2048]{0:T(1024)S(1)}, f32[2048]{0:T(1024)}, u32[]{:S(2)}) copy-start(f32[2048]{0:T(1024)} %param.28) | copy-start | bytes 24580
  164.9 13.8 %all-to-all-start.1 = ((bf16[8,128,256]{2,1,0:T(8,128)(2,1)}), bf16[8,128,256]{2,1,0:T(8,128)(2,1)S(1)}, u32[]{:S(2)}, u32[]{:S(2)}) async-start(bf16[8,128,256]{2,1,0:T(8,128)(2,1)} %broadcast_in_dim.70), calls=%async_computation.1 | async-start | bytes 1048576 | tf_op jit(solution)/shard_map/all_to_all | solution.py:125
  284.3 12.3 %copy-start.10 = (f32[128,10]{0,1:T(8,128)S(1)}, f32[128,10]{0,1:T(8,128)}, u32[]{:S(2)}) copy-start(f32[128,10]{0,1:T(8,128)} %param.30) | copy-start | bytes 15364
  284.3 81.3 %all-to-all-start.3 = ((bf16[16,20,2048]{2,1,0:T(8,128)(2,1)}), bf16[16,20,2048]{2,1,0:T(8,128)(2,1)}, u32[]{:S(2)}, u32[]{:S(2)}) async-start(bf16[16,20,2048]{2,1,0:T(8,128)(2,1)} %reshape.166), calls=%async_computation.3 | async-start | bytes 3145728 | tf_op jit(solution)/shard_map/all_to_all | solution.py:163
Sparse Core Ops, SparseCore 0:
  53.1 82.6 all-gather.1

commit v2 on v1

--- a/solution.py
+++ b/solution.py
@@ -18,6 +18,46 @@
 
 def batch_product(left, right):
     return jnp.einsum("hij,hjk->hik", left, right, precision=precise_variant)
+
+
+def block_product(left, right):
+    return jnp.einsum("...ij,...jk->...ik", left, right, precision=precise_variant)
+
+
+def unit_lower_inverse(tri, block=16):
+    heads, size_all, _ = tri.shape
+    count = size_all // block
+    eye_block = jnp.eye(block, dtype=tri.dtype)
+    diagonal = jnp.stack(
+        [tri[:, k * block : (k + 1) * block, k * block : (k + 1) * block] for k in range(count)],
+        axis=1,
+    )
+    nil = diagonal - eye_block
+    power = block_product(nil, nil)
+    inverse = block_product(eye_block - nil, eye_block + power)
+    reach = 4
+    while reach < block:
+        power = block_product(power, power)
+        inverse = block_product(inverse, eye_block + power)
+        reach *= 2
+    size = block
+    while size < size_all:
+        pairs = inverse.shape[1] // 2
+        first = inverse[:, 0::2]
+        second = inverse[:, 1::2]
+        coupling = jnp.stack(
+            [
+                tri[:, (2 * k + 1) * size : (2 * k + 2) * size, 2 * k * size : (2 * k + 1) * size]
+                for k in range(pairs)
+            ],
+            axis=1,
+        )
+        lower_left = -block_product(second, block_product(coupling, first))
+        top = jnp.concatenate([first, jnp.zeros_like(first)], axis=-1)
+        bottom = jnp.concatenate([lower_left, second], axis=-1)
+        inverse = jnp.concatenate([top, bottom], axis=-2)
+        size *= 2
+    return inverse[:, 0]
 
 
 def on_device(
@@ -64,9 +104,7 @@
         [beta_heads[:, :, None] * value_heads, (beta_heads * decay_factor)[:, :, None] * key_heads],
         axis=-1,
     )
-    solved = lax.linalg.triangular_solve(
-        tri_matrix, right_side, left_side=True, lower=True, unit_diagonal=True
-    )
+    solved = batch_product(unit_lower_inverse(tri_matrix), right_side)
     new_contribution = solved[:, :, :DV]
     carried_state = solved[:, :, DV:]
     tail_decay = jnp.exp(log_decay[:, -1:] - log_decay)
@@ -79,28 +117,42 @@
         "iys,iyn->isn", keys_weighted, new_contribution, precision=precise_variant
     )
 
+    query_inner = (
+        jnp.einsum("htk,hsk->hts", query_head_rows, key_heads, precision=precise_variant) * decay
+    )
+    query_effective = query_head_rows * decay_factor[:, :, None] - batch_product(
+        query_inner, carried_state
+    )
+    core_local = batch_product(query_inner, new_contribution)
     pairs = lax.all_gather(
         jnp.concatenate([state_map, state_increment], axis=0).astype(jnp.bfloat16), "seq"
     )
-
-    def horner(k, state):
-        step_pair = pairs[k].astype(jnp.float32)
-        return batch_product(step_pair[:head_count], state) + step_pair[head_count:]
-
-    opening_state = lax.fori_loop(0, lax.axis_index("seq"), horner, init_state)
-    written_rows = new_contribution - jnp.einsum(
-        "ucx,uxj->ucj", carried_state, opening_state, precision=precise_variant
-    )
-    query_inner = (
-        jnp.einsum("htk,hsk->hts", query_head_rows, key_heads, precision=precise_variant) * decay
-    )
-    core = jnp.einsum(
-        "ucx,uxj->ucj",
-        query_head_rows * decay_factor[:, :, None],
-        opening_state,
-        precision=precise_variant,
-    )
-    core = core + jnp.einsum("hts,hsv->htv", query_inner, written_rows, precision=precise_variant)
+    segments = pairs.astype(jnp.float32)
+    position = lax.axis_index("seq")
+    levels = [segments]
+    while segments.shape[0] > 2:
+        earlier = segments[0::2]
+        later = segments[1::2]
+        joined = jnp.einsum(
+            "phij,phjk->phik",
+            later[:, :head_count],
+            jnp.concatenate([earlier[:, :head_count], earlier[:, head_count:]], axis=-1),
+            precision=precise_variant,
+        )
+        segments = jnp.concatenate(
+            [joined[..., :DK], joined[..., DK:] + later[:, head_count:]], axis=1
+        )
+        levels.append(segments)
+    opening_state = init_state
+    cursor = 0
+    for level in reversed(range(len(levels))):
+        span = 2**level
+        taken = (position // span) % 2 == 1
+        piece = lax.dynamic_index_in_dim(levels[level], cursor // span, 0, keepdims=False)
+        advanced = batch_product(piece[:head_count], opening_state) + piece[head_count:]
+        opening_state = jnp.where(taken, advanced, opening_state)
+        cursor = cursor + jnp.where(taken, span, 0)
+    core = batch_product(query_effective, opening_state) + core_local
     core = core.transpose(1, 0, 2)
     gate_rows = out_gate.astype(jnp.float32).reshape(length, head_count, DV)
     gated = (

time: 394 us -> 359 us (0.911)
  other arithmetic: 44.3 us -> 7.96 us
  blocking collectives: 109 us -> 92.9 us
  matrix products: 18.1 us -> 27.5 us
  local copies, waits for them, and re-layouts: 11.4 us -> 17.6 us
    another operation x4 -> x0, other arithmetic: 39.4 us -> none  [on_device(): lax.linalg.triangular_solve(tri_matrix, right_side, left_side=True, lower...]
    all_to_all x1, blocking collectives: 91 us -> 74.9 us  [on_device(): lax.all_to_all(outgoing, 'seq', split_axis=0, concat_axis=0, tiled=True)]
    dot_general x3 -> x23, matrix products: 2.63 us -> 13.6 us  [the longest x3 5.37 us: on_device(): jnp.einsum('phij,phjk->phik', later[:, :head_count], jnp.concatenate([ear...]
    slice x0 -> x11, local copies, waits for them, and re-layouts: none -> 4.42 us  [the longest x3 3.73 us: on_device(): earlier = segments[0::2]]
where the time goes in v2:
time: 359 us; the launch traced here: 358 us
  waiting for transfers between devices  168 us (47%)
  blocking collectives  92.9 us (26%)
  starting transfers between devices  30 us (8%)
  matrix products  27.5 us (8%)
  local copies, waits for them, and re-layouts  17.6 us (5%)
  between operations  14.3 us (4%)
  other arithmetic  7.96 us (2%)
    all_gather x1, waiting for transfers between devices, on_device(): lax.all_gather(jnp.concatenate([state_map, state_increment], axis=0).asty...  80.2 us
    all_to_all x1, blocking collectives, on_device(): lax.all_to_all(outgoing, 'seq', split_axis=0, concat_axis=0, tiled=True)  74.9 us
    all_to_all x1, waiting for transfers between devices, on_device(): lax.all_to_all(result.reshape(peer_count, item_count, model_width), 'seq'...  68.9 us
    all_to_all x1, blocking collectives, on_device(): lax.all_to_all(moe_pieces.transpose(1, 0, 2), 'head', split_axis=0, conca...  18 us
    all_to_all x1, starting transfers between devices, on_device(): lax.all_to_all(attn_pieces.transpose(1, 0, 2), 'head', split_axis=0, conc...  13.4 us
    all_to_all x1, starting transfers between devices, on_device(): lax.all_to_all(result.reshape(peer_count, item_count, model_width), 'seq'...  12.3 us
    all_to_all x1, waiting for transfers between devices, on_device(): lax.all_to_all(attn_pieces.transpose(1, 0, 2), 'head', split_axis=0, conc...  9.48 us
    all_to_all x1, waiting for transfers between devices, on_device(): lax.all_to_all(jnp.broadcast_to(resid_share[None], (column_total, length,...  9.06 us
  transfers between devices with their start and end apart: 4, of which 4 were waited for; matrix products, arithmetic and copies ran while one was open for 1% of the time, Pallas kernels for 0%

profile of v2, /device:TPU:1, one launch (start us, length us, event | category | flops | bytes accessed | tf_op | source)
XLA Modules:
  0.0 357.9 jit_solution(178895640581850699)
XLA Ops:
  6.6 1.0 reshape.193
  8.1 0.7 log.3
  9.2 1.4 fusion.28
  16.8 0.6 fusion.48
  18.6 0.7 pad_maximum_fusion.2
  20.2 0.7 convolution_multiply_fusion.1
  20.9 1.1 convolution_subtract_fusion.1
  22.0 80.2 %all-gather.2.cloned.1.call-done = bf16[16,8,128,128]{3,2,1,0:T(8,128)(2,1)} async-done(((bf16[1,8,128,128]{3,2,1,0:T(8,128)(2,1)}), bf16[16,8,128,128]{3,2,1,0:T(8,128)(2,1)}) %all-gather.2.cloned.1.call-update) | async-done | bytes 4194320 | tf_op jit(solution)/shard_map/all_gather | solution.py:127
  102.2 3.3 fusion.125
  105.8 1.9 copy-done.1
  107.7 2.4 fusion
  110.1 0.6 fusion.123
  111.8 1.9 fusion.5
  114.6 1.0 fusion.33
  117.0 1.1 convert_element_type.113
  120.2 0.8 copy.266
  121.0 13.4 %all-to-all-start = ((bf16[8,128,256]{2,1,0:T(8,128)(2,1)}), bf16[8,128,256]{2,1,0:T(8,128)(2,1)S(1)}, u32[]{:S(2)}, u32[]{:S(2)}) async-start(bf16[8,128,256]{2,1,0:T(8,128)(2,1)} %bitcast.179), calls=%async_computation | async-start | bytes 1048576 | tf_op jit(solution)/shard_map/all_to_all | solution.py:170
  134.4 9.5 %all-to-all-done = bf16[8,128,256]{2,1,0:T(8,128)(2,1)S(1)} async-done(((bf16[8,128,256]{2,1,0:T(8,128)(2,1)}), bf16[8,128,256]{2,1,0:T(8,128)(2,1)S(1)}, u32[]{:S(2)}, u32[]{:S(2)}) %all-to-all-start) | async-done | bytes 524320 | tf_op jit(solution)/shard_map/all_to_all | solution.py:170
  144.0 0.9 add_convert_fusion.1
  144.9 0.8 broadcast_in_dim.37
  145.7 4.3 %all-to-all-start.1 = ((bf16[8,128,256]{2,1,0:T(8,128)(2,1)}), bf16[8,128,256]{2,1,0:T(8,128)(2,1)S(1)}, u32[]{:S(2)}, u32[]{:S(2)}) async-start(bf16[8,128,256]{2,1,0:T(8,128)(2,1)} %broadcast_in_dim.37), calls=%async_computation.1 | async-start | bytes 1048576 | tf_op jit(solution)/shard_map/all_to_all | solution.py:177
  150.4 9.1 %all-to-all-done.1 = bf16[8,128,256]{2,1,0:T(8,128)(2,1)S(1)} async-done(((bf16[8,128,256]{2,1,0:T(8,128)(2,1)}), bf16[8,128,256]{2,1,0:T(8,128)(2,1)S(1)}, u32[]{:S(2)}, u32[]{:S(2)}) %all-to-all-start.1) | async-done | bytes 524320 | tf_op jit(solution)/shard_map/all_to_all | solution.py:177
  161.0 74.9 %all_to_all.25 = bf16[16,20,2048]{2,1,0:T(8,128)(2,1)} all-to-all(bf16[16,20,2048]{2,1,0:T(8,128)(2,1)S(1)} %convolution_convert_fusion), channel_id=1, replica_groups=mesh['dp'=8,'seq'=16,'head'=8] {'seq'}, dimensions={0} | all-to-all | bytes 2621440 | tf_op jit(solution)/shard_map/all_to_all | solution.py:208
  235.9 2.3 reshape.187
  238.2 3.3 fusion.12
  241.4 4.4 %convolution_convert_fusion.1 = bf16[320,2048]{1,0:T(8,128)(2,1)} fusion(bf16[1,512,2048]{2,1,0:T(8,128)(2,1)S(1)} %copy-done, bf16[320,2048]{1,0:T(8,128)(2,1)S(1)} %reshape.187, bf16[1,2048,512]{2,1,0:T(8,128)(2,1)} %param.30, f32[320,512]{1,0:T(8,128)} %fusion.12), kind=kOutput, calls=%fused_computation.8 | convolution fusion | flops 1343815680 | bytes 7471104 | tf_op jit(solution)/shard_map/dot_general | solution.py:214
  245.8 3.2 reshape.188
  249.0 12.3 %all-to-all-start.3 = ((bf16[16,20,2048]{2,1,0:T(8,128)(2,1)}), bf16[16,20,2048]{2,1,0:T(8,128)(2,1)}, u32[]{:S(2)}, u32[]{:S(2)}) async-start(bf16[16,20,2048]{2,1,0:T(8,128)(2,1)} %reshape.188), calls=%async_computation.3 | async-start | bytes 3145728 | tf_op jit(solution)/shard_map/all_to_all | solution.py:215
  261.5 68.9 %all-to-all-done.3 = bf16[16,20,2048]{2,1,0:T(8,128)(2,1)} async-done(((bf16[16,20,2048]{2,1,0:T(8,128)(2,1)}), bf16[16,20,2048]{2,1,0:T(8,128)(2,1)}, u32[]{:S(2)}, u32[]{:S(2)}) %all-to-all-start.3) | async-done | bytes 1310752 | tf_op jit(solution)/shard_map/all_to_all | solution.py:215
  330.4 1.9 fusion.4
  332.3 18.0 %all_to_all.26 = bf16[8,128,256]{2,1,0:T(8,128)(2,1)S(1)} all-to-all(bf16[8,128,256]{2,1,0:T(8,128)(2,1)S(1)} %bitcast.185), channel_id=1, replica_groups=mesh['dp'=8,'seq'=16,'head'=8] {'head'}, dimensions={0} | all-to-all | bytes 1048576 | tf_op jit(solution)/shard_map/all_to_all | solution.py:227
  350.4 0.6 add_convert_fusion
  (129 shorter events, 16.4 us)
Async XLA Ops:
  6.5 234.9 %copy-start = (bf16[1,512,2048]{2,1,0:T(8,128)(2,1)S(1)}, bf16[1,512,2048]{2,1,0:T(8,128)(2,1)}, u32[]{:S(2)}) copy-start(bf16[1,512,2048]{2,1,0:T(8,128)(2,1)} %param.31) | copy-start | bytes 6291460
  6.5 95.7 %all-gather.2.cloned.1.call-start = ((), (), s32[]{:S(2)}) async-start(), calls=%async_computation.5 | async-start | bytes 4456448 | tf_op jit(solution)/shard_map/all_gather | solution.py:127
  9.1 6.6 %copy-start.7 = (f32[128,4]{0,1:T(4,128)}, f32[128,4]{0,1:T(4,128)S(1)}, u32[]{:S(2)}) copy-start(f32[128,4]{0,1:T(4,128)S(1)} %copy.207) | copy-start | bytes 6148
  14.0 1.8 copy-start.12
  14.0 1.9 copy-start.6
  15.9 0.6 copy-start.13
  16.7 2.8 copy-start.9
  17.4 2.7 copy-start.5
  17.4 2.8 copy-start.8
  18.0 2.9 copy-start.14
  105.5 2.2 copy-start.1
  114.6 1.1 copy-start.4
  116.9 1.4 copy-start.3
  118.0 1.6 copy-start.16
  118.0 1.7 copy-start.2
  120.2 29.8 %copy-start.10 = (s32[128,10]{0,1:T(8,128)S(1)}, s32[128,10]{0,1:T(8,128)}, u32[]{:S(2)}) copy-start(s32[128,10]{0,1:T(8,128)} %param.27) | copy-start | bytes 15364
  121.0 22.9 %all-to-all-start = ((bf16[8,128,256]{2,1,0:T(8,128)(2,1)}), bf16[8,128,256]{2,1,0:T(8,128)(2,1)S(1)}, u32[]{:S(2)}, u32[]{:S(2)}) async-start(bf16[8,128,256]{2,1,0:T(8,128)(2,1)} %bitcast.179), calls=%async_computation | async-start | bytes 1048576 | tf_op jit(solution)/shard_map/all_to_all | solution.py:170
  144.0 16.0 %copy-start.15 = (f32[2048]{0:T(1024)S(1)}, f32[2048]{0:T(1024)}, u32[]{:S(2)}) copy-start(f32[2048]{0:T(1024)} %param.26) | copy-start | bytes 24580
  145.7 13.8 %all-to-all-start.1 = ((bf16[8,128,256]{2,1,0:T(8,128)(2,1)}), bf16[8,128,256]{2,1,0:T(8,128)(2,1)S(1)}, u32[]{:S(2)}, u32[]{:S(2)}) async-start(bf16[8,128,256]{2,1,0:T(8,128)(2,1)} %broadcast_in_dim.37), calls=%async_computation.1 | async-start | bytes 1048576 | tf_op jit(solution)/shard_map/all_to_all | solution.py:177
  249.0 12.4 %copy-start.11 = (f32[128,10]{0,1:T(8,128)S(1)}, f32[128,10]{0,1:T(8,128)}, u32[]{:S(2)}) copy-start(f32[128,10]{0,1:T(8,128)} %param.28) | copy-start | bytes 15364
  249.0 81.3 %all-to-all-start.3 = ((bf16[16,20,2048]{2,1,0:T(8,128)(2,1)}), bf16[16,20,2048]{2,1,0:T(8,128)(2,1)}, u32[]{:S(2)}, u32[]{:S(2)}) async-start(bf16[16,20,2048]{2,1,0:T(8,128)(2,1)} %reshape.188), calls=%async_computation.3 | async-start | bytes 3145728 | tf_op jit(solution)/shard_map/all_to_all | solution.py:215
Sparse Core Ops, SparseCore 0:
  19.5 82.6 all-gather.1

commit v3 on v2

--- a/solution.py
+++ b/solution.py
@@ -124,11 +124,24 @@
         query_inner, carried_state
     )
     core_local = batch_product(query_inner, new_contribution)
-    pairs = lax.all_gather(
-        jnp.concatenate([state_map, state_increment], axis=0).astype(jnp.bfloat16), "seq"
-    )
+    own_pair = jnp.concatenate([state_map, state_increment], axis=0).astype(jnp.bfloat16)
+    ring = lax.axis_size("seq")
+    position = lax.axis_index("seq")
+    forward_pairs = [(j, (j + 1) % ring) for j in range(ring)]
+    backward_pairs = [(j, (j - 1) % ring) for j in range(ring)]
+    pairs = jnp.zeros((ring,) + own_pair.shape, own_pair.dtype)
+    pairs = lax.dynamic_update_index_in_dim(pairs, own_pair, position, 0)
+    going_up = own_pair
+    going_down = own_pair
+    for step in range(1, ring // 2 + 1):
+        going_up = lax.ppermute(going_up, "seq", forward_pairs)
+        pairs = lax.dynamic_update_index_in_dim(pairs, going_up, (position - step) % ring, 0)
+        if step < ring - step:
+            going_down = lax.ppermute(going_down, "seq", backward_pairs)
+            pairs = lax.dynamic_update_index_in_dim(
+                pairs, going_down, (position + step) % ring, 0
+            )
     segments = pairs.astype(jnp.float32)
-    position = lax.axis_index("seq")
     levels = [segments]
     while segments.shape[0] > 2:
         earlier = segments[0::2]

time: 359 us -> 355 us (0.989)
  waiting for transfers between devices: 168 us -> 96.1 us
  starting transfers between devices: 30 us -> 91 us
  local copies, waits for them, and re-layouts: 17.6 us -> 33.9 us
  between operations: 14.3 us -> 1.07 us
    all_gather x1 -> x0, waiting for transfers between devices: 80.2 us -> none  [on_device(): lax.all_gather(jnp.concatenate([state_map, state_increment], axis=0).asty...]
    ppermute x0 -> x15, starting transfers between devices: none -> 61.7 us  [the longest x7 43.3 us: on_device(): going_down = lax.ppermute(going_down, 'seq', backward_pairs)]
    dynamic_update_slice x0 -> x15, local copies, waits for them, and re-layouts: none -> 12.9 us  [the longest x8 6.81 us: on_device(): lax.dynamic_update_index_in_dim(pairs, going_up, (position - step) % ring...]
    ppermute x0 -> x15, waiting for transfers between devices: none -> 8.66 us  [the longest x8 8.65 us: on_device(): going_up = lax.ppermute(going_up, 'seq', forward_pairs)]
  transfers between devices with their start and end apart: 4 -> 18, of which waited for: 4 -> 10; matrix products, arithmetic and copies ran while one was open for 1% -> 6% of each run, Pallas kernels for 0% -> 0%
where the time goes in v3:
time: 355 us; the launch traced here: 354 us
  waiting for transfers between devices  96.1 us (27%)
  blocking collectives  91.2 us (26%)
  starting transfers between devices  91 us (26%)
  local copies, waits for them, and re-layouts  33.9 us (10%)
  matrix products  29.7 us (8%)
  other arithmetic  10.8 us (3%)
    all_to_all x1, blocking collectives, on_device(): lax.all_to_all(outgoing, 'seq', split_axis=0, concat_axis=0, tiled=True)  73.2 us
    all_to_all x1, waiting for transfers between devices, on_device(): lax.all_to_all(result.reshape(peer_count, item_count, model_width), 'seq'...  68.9 us
    ppermute x7, starting transfers between devices, on_device(): going_down = lax.ppermute(going_down, 'seq', backward_pairs)  43.3 us
    ppermute x8, starting transfers between devices, on_device(): going_up = lax.ppermute(going_up, 'seq', forward_pairs)  18.4 us
    all_to_all x1, blocking collectives, on_device(): lax.all_to_all(moe_pieces.transpose(1, 0, 2), 'head', split_axis=0, conca...  18 us
    all_to_all x1, starting transfers between devices, on_device(): lax.all_to_all(attn_pieces.transpose(1, 0, 2), 'head', split_axis=0, conc...  12.9 us
    all_to_all x1, starting transfers between devices, on_device(): lax.all_to_all(result.reshape(peer_count, item_count, model_width), 'seq'...  12.2 us
    all_to_all x1, waiting for transfers between devices, on_device(): lax.all_to_all(attn_pieces.transpose(1, 0, 2), 'head', split_axis=0, conc...  9.48 us
  transfers between devices with their start and end apart: 18, of which 10 were waited for; matrix products, arithmetic and copies ran while one was open for 6% of the time, Pallas kernels for 0%

profile of v3, /device:TPU:1, one launch (start us, length us, event | category | flops | bytes accessed | tf_op | source)
XLA Modules:
  0.0 353.7 jit_solution(2946614032562200258)
XLA Ops:
  13.6 4.8 %collective-permute-start = (bf16[8,128,128]{2,1,0:T(8,128)(2,1)}, bf16[8,128,128]{2,1,0:T(8,128)(2,1)}, u32[]{:S(2)}, u32[]{:S(2)}) collective-permute-start(bf16[8,128,128]{2,1,0:T(8,128)(2,1)} %pad_maximum_fusion.2), channel_id=1, source_target_pairs={{0,8},{8,16},{16,24},{24,32},{32,40},{40,48},{48,56},{56,64},{64,7... | collective-permute-start | bytes 786440 | tf_op jit(solution)/shard_map/ppermute | solution.py:137
  18.4 15.9 %collective-permute-start.1 = (bf16[8,128,128]{2,1,0:T(8,128)(2,1)}, bf16[8,128,128]{2,1,0:T(8,128)(2,1)}, u32[]{:S(2)}, u32[]{:S(2)}) collective-permute-start(bf16[8,128,128]{2,1,0:T(8,128)(2,1)} %pad_maximum_fusion.2), channel_id=1, source_target_pairs={{0,120},{8,0},{16,8},{24,16},{32,24},{40,32},{48,40},{56,48},{64,5... | collective-permute-start | bytes 786440 | tf_op jit(solution)/shard_map/ppermute | solution.py:140
  37.3 3.0 broadcast_in_dim.126
  42.2 1.9 collective-permute-start.2
  44.2 4.6 %collective-permute-start.3 = (bf16[8,128,128]{2,1,0:T(8,128)(2,1)}, bf16[8,128,128]{2,1,0:T(8,128)(2,1)S(1)}, u32[]{:S(2)}, u32[]{:S(2)}) collective-permute-start(bf16[8,128,128]{2,1,0:T(8,128)(2,1)} %collective-permute-done.1), channel_id=1, source_target_pairs={{0,120},{8,0},{16,8},{24,16},{32,24},{40,32},{48,40},{56,48},{64,5... | collective-permute-start | bytes 786440 | tf_op jit(solution)/shard_map/ppermute | solution.py:140
  52.4 1.9 collective-permute-start.4
  54.3 4.6 %collective-permute-start.5 = (bf16[8,128,128]{2,1,0:T(8,128)(2,1)S(1)}, bf16[8,128,128]{2,1,0:T(8,128)(2,1)S(1)}, u32[]{:S(2)}, u32[]{:S(2)}) collective-permute-start(bf16[8,128,128]{2,1,0:T(8,128)(2,1)S(1)} %collective-permute-done.3), channel_id=1, source_target_pairs={{0,120},{8,0},{16,8},{24,16},{32,24},{40,32},{48,40},{56,48},{64,5... | collective-permute-start | bytes 786440 | tf_op jit(solution)/shard_map/ppermute | solution.py:140
  61.4 1.9 collective-permute-start.6
  63.4 4.6 %collective-permute-start.7 = (bf16[8,128,128]{2,1,0:T(8,128)(2,1)S(1)}, bf16[8,128,128]{2,1,0:T(8,128)(2,1)S(1)}, u32[]{:S(2)}, u32[]{:S(2)}) collective-permute-start(bf16[8,128,128]{2,1,0:T(8,128)(2,1)S(1)} %collective-permute-done.5), channel_id=1, source_target_pairs={{0,120},{8,0},{16,8},{24,16},{32,24},{40,32},{48,40},{56,48},{64,5... | collective-permute-start | bytes 786440 | tf_op jit(solution)/shard_map/ppermute | solution.py:140
  69.7 1.9 collective-permute-start.8
  71.7 4.6 %collective-permute-start.9 = (bf16[8,128,128]{2,1,0:T(8,128)(2,1)S(1)}, bf16[8,128,128]{2,1,0:T(8,128)(2,1)S(1)}, u32[]{:S(2)}, u32[]{:S(2)}) collective-permute-start(bf16[8,128,128]{2,1,0:T(8,128)(2,1)S(1)} %collective-permute-done.7), channel_id=1, source_target_pairs={{0,120},{8,0},{16,8},{24,16},{32,24},{40,32},{48,40},{56,48},{64,5... | collective-permute-start | bytes 786440 | tf_op jit(solution)/shard_map/ppermute | solution.py:140
  78.1 1.9 collective-permute-start.10
  80.0 4.6 %collective-permute-start.11 = (bf16[8,128,128]{2,1,0:T(8,128)(2,1)S(1)}, bf16[8,128,128]{2,1,0:T(8,128)(2,1)S(1)}, u32[]{:S(2)}, u32[]{:S(2)}) collective-permute-start(bf16[8,128,128]{2,1,0:T(8,128)(2,1)S(1)} %collective-permute-done.9), channel_id=1, source_target_pairs={{0,120},{8,0},{16,8},{24,16},{32,24},{40,32},{48,40},{56,48},{64,5... | collective-permute-start | bytes 786440 | tf_op jit(solution)/shard_map/ppermute | solution.py:140
  86.4 1.9 collective-permute-start.12
  88.3 4.6 %collective-permute-start.13 = (bf16[8,128,128]{2,1,0:T(8,128)(2,1)S(1)}, bf16[8,128,128]{2,1,0:T(8,128)(2,1)S(1)}, u32[]{:S(2)}, u32[]{:S(2)}) collective-permute-start(bf16[8,128,128]{2,1,0:T(8,128)(2,1)S(1)} %collective-permute-done.11), channel_id=1, source_target_pairs={{0,120},{8,0},{16,8},{24,16},{32,24},{40,32},{48,40},{56,48},{64,5... | collective-permute-start | bytes 786440 | tf_op jit(solution)/shard_map/ppermute | solution.py:140
  94.7 2.1 collective-permute-start.14
  98.3 5.9 %collective-permute-done.14 = bf16[8,128,128]{2,1,0:T(8,128)(2,1)S(1)} collective-permute-done((bf16[8,128,128]{2,1,0:T(8,128)(2,1)S(1)}, bf16[8,128,128]{2,1,0:T(8,128)(2,1)S(1)}, u32[]{:S(2)}, u32[]{:S(2)}) %collective-permute-start.14) | collective-permute-done | bytes 262176 | tf_op jit(solution)/shard_map/ppermute | solution.py:137
  104.9 3.3 fusion.123
  108.2 3.3 convert_element_type.113
  111.8 3.6 %fusion = f32[8,4,128,256]{3,2,1,0:T(8,128)S(1)} fusion(f32[8,4,128,128]{3,2,1,0:T(8,128)S(1)} %get-tuple-element.10, f32[8,4,128,128]{3,2,1,0:T(8,128)S(1)} %get-tuple-element.9, bf16[16,8,128,128]{3,2,1,0:T(8,128)(2,1)} %bitcast_dynamic-update-slice_fusion), kind=kOutput, calls=%fused_computation.3 | convolution fusion | flops 1611661312 | bytes 10485760 | tf_op jit(solution)/shard_map/phij,phjk->phik/dot_general | solution.py:149
  126.0 12.9 %all-to-all-start = ((bf16[8,128,256]{2,1,0:T(8,128)(2,1)}), bf16[8,128,256]{2,1,0:T(8,128)(2,1)S(1)}, u32[]{:S(2)}, u32[]{:S(2)}) async-start(bf16[8,128,256]{2,1,0:T(8,128)(2,1)} %bitcast.207), calls=%async_computation | async-start | bytes 1048576 | tf_op jit(solution)/shard_map/all_to_all | solution.py:183
  138.9 9.5 %all-to-all-done = bf16[8,128,256]{2,1,0:T(8,128)(2,1)S(1)} async-done(((bf16[8,128,256]{2,1,0:T(8,128)(2,1)}), bf16[8,128,256]{2,1,0:T(8,128)(2,1)S(1)}, u32[]{:S(2)}, u32[]{:S(2)}) %all-to-all-start) | async-done | bytes 524320 | tf_op jit(solution)/shard_map/all_to_all | solution.py:183
  150.1 4.3 %all-to-all-start.1 = ((bf16[8,128,256]{2,1,0:T(8,128)(2,1)}), bf16[8,128,256]{2,1,0:T(8,128)(2,1)S(1)}, u32[]{:S(2)}, u32[]{:S(2)}) async-start(bf16[8,128,256]{2,1,0:T(8,128)(2,1)} %broadcast_in_dim.144), calls=%async_computation.1 | async-start | bytes 1048576 | tf_op jit(solution)/shard_map/all_to_all | solution.py:190
  154.8 9.1 %all-to-all-done.1 = bf16[8,128,256]{2,1,0:T(8,128)(2,1)S(1)} async-done(((bf16[8,128,256]{2,1,0:T(8,128)(2,1)}), bf16[8,128,256]{2,1,0:T(8,128)(2,1)S(1)}, u32[]{:S(2)}, u32[]{:S(2)}) %all-to-all-start.1) | async-done | bytes 524320 | tf_op jit(solution)/shard_map/all_to_all | solution.py:190
  165.4 73.2 %all_to_all.25 = bf16[16,20,2048]{2,1,0:T(8,128)(2,1)} all-to-all(bf16[16,20,2048]{2,1,0:T(8,128)(2,1)S(1)} %convolution_convert_fusion), channel_id=1, replica_groups=mesh['dp'=8,'seq'=16,'head'=8] {'seq'}, dimensions={0} | all-to-all | bytes 2621440 | tf_op jit(solution)/shard_map/all_to_all | solution.py:221
  238.6 2.3 reshape.187
  240.9 3.3 fusion.12
  244.1 4.4 %convolution_convert_fusion.1 = bf16[320,2048]{1,0:T(8,128)(2,1)} fusion(bf16[1,512,2048]{2,1,0:T(8,128)(2,1)S(1)} %copy-done, bf16[320,2048]{1,0:T(8,128)(2,1)S(1)} %reshape.187, bf16[1,2048,512]{2,1,0:T(8,128)(2,1)} %param.30, f32[320,512]{1,0:T(8,128)} %fusion.12), kind=kOutput, calls=%fused_computation.8 | convolution fusion | flops 1343815680 | bytes 7471104 | tf_op jit(solution)/shard_map/dot_general | solution.py:227
  248.6 3.2 reshape.188
  251.8 12.2 %all-to-all-start.3 = ((bf16[16,20,2048]{2,1,0:T(8,128)(2,1)}), bf16[16,20,2048]{2,1,0:T(8,128)(2,1)}, u32[]{:S(2)}, u32[]{:S(2)}) async-start(bf16[16,20,2048]{2,1,0:T(8,128)(2,1)} %reshape.188), calls=%async_computation.3 | async-start | bytes 3145728 | tf_op jit(solution)/shard_map/all_to_all | solution.py:228
  264.1 68.9 %all-to-all-done.3 = bf16[16,20,2048]{2,1,0:T(8,128)(2,1)} async-done(((bf16[16,20,2048]{2,1,0:T(8,128)(2,1)}), bf16[16,20,2048]{2,1,0:T(8,128)(2,1)}, u32[]{:S(2)}, u32[]{:S(2)}) %all-to-all-start.3) | async-done | bytes 1310752 | tf_op jit(solution)/shard_map/all_to_all | solution.py:228
  334.9 18.0 %all_to_all.26 = bf16[8,128,256]{2,1,0:T(8,128)(2,1)S(1)} all-to-all(bf16[8,128,256]{2,1,0:T(8,128)(2,1)S(1)} %bitcast.213), channel_id=1, replica_groups=mesh['dp'=8,'seq'=16,'head'=8] {'head'}, dimensions={0} | all-to-all | bytes 1048576 | tf_op jit(solution)/shard_map/all_to_all | solution.py:240
  (169 shorter events, 50.8 us)
Async XLA Ops:
  0.0 244.1 %copy-start = (bf16[1,512,2048]{2,1,0:T(8,128)(2,1)S(1)}, bf16[1,512,2048]{2,1,0:T(8,128)(2,1)}, u32[]{:S(2)}) copy-start(bf16[1,512,2048]{2,1,0:T(8,128)(2,1)} %param.31) | copy-start | bytes 6291460
  2.6 6.6 %copy-start.7 = (f32[128,4]{0,1:T(4,128)}, f32[128,4]{0,1:T(4,128)S(1)}, u32[]{:S(2)}) copy-start(f32[128,4]{0,1:T(4,128)S(1)} %copy.219) | copy-start | bytes 6148
  7.2 2.1 copy-start.10
  9.3 2.3 copy-start.11
  12.8 23.0 %copy-start.2 = (bf16[4,128,128]{2,1,0:T(8,128)(2,1)}, bf16[4,128,128]{2,1,0:T(8,128)(2,1)S(1)}, u32[]{:S(2)}) copy-start(bf16[4,128,128]{2,1,0:T(8,128)(2,1)S(1)} %fusion.29) | copy-start | bytes 393220
  13.6 28.7 %collective-permute-start = (bf16[8,128,128]{2,1,0:T(8,128)(2,1)}, bf16[8,128,128]{2,1,0:T(8,128)(2,1)}, u32[]{:S(2)}, u32[]{:S(2)}) collective-permute-start(bf16[8,128,128]{2,1,0:T(8,128)(2,1)} %pad_maximum_fusion.2), channel_id=1, source_target_pairs={{0,8},{8,16},{16,24},{24,32},{32,40},{40,48},{48,56},{56,64},{64,7... | collective-permute-start | bytes 786440 | tf_op jit(solution)/shard_map/ppermute | solution.py:137
  18.4 25.8 %collective-permute-start.1 = (bf16[8,128,128]{2,1,0:T(8,128)(2,1)}, bf16[8,128,128]{2,1,0:T(8,128)(2,1)}, u32[]{:S(2)}, u32[]{:S(2)}) collective-permute-start(bf16[8,128,128]{2,1,0:T(8,128)(2,1)} %pad_maximum_fusion.2), channel_id=1, source_target_pairs={{0,120},{8,0},{16,8},{24,16},{32,24},{40,32},{48,40},{56,48},{64,5... | collective-permute-start | bytes 786440 | tf_op jit(solution)/shard_map/ppermute | solution.py:140
  35.8 4.5 %copy-start.3 = (bf16[4,128,128]{2,1,0:T(8,128)(2,1)S(1)}, bf16[4,128,128]{2,1,0:T(8,128)(2,1)}, u32[]{:S(2)}) copy-start(bf16[4,128,128]{2,1,0:T(8,128)(2,1)} %copy-done.2) | copy-start | bytes 393220
  37.3 3.8 %copy-start.6 = (bf16[128,512]{1,0:T(8,128)(2,1)S(1)}, bf16[128,512]{1,0:T(8,128)(2,1)}, u32[]{:S(2)}) copy-start(bf16[128,512]{1,0:T(8,128)(2,1)} %param.20) | copy-start | bytes 393220
  37.3 4.5 %copy-start.12 = (f32[4,128]{1,0:T(4,128)S(1)}, f32[4,128]{1,0:T(4,128)}, u32[]{:S(2)}) copy-start(f32[4,128]{1,0:T(4,128)} %copy-done.11) | copy-start | bytes 6148
  42.2 10.2 %collective-permute-start.2 = (bf16[8,128,128]{2,1,0:T(8,128)(2,1)}, bf16[8,128,128]{2,1,0:T(8,128)(2,1)S(1)}, u32[]{:S(2)}, u32[]{:S(2)}) collective-permute-start(bf16[8,128,128]{2,1,0:T(8,128)(2,1)} %collective-permute-done), channel_id=1, source_target_pairs={{0,8},{8,16},{16,24},{24,32},{32,40},{40,48},{48,56},{56,64},{64,7... | collective-permute-start | bytes 786440 | tf_op jit(solution)/shard_map/ppermute | solution.py:137
  44.2 10.1 %collective-permute-start.3 = (bf16[8,128,128]{2,1,0:T(8,128)(2,1)}, bf16[8,128,128]{2,1,0:T(8,128)(2,1)S(1)}, u32[]{:S(2)}, u32[]{:S(2)}) collective-permute-start(bf16[8,128,128]{2,1,0:T(8,128)(2,1)} %collective-permute-done.1), channel_id=1, source_target_pairs={{0,120},{8,0},{16,8},{24,16},{32,24},{40,32},{48,40},{56,48},{64,5... | collective-permute-start | bytes 786440 | tf_op jit(solution)/shard_map/ppermute | solution.py:140
  52.4 9.0 %collective-permute-start.4 = (bf16[8,128,128]{2,1,0:T(8,128)(2,1)S(1)}, bf16[8,128,128]{2,1,0:T(8,128)(2,1)S(1)}, u32[]{:S(2)}, u32[]{:S(2)}) collective-permute-start(bf16[8,128,128]{2,1,0:T(8,128)(2,1)S(1)} %collective-permute-done.2), channel_id=1, source_target_pairs={{0,8},{8,16},{16,24},{24,32},{32,40},{40,48},{48,56},{56,64},{64,7... | collective-permute-start | bytes 786440 | tf_op jit(solution)/shard_map/ppermute | solution.py:137
  54.3 9.0 %collective-permute-start.5 = (bf16[8,128,128]{2,1,0:T(8,128)(2,1)S(1)}, bf16[8,128,128]{2,1,0:T(8,128)(2,1)S(1)}, u32[]{:S(2)}, u32[]{:S(2)}) collective-permute-start(bf16[8,128,128]{2,1,0:T(8,128)(2,1)S(1)} %collective-permute-done.3), channel_id=1, source_target_pairs={{0,120},{8,0},{16,8},{24,16},{32,24},{40,32},{48,40},{56,48},{64,5... | collective-permute-start | bytes 786440 | tf_op jit(solution)/shard_map/ppermute | solution.py:140
  61.4 8.3 %collective-permute-start.6 = (bf16[8,128,128]{2,1,0:T(8,128)(2,1)S(1)}, bf16[8,128,128]{2,1,0:T(8,128)(2,1)S(1)}, u32[]{:S(2)}, u32[]{:S(2)}) collective-permute-start(bf16[8,128,128]{2,1,0:T(8,128)(2,1)S(1)} %collective-permute-done.4), channel_id=1, source_target_pairs={{0,8},{8,16},{16,24},{24,32},{32,40},{40,48},{48,56},{56,64},{64,7... | collective-permute-start | bytes 786440 | tf_op jit(solution)/shard_map/ppermute | solution.py:137
  63.4 8.3 %collective-permute-start.7 = (bf16[8,128,128]{2,1,0:T(8,128)(2,1)S(1)}, bf16[8,128,128]{2,1,0:T(8,128)(2,1)S(1)}, u32[]{:S(2)}, u32[]{:S(2)}) collective-permute-start(bf16[8,128,128]{2,1,0:T(8,128)(2,1)S(1)} %collective-permute-done.5), channel_id=1, source_target_pairs={{0,120},{8,0},{16,8},{24,16},{32,24},{40,32},{48,40},{56,48},{64,5... | collective-permute-start | bytes 786440 | tf_op jit(solution)/shard_map/ppermute | solution.py:140
  69.7 8.3 %collective-permute-start.8 = (bf16[8,128,128]{2,1,0:T(8,128)(2,1)S(1)}, bf16[8,128,128]{2,1,0:T(8,128)(2,1)S(1)}, u32[]{:S(2)}, u32[]{:S(2)}) collective-permute-start(bf16[8,128,128]{2,1,0:T(8,128)(2,1)S(1)} %collective-permute-done.6), channel_id=1, source_target_pairs={{0,8},{8,16},{16,24},{24,32},{32,40},{40,48},{48,56},{56,64},{64,7... | collective-permute-start | bytes 786440 | tf_op jit(solution)/shard_map/ppermute | solution.py:137
  71.7 8.3 %collective-permute-start.9 = (bf16[8,128,128]{2,1,0:T(8,128)(2,1)S(1)}, bf16[8,128,128]{2,1,0:T(8,128)(2,1)S(1)}, u32[]{:S(2)}, u32[]{:S(2)}) collective-permute-start(bf16[8,128,128]{2,1,0:T(8,128)(2,1)S(1)} %collective-permute-done.7), channel_id=1, source_target_pairs={{0,120},{8,0},{16,8},{24,16},{32,24},{40,32},{48,40},{56,48},{64,5... | collective-permute-start | bytes 786440 | tf_op jit(solution)/shard_map/ppermute | solution.py:140
  78.1 8.3 %collective-permute-start.10 = (bf16[8,128,128]{2,1,0:T(8,128)(2,1)S(1)}, bf16[8,128,128]{2,1,0:T(8,128)(2,1)S(1)}, u32[]{:S(2)}, u32[]{:S(2)}) collective-permute-start(bf16[8,128,128]{2,1,0:T(8,128)(2,1)S(1)} %collective-permute-done.8), channel_id=1, source_target_pairs={{0,8},{8,16},{16,24},{24,32},{32,40},{40,48},{48,56},{56,64},{64,7... | collective-permute-start | bytes 786440 | tf_op jit(solution)/shard_map/ppermute | solution.py:137
  80.0 8.3 %collective-permute-start.11 = (bf16[8,128,128]{2,1,0:T(8,128)(2,1)S(1)}, bf16[8,128,128]{2,1,0:T(8,128)(2,1)S(1)}, u32[]{:S(2)}, u32[]{:S(2)}) collective-permute-start(bf16[8,128,128]{2,1,0:T(8,128)(2,1)S(1)} %collective-permute-done.9), channel_id=1, source_target_pairs={{0,120},{8,0},{16,8},{24,16},{32,24},{40,32},{48,40},{56,48},{64,5... | collective-permute-start | bytes 786440 | tf_op jit(solution)/shard_map/ppermute | solution.py:140
  86.4 8.4 %collective-permute-start.12 = (bf16[8,128,128]{2,1,0:T(8,128)(2,1)S(1)}, bf16[8,128,128]{2,1,0:T(8,128)(2,1)S(1)}, u32[]{:S(2)}, u32[]{:S(2)}) collective-permute-start(bf16[8,128,128]{2,1,0:T(8,128)(2,1)S(1)} %collective-permute-done.10), channel_id=1, source_target_pairs={{0,8},{8,16},{16,24},{24,32},{32,40},{40,48},{48,56},{56,64},{64,7... | collective-permute-start | bytes 786440 | tf_op jit(solution)/shard_map/ppermute | solution.py:137
  88.3 9.3 %collective-permute-start.13 = (bf16[8,128,128]{2,1,0:T(8,128)(2,1)S(1)}, bf16[8,128,128]{2,1,0:T(8,128)(2,1)S(1)}, u32[]{:S(2)}, u32[]{:S(2)}) collective-permute-start(bf16[8,128,128]{2,1,0:T(8,128)(2,1)S(1)} %collective-permute-done.11), channel_id=1, source_target_pairs={{0,120},{8,0},{16,8},{24,16},{32,24},{40,32},{48,40},{56,48},{64,5... | collective-permute-start | bytes 786440 | tf_op jit(solution)/shard_map/ppermute | solution.py:140
  94.7 9.5 %collective-permute-start.14 = (bf16[8,128,128]{2,1,0:T(8,128)(2,1)S(1)}, bf16[8,128,128]{2,1,0:T(8,128)(2,1)S(1)}, u32[]{:S(2)}, u32[]{:S(2)}) collective-permute-start(bf16[8,128,128]{2,1,0:T(8,128)(2,1)S(1)} %collective-permute-done.12), channel_id=1, source_target_pairs={{0,8},{8,16},{16,24},{24,32},{32,40},{40,48},{48,56},{56,64},{64,7... | collective-permute-start | bytes 786440 | tf_op jit(solution)/shard_map/ppermute | solution.py:137
  120.8 3.7 %copy-start.4 = (f32[128,512]{0,1:T(8,128)S(1)}, f32[128,512]{0,1:T(8,128)}, u32[]{:S(2)}) copy-start(f32[128,512]{0,1:T(8,128)} %copy.241) | copy-start | bytes 786436
  120.8 3.7 %copy-start.14 = (f32[128]{0:T(128)S(1)}, f32[128]{0:T(128)}, u32[]{:S(2)}) copy-start(f32[128]{0:T(128)} %param.24) | copy-start | bytes 1540
  121.3 3.4 copy-start.1
  125.2 29.2 %copy-start.8 = (s32[128,10]{0,1:T(8,128)S(1)}, s32[128,10]{0,1:T(8,128)}, u32[]{:S(2)}) copy-start(s32[128,10]{0,1:T(8,128)} %param.27) | copy-start | bytes 15364
  126.0 38.5 %copy-start.13 = (f32[2048]{0:T(1024)S(1)}, f32[2048]{0:T(1024)}, u32[]{:S(2)}) copy-start(f32[2048]{0:T(1024)} %param.26) | copy-start | bytes 24580
  126.0 22.3 %all-to-all-start = ((bf16[8,128,256]{2,1,0:T(8,128)(2,1)}), bf16[8,128,256]{2,1,0:T(8,128)(2,1)S(1)}, u32[]{:S(2)}, u32[]{:S(2)}) async-start(bf16[8,128,256]{2,1,0:T(8,128)(2,1)} %bitcast.207), calls=%async_computation | async-start | bytes 1048576 | tf_op jit(solution)/shard_map/all_to_all | solution.py:183
  150.1 13.8 %all-to-all-start.1 = ((bf16[8,128,256]{2,1,0:T(8,128)(2,1)}), bf16[8,128,256]{2,1,0:T(8,128)(2,1)S(1)}, u32[]{:S(2)}, u32[]{:S(2)}) async-start(bf16[8,128,256]{2,1,0:T(8,128)(2,1)} %broadcast_in_dim.144), calls=%async_computation.1 | async-start | bytes 1048576 | tf_op jit(solution)/shard_map/all_to_all | solution.py:190
  248.6 15.4 %copy-start.9 = (f32[128,10]{0,1:T(8,128)S(1)}, f32[128,10]{0,1:T(8,128)}, u32[]{:S(2)}) copy-start(f32[128,10]{0,1:T(8,128)} %param.28) | copy-start | bytes 15364
  251.8 81.2 %all-to-all-start.3 = ((bf16[16,20,2048]{2,1,0:T(8,128)(2,1)}), bf16[16,20,2048]{2,1,0:T(8,128)(2,1)}, u32[]{:S(2)}, u32[]{:S(2)}) async-start(bf16[16,20,2048]{2,1,0:T(8,128)(2,1)} %reshape.188), calls=%async_computation.3 | async-start | bytes 3145728 | tf_op jit(solution)/shard_map/all_to_all | solution.py:228
  (1 other events, 1.1 us)

commit v4 on v3

--- a/solution.py
+++ b/solution.py
@@ -18,6 +18,16 @@
 
 def batch_product(left, right):
     return jnp.einsum("hij,hjk->hik", left, right, precision=precise_variant)
+
+
+def batch_product_wide(left, right_a, right_b):
+    joined = jnp.einsum(
+        "hij,hjk->hik",
+        left,
+        jnp.concatenate([right_a, right_b], axis=-1),
+        precision=precise_variant,
+    )
+    return joined
 
 
 def block_product(left, right):
@@ -129,42 +139,29 @@
     position = lax.axis_index("seq")
     forward_pairs = [(j, (j + 1) % ring) for j in range(ring)]
     backward_pairs = [(j, (j - 1) % ring) for j in range(ring)]
-    pairs = jnp.zeros((ring,) + own_pair.shape, own_pair.dtype)
-    pairs = lax.dynamic_update_index_in_dim(pairs, own_pair, position, 0)
     going_up = own_pair
     going_down = own_pair
+    later_map = None
+    later_add = None
+    opening_state = init_state
     for step in range(1, ring // 2 + 1):
         going_up = lax.ppermute(going_up, "seq", forward_pairs)
-        pairs = lax.dynamic_update_index_in_dim(pairs, going_up, (position - step) % ring, 0)
+        piece = going_up.astype(jnp.float32)
+        if later_map is None:
+            later_map = piece[:head_count]
+            later_add = piece[head_count:]
+        else:
+            joined = batch_product_wide(later_map, piece[:head_count], piece[head_count:])
+            useful = step <= position
+            later_add = jnp.where(useful, joined[..., DK:] + later_add, later_add)
+            later_map = jnp.where(useful, joined[..., :DK], later_map)
         if step < ring - step:
             going_down = lax.ppermute(going_down, "seq", backward_pairs)
-            pairs = lax.dynamic_update_index_in_dim(
-                pairs, going_down, (position + step) % ring, 0
-            )
-    segments = pairs.astype(jnp.float32)
-    levels = [segments]
-    while segments.shape[0] > 2:
-        earlier = segments[0::2]
-        later = segments[1::2]
-        joined = jnp.einsum(
-            "phij,phjk->phik",
-            later[:, :head_count],
-            jnp.concatenate([earlier[:, :head_count], earlier[:, head_count:]], axis=-1),
-            precision=precise_variant,
-        )
-        segments = jnp.concatenate(
-            [joined[..., :DK], joined[..., DK:] + later[:, head_count:]], axis=1
-        )
-        levels.append(segments)
-    opening_state = init_state
-    cursor = 0
-    for level in reversed(range(len(levels))):
-        span = 2**level
-        taken = (position // span) % 2 == 1
-        piece = lax.dynamic_index_in_dim(levels[level], cursor // span, 0, keepdims=False)
-        advanced = batch_product(piece[:head_count], opening_state) + piece[head_count:]
-        opening_state = jnp.where(taken, advanced, opening_state)
-        cursor = cursor + jnp.where(taken, span, 0)
+            piece = going_down.astype(jnp.float32)
+            advanced = batch_product(piece[:head_count], opening_state) + piece[head_count:]
+            opening_state = jnp.where(position + step >= ring, advanced, opening_state)
+    carried_open = batch_product(later_map, opening_state) + later_add
+    opening_state = jnp.where(position > 0, carried_open, opening_state)
     core = batch_product(query_effective, opening_state) + core_local
     core = core.transpose(1, 0, 2)
     gate_rows = out_gate.astype(jnp.float32).reshape(length, head_count, DV)
@@ -219,14 +216,14 @@
         "tps,td->psd", placement_map, normed, preferred_element_type=jnp.float32
     ).astype(jnp.bfloat16)
     incoming = lax.all_to_all(outgoing, "seq", split_axis=0, concat_axis=0, tiled=True)
-    item_count = incoming.shape[1]
-    flat_rows = incoming.reshape(-1, model_width)
-    gate_e = jnp.dot(flat_rows, w_gate[0], preferred_element_type=jnp.float32)
-    up_e = jnp.dot(flat_rows, w_up[0], preferred_element_type=jnp.float32)
+    gate_e = jnp.einsum("psd,dh->psh", incoming, w_gate[0], preferred_element_type=jnp.float32)
+    up_e = jnp.einsum("psd,dh->psh", incoming, w_up[0], preferred_element_type=jnp.float32)
     hidden = (jax.nn.silu(gate_e) * up_e).astype(jnp.bfloat16)
-    result = jnp.dot(hidden, w_down[0], preferred_element_type=jnp.float32).astype(jnp.bfloat16)
+    result = jnp.einsum(
+        "psh,hd->psd", hidden, w_down[0], preferred_element_type=jnp.float32
+    ).astype(jnp.bfloat16)
     returned = lax.all_to_all(
-        result.reshape(peer_count, item_count, model_width),
+        result,
         "seq",
         split_axis=0,
         concat_axis=0,

time: 355 us -> 329 us (0.927)
  local copies, waits for them, and re-layouts: 33.9 us -> 8.94 us
  waiting for transfers between devices: 96.1 us -> 102 us
  other arithmetic: 10.8 us -> 6.67 us
    dynamic_update_slice x15 -> x0, local copies, waits for them, and re-layouts: 12.9 us -> none  [the longest x8 6.81 us: on_device(): lax.dynamic_update_index_in_dim(pairs, going_up, (position - step) % ring...]
    reshape x2 -> x0, local copies, waits for them, and re-layouts: 5.49 us -> none  [the longest x1 3.21 us: on_device(): result.reshape(peer_count, item_count, model_width)]
    ppermute x8, waiting for transfers between devices: 8.65 us -> 14.1 us  [on_device(): going_up = lax.ppermute(going_up, 'seq', forward_pairs)]
    dot_general x5 -> x9, matrix products: 14.3 us -> 10.2 us  [the longest x1 5.17 us: on_device(): jnp.einsum('psh,hd->psd', hidden, w_down[0], preferred_element_type=jnp.f...]
  transfers between devices with their start and end apart: 18 -> 18, of which waited for: 10 -> 10; matrix products, arithmetic and copies ran while one was open for 6% -> 4% of each run, Pallas kernels for 0% -> 0%
where the time goes in v4:
time: 329 us; the launch traced here: 328 us
  waiting for transfers between devices  102 us (31%)
  starting transfers between devices  91.3 us (28%)
  blocking collectives  90.9 us (28%)
  matrix products  27.4 us (8%)
  local copies, waits for them, and re-layouts  8.94 us (3%)
  other arithmetic  6.67 us (2%)
    all_to_all x1, blocking collectives, on_device(): lax.all_to_all(outgoing, 'seq', split_axis=0, concat_axis=0, tiled=True)  72.9 us
    all_to_all x1, waiting for transfers between devices, on_device(): lax.all_to_all(result, 'seq', split_axis=0, concat_axis=0, tiled=True)  68.9 us
    ppermute x7, starting transfers between devices, on_device(): going_down = lax.ppermute(going_down, 'seq', backward_pairs)  43.7 us
    ppermute x8, starting transfers between devices, on_device(): going_up = lax.ppermute(going_up, 'seq', forward_pairs)  18.3 us
    all_to_all x1, blocking collectives, on_device(): lax.all_to_all(moe_pieces.transpose(1, 0, 2), 'head', split_axis=0, conca...  18 us
    ppermute x8, waiting for transfers between devices, on_device(): going_up = lax.ppermute(going_up, 'seq', forward_pairs)  14.1 us
    all_to_all x1, starting transfers between devices, on_device(): lax.all_to_all(attn_pieces.transpose(1, 0, 2), 'head', split_axis=0, conc...  12.8 us
    all_to_all x1, starting transfers between devices, on_device(): lax.all_to_all(result, 'seq', split_axis=0, concat_axis=0, tiled=True)  12.3 us
  transfers between devices with their start and end apart: 18, of which 10 were waited for; matrix products, arithmetic and copies ran while one was open for 4% of the time, Pallas kernels for 0%

profile of v4, /device:TPU:1, one launch (start us, length us, event | category | flops | bytes accessed | tf_op | source)
XLA Modules:
  0.0 327.7 jit_solution(1884875164949415152)
XLA Ops:
  2.7 1.4 fusion.23
  14.1 4.8 %collective-permute-start = (bf16[8,128,128]{2,1,0:T(8,128)(2,1)}, bf16[8,128,128]{2,1,0:T(8,128)(2,1)S(1)}, u32[]{:S(2)}, u32[]{:S(2)}) collective-permute-start(bf16[8,128,128]{2,1,0:T(8,128)(2,1)} %pad_maximum_fusion), channel_id=1, source_target_pairs={{0,8},{8,16},{16,24},{24,32},{32,40},{40,48},{48,56},{56,64},{64,7... | collective-permute-start | bytes 786440 | tf_op jit(solution)/shard_map/ppermute | solution.py:148
  18.9 15.9 %collective-permute-start.8 = (bf16[8,128,128]{2,1,0:T(8,128)(2,1)}, bf16[8,128,128]{2,1,0:T(8,128)(2,1)}, u32[]{:S(2)}, u32[]{:S(2)}) collective-permute-start(bf16[8,128,128]{2,1,0:T(8,128)(2,1)} %pad_maximum_fusion), channel_id=1, source_target_pairs={{0,120},{8,0},{16,8},{24,16},{32,24},{40,32},{48,40},{56,48},{64,5... | collective-permute-start | bytes 786440 | tf_op jit(solution)/shard_map/ppermute | solution.py:159
  35.3 1.4 convolution_multiply_fusion.1
  36.8 2.3 collective-permute-done
  39.1 1.9 collective-permute-start.1
  43.0 4.6 %collective-permute-start.9 = (bf16[8,128,128]{2,1,0:T(8,128)(2,1)}, bf16[8,128,128]{2,1,0:T(8,128)(2,1)S(1)}, u32[]{:S(2)}, u32[]{:S(2)}) collective-permute-start(bf16[8,128,128]{2,1,0:T(8,128)(2,1)} %collective-permute-done.8), channel_id=1, source_target_pairs={{0,120},{8,0},{16,8},{24,16},{32,24},{40,32},{48,40},{56,48},{64,5... | collective-permute-start | bytes 786440 | tf_op jit(solution)/shard_map/ppermute | solution.py:159
  47.6 1.4 fusion.18
  50.0 1.9 collective-permute-start.2
  52.4 4.8 %collective-permute-start.10 = (bf16[8,128,128]{2,1,0:T(8,128)(2,1)S(1)}, bf16[8,128,128]{2,1,0:T(8,128)(2,1)S(1)}, u32[]{:S(2)}, u32[]{:S(2)}) collective-permute-start(bf16[8,128,128]{2,1,0:T(8,128)(2,1)S(1)} %collective-permute-done.9), channel_id=1, source_target_pairs={{0,120},{8,0},{16,8},{24,16},{32,24},{40,32},{48,40},{56,48},{64,5... | collective-permute-start | bytes 786440 | tf_op jit(solution)/shard_map/ppermute | solution.py:159
  57.4 1.7 collective-permute-done.2
  59.2 1.9 collective-permute-start.3
  61.7 4.6 %collective-permute-start.11 = (bf16[8,128,128]{2,1,0:T(8,128)(2,1)S(1)}, bf16[8,128,128]{2,1,0:T(8,128)(2,1)S(1)}, u32[]{:S(2)}, u32[]{:S(2)}) collective-permute-start(bf16[8,128,128]{2,1,0:T(8,128)(2,1)S(1)} %collective-permute-done.10), channel_id=1, source_target_pairs={{0,120},{8,0},{16,8},{24,16},{32,24},{40,32},{48,40},{56,48},{64,5... | collective-permute-start | bytes 786440 | tf_op jit(solution)/shard_map/ppermute | solution.py:159
  67.5 1.9 collective-permute-start.4
  70.1 4.8 %collective-permute-start.12 = (bf16[8,128,128]{2,1,0:T(8,128)(2,1)S(1)}, bf16[8,128,128]{2,1,0:T(8,128)(2,1)S(1)}, u32[]{:S(2)}, u32[]{:S(2)}) collective-permute-start(bf16[8,128,128]{2,1,0:T(8,128)(2,1)S(1)} %collective-permute-done.11), channel_id=1, source_target_pairs={{0,120},{8,0},{16,8},{24,16},{32,24},{40,32},{48,40},{56,48},{64,5... | collective-permute-start | bytes 786440 | tf_op jit(solution)/shard_map/ppermute | solution.py:159
  75.9 1.9 collective-permute-start.5
  78.4 4.6 %collective-permute-start.13 = (bf16[8,128,128]{2,1,0:T(8,128)(2,1)S(1)}, bf16[8,128,128]{2,1,0:T(8,128)(2,1)S(1)}, u32[]{:S(2)}, u32[]{:S(2)}) collective-permute-start(bf16[8,128,128]{2,1,0:T(8,128)(2,1)S(1)} %collective-permute-done.12), channel_id=1, source_target_pairs={{0,120},{8,0},{16,8},{24,16},{32,24},{40,32},{48,40},{56,48},{64,5... | collective-permute-start | bytes 786440 | tf_op jit(solution)/shard_map/ppermute | solution.py:159
  84.3 1.9 collective-permute-start.6
  86.8 4.6 %collective-permute-start.14 = (bf16[8,128,128]{2,1,0:T(8,128)(2,1)S(1)}, bf16[8,128,128]{2,1,0:T(8,128)(2,1)S(1)}, u32[]{:S(2)}, u32[]{:S(2)}) collective-permute-start(bf16[8,128,128]{2,1,0:T(8,128)(2,1)S(1)} %collective-permute-done.13), channel_id=1, source_target_pairs={{0,120},{8,0},{16,8},{24,16},{32,24},{40,32},{48,40},{56,48},{64,5... | collective-permute-start | bytes 786440 | tf_op jit(solution)/shard_map/ppermute | solution.py:159
  92.7 1.9 collective-permute-start.7
  95.6 6.7 %collective-permute-done.7 = bf16[8,128,128]{2,1,0:T(8,128)(2,1)S(1)} collective-permute-done((bf16[8,128,128]{2,1,0:T(8,128)(2,1)S(1)}, bf16[8,128,128]{2,1,0:T(8,128)(2,1)S(1)}, u32[]{:S(2)}, u32[]{:S(2)}) %collective-permute-start.7) | collective-permute-done | bytes 262176 | tf_op jit(solution)/shard_map/ppermute | solution.py:148
  106.1 12.8 %all-to-all-start = ((bf16[8,128,256]{2,1,0:T(8,128)(2,1)}), bf16[8,128,256]{2,1,0:T(8,128)(2,1)S(1)}, u32[]{:S(2)}, u32[]{:S(2)}) async-start(bf16[8,128,256]{2,1,0:T(8,128)(2,1)} %bitcast.165), calls=%async_computation | async-start | bytes 1048576 | tf_op jit(solution)/shard_map/all_to_all | solution.py:180
  118.9 9.5 %all-to-all-done = bf16[8,128,256]{2,1,0:T(8,128)(2,1)S(1)} async-done(((bf16[8,128,256]{2,1,0:T(8,128)(2,1)}), bf16[8,128,256]{2,1,0:T(8,128)(2,1)S(1)}, u32[]{:S(2)}, u32[]{:S(2)}) %all-to-all-start) | async-done | bytes 524320 | tf_op jit(solution)/shard_map/all_to_all | solution.py:180
  130.2 4.3 %all-to-all-start.1 = ((bf16[8,128,256]{2,1,0:T(8,128)(2,1)}), bf16[8,128,256]{2,1,0:T(8,128)(2,1)S(1)}, u32[]{:S(2)}, u32[]{:S(2)}) async-start(bf16[8,128,256]{2,1,0:T(8,128)(2,1)} %broadcast_in_dim.37), calls=%async_computation.1 | async-start | bytes 1048576 | tf_op jit(solution)/shard_map/all_to_all | solution.py:187
  134.9 9.1 %all-to-all-done.1 = bf16[8,128,256]{2,1,0:T(8,128)(2,1)S(1)} async-done(((bf16[8,128,256]{2,1,0:T(8,128)(2,1)}), bf16[8,128,256]{2,1,0:T(8,128)(2,1)S(1)}, u32[]{:S(2)}, u32[]{:S(2)}) %all-to-all-start.1) | async-done | bytes 524320 | tf_op jit(solution)/shard_map/all_to_all | solution.py:187
  145.5 72.9 %all_to_all.25 = bf16[16,20,2048]{2,1,0:T(8,128)(2,1)S(1)} all-to-all(bf16[16,20,2048]{2,1,0:T(8,128)(2,1)S(1)} %convolution_convert_fusion.1), channel_id=1, replica_groups=mesh['dp'=8,'seq'=16,'head'=8] {'seq'}, dimensions={0} | all-to-all | bytes 2621440 | tf_op jit(solution)/shard_map/all_to_all | solution.py:218
  218.4 1.1 copy-done.2
  220.5 5.2 %convolution_convert_fusion = bf16[16,20,2048]{2,1,0:T(8,128)(2,1)} fusion(bf16[1,512,2048]{2,1,0:T(8,128)(2,1)S(1)} %copy-done, bf16[16,20,2048]{2,1,0:T(8,128)(2,1)} %copy-done.2, bf16[1,2048,512]{2,1,0:T(8,128)(2,1)} %param.30, f32[16,20,512]{2,1,0:T(8,128)S(1)} %fusion.4), kind=kOutput, calls=%fused_computation | convolution fusion | flops 1343815680 | bytes 7471104 | tf_op jit(solution)/shard_map/psh,hd->psd/dot_general | solution.py:222
  225.7 12.3 %all-to-all-start.3 = ((bf16[16,20,2048]{2,1,0:T(8,128)(2,1)}), bf16[16,20,2048]{2,1,0:T(8,128)(2,1)}, u32[]{:S(2)}, u32[]{:S(2)}) async-start(bf16[16,20,2048]{2,1,0:T(8,128)(2,1)} %convolution_convert_fusion), calls=%async_computation.3 | async-start | bytes 3145728 | tf_op jit(solution)/shard_map/all_to_all | solution.py:225
  238.2 68.9 %all-to-all-done.3 = bf16[16,20,2048]{2,1,0:T(8,128)(2,1)} async-done(((bf16[16,20,2048]{2,1,0:T(8,128)(2,1)}), bf16[16,20,2048]{2,1,0:T(8,128)(2,1)}, u32[]{:S(2)}, u32[]{:S(2)}) %all-to-all-start.3) | async-done | bytes 1310752 | tf_op jit(solution)/shard_map/all_to_all | solution.py:225
  307.0 1.9 fusion
  309.0 18.0 %all_to_all.26 = bf16[8,128,256]{2,1,0:T(8,128)(2,1)S(1)} all-to-all(bf16[8,128,256]{2,1,0:T(8,128)(2,1)S(1)} %bitcast.171), channel_id=1, replica_groups=mesh['dp'=8,'seq'=16,'head'=8] {'head'}, dimensions={0} | all-to-all | bytes 1048576 | tf_op jit(solution)/shard_map/all_to_all | solution.py:237
  (154 shorter events, 34.1 us)
Async XLA Ops:
  0.0 220.5 %copy-start = (bf16[1,512,2048]{2,1,0:T(8,128)(2,1)S(1)}, bf16[1,512,2048]{2,1,0:T(8,128)(2,1)}, u32[]{:S(2)}) copy-start(bf16[1,512,2048]{2,1,0:T(8,128)(2,1)} %param.31) | copy-start | bytes 6291460
  2.6 6.6 %copy-start.6 = (f32[128,4]{0,1:T(4,128)}, f32[128,4]{0,1:T(4,128)S(1)}, u32[]{:S(2)}) copy-start(f32[128,4]{0,1:T(4,128)S(1)} %copy.207) | copy-start | bytes 6148
  7.5 1.8 copy-start.10
  7.5 2.4 copy-start.5
  10.5 24.3 %copy-start.7 = (bf16[128,256]{1,0:T(8,128)(2,1)S(1)}, bf16[128,256]{1,0:T(8,128)(2,1)}, u32[]{:S(2)}) copy-start(bf16[128,256]{1,0:T(8,128)(2,1)} %param.17) | copy-start | bytes 196612
  13.3 28.8 %copy-start.4 = (bf16[128,512]{1,0:T(8,128)(2,1)S(1)}, bf16[128,512]{1,0:T(8,128)(2,1)}, u32[]{:S(2)}) copy-start(bf16[128,512]{1,0:T(8,128)(2,1)} %param.20) | copy-start | bytes 393220
  14.1 25.0 %collective-permute-start = (bf16[8,128,128]{2,1,0:T(8,128)(2,1)}, bf16[8,128,128]{2,1,0:T(8,128)(2,1)S(1)}, u32[]{:S(2)}, u32[]{:S(2)}) collective-permute-start(bf16[8,128,128]{2,1,0:T(8,128)(2,1)} %pad_maximum_fusion), channel_id=1, source_target_pairs={{0,8},{8,16},{16,24},{24,32},{32,40},{40,48},{48,56},{56,64},{64,7... | collective-permute-start | bytes 786440 | tf_op jit(solution)/shard_map/ppermute | solution.py:148
  18.9 24.1 %collective-permute-start.8 = (bf16[8,128,128]{2,1,0:T(8,128)(2,1)}, bf16[8,128,128]{2,1,0:T(8,128)(2,1)}, u32[]{:S(2)}, u32[]{:S(2)}) collective-permute-start(bf16[8,128,128]{2,1,0:T(8,128)(2,1)} %pad_maximum_fusion), channel_id=1, source_target_pairs={{0,120},{8,0},{16,8},{24,16},{32,24},{40,32},{48,40},{56,48},{64,5... | collective-permute-start | bytes 786440 | tf_op jit(solution)/shard_map/ppermute | solution.py:159
  39.1 9.9 %collective-permute-start.1 = (bf16[8,128,128]{2,1,0:T(8,128)(2,1)S(1)}, bf16[8,128,128]{2,1,0:T(8,128)(2,1)}, u32[]{:S(2)}, u32[]{:S(2)}) collective-permute-start(bf16[8,128,128]{2,1,0:T(8,128)(2,1)S(1)} %collective-permute-done), channel_id=1, source_target_pairs={{0,8},{8,16},{16,24},{24,32},{32,40},{40,48},{48,56},{56,64},{64,7... | collective-permute-start | bytes 786440 | tf_op jit(solution)/shard_map/ppermute | solution.py:148
  43.0 9.4 %collective-permute-start.9 = (bf16[8,128,128]{2,1,0:T(8,128)(2,1)}, bf16[8,128,128]{2,1,0:T(8,128)(2,1)S(1)}, u32[]{:S(2)}, u32[]{:S(2)}) collective-permute-start(bf16[8,128,128]{2,1,0:T(8,128)(2,1)} %collective-permute-done.8), channel_id=1, source_target_pairs={{0,120},{8,0},{16,8},{24,16},{32,24},{40,32},{48,40},{56,48},{64,5... | collective-permute-start | bytes 786440 | tf_op jit(solution)/shard_map/ppermute | solution.py:159
  50.0 9.1 %collective-permute-start.2 = (bf16[8,128,128]{2,1,0:T(8,128)(2,1)}, bf16[8,128,128]{2,1,0:T(8,128)(2,1)S(1)}, u32[]{:S(2)}, u32[]{:S(2)}) collective-permute-start(bf16[8,128,128]{2,1,0:T(8,128)(2,1)} %collective-permute-done.1), channel_id=1, source_target_pairs={{0,8},{8,16},{16,24},{24,32},{32,40},{40,48},{48,56},{56,64},{64,7... | collective-permute-start | bytes 786440 | tf_op jit(solution)/shard_map/ppermute | solution.py:148
  52.4 9.3 %collective-permute-start.10 = (bf16[8,128,128]{2,1,0:T(8,128)(2,1)S(1)}, bf16[8,128,128]{2,1,0:T(8,128)(2,1)S(1)}, u32[]{:S(2)}, u32[]{:S(2)}) collective-permute-start(bf16[8,128,128]{2,1,0:T(8,128)(2,1)S(1)} %collective-permute-done.9), channel_id=1, source_target_pairs={{0,120},{8,0},{16,8},{24,16},{32,24},{40,32},{48,40},{56,48},{64,5... | collective-permute-start | bytes 786440 | tf_op jit(solution)/shard_map/ppermute | solution.py:159
  59.2 8.3 %collective-permute-start.3 = (bf16[8,128,128]{2,1,0:T(8,128)(2,1)S(1)}, bf16[8,128,128]{2,1,0:T(8,128)(2,1)S(1)}, u32[]{:S(2)}, u32[]{:S(2)}) collective-permute-start(bf16[8,128,128]{2,1,0:T(8,128)(2,1)S(1)} %collective-permute-done.2), channel_id=1, source_target_pairs={{0,8},{8,16},{16,24},{24,32},{32,40},{40,48},{48,56},{56,64},{64,7... | collective-permute-start | bytes 786440 | tf_op jit(solution)/shard_map/ppermute | solution.py:148
  61.7 8.4 %collective-permute-start.11 = (bf16[8,128,128]{2,1,0:T(8,128)(2,1)S(1)}, bf16[8,128,128]{2,1,0:T(8,128)(2,1)S(1)}, u32[]{:S(2)}, u32[]{:S(2)}) collective-permute-start(bf16[8,128,128]{2,1,0:T(8,128)(2,1)S(1)} %collective-permute-done.10), channel_id=1, source_target_pairs={{0,120},{8,0},{16,8},{24,16},{32,24},{40,32},{48,40},{56,48},{64,5... | collective-permute-start | bytes 786440 | tf_op jit(solution)/shard_map/ppermute | solution.py:159
  67.5 8.3 %collective-permute-start.4 = (bf16[8,128,128]{2,1,0:T(8,128)(2,1)S(1)}, bf16[8,128,128]{2,1,0:T(8,128)(2,1)S(1)}, u32[]{:S(2)}, u32[]{:S(2)}) collective-permute-start(bf16[8,128,128]{2,1,0:T(8,128)(2,1)S(1)} %collective-permute-done.3), channel_id=1, source_target_pairs={{0,8},{8,16},{16,24},{24,32},{32,40},{40,48},{48,56},{56,64},{64,7... | collective-permute-start | bytes 786440 | tf_op jit(solution)/shard_map/ppermute | solution.py:148
  70.1 8.3 %collective-permute-start.12 = (bf16[8,128,128]{2,1,0:T(8,128)(2,1)S(1)}, bf16[8,128,128]{2,1,0:T(8,128)(2,1)S(1)}, u32[]{:S(2)}, u32[]{:S(2)}) collective-permute-start(bf16[8,128,128]{2,1,0:T(8,128)(2,1)S(1)} %collective-permute-done.11), channel_id=1, source_target_pairs={{0,120},{8,0},{16,8},{24,16},{32,24},{40,32},{48,40},{56,48},{64,5... | collective-permute-start | bytes 786440 | tf_op jit(solution)/shard_map/ppermute | solution.py:159
  75.9 8.3 %collective-permute-start.5 = (bf16[8,128,128]{2,1,0:T(8,128)(2,1)S(1)}, bf16[8,128,128]{2,1,0:T(8,128)(2,1)S(1)}, u32[]{:S(2)}, u32[]{:S(2)}) collective-permute-start(bf16[8,128,128]{2,1,0:T(8,128)(2,1)S(1)} %collective-permute-done.4), channel_id=1, source_target_pairs={{0,8},{8,16},{16,24},{24,32},{32,40},{40,48},{48,56},{56,64},{64,7... | collective-permute-start | bytes 786440 | tf_op jit(solution)/shard_map/ppermute | solution.py:148
  78.4 8.4 %collective-permute-start.13 = (bf16[8,128,128]{2,1,0:T(8,128)(2,1)S(1)}, bf16[8,128,128]{2,1,0:T(8,128)(2,1)S(1)}, u32[]{:S(2)}, u32[]{:S(2)}) collective-permute-start(bf16[8,128,128]{2,1,0:T(8,128)(2,1)S(1)} %collective-permute-done.12), channel_id=1, source_target_pairs={{0,120},{8,0},{16,8},{24,16},{32,24},{40,32},{48,40},{56,48},{64,5... | collective-permute-start | bytes 786440 | tf_op jit(solution)/shard_map/ppermute | solution.py:159
  84.3 8.4 %collective-permute-start.6 = (bf16[8,128,128]{2,1,0:T(8,128)(2,1)S(1)}, bf16[8,128,128]{2,1,0:T(8,128)(2,1)S(1)}, u32[]{:S(2)}, u32[]{:S(2)}) collective-permute-start(bf16[8,128,128]{2,1,0:T(8,128)(2,1)S(1)} %collective-permute-done.5), channel_id=1, source_target_pairs={{0,8},{8,16},{16,24},{24,32},{32,40},{40,48},{48,56},{56,64},{64,7... | collective-permute-start | bytes 786440 | tf_op jit(solution)/shard_map/ppermute | solution.py:148
  86.8 8.5 %collective-permute-start.14 = (bf16[8,128,128]{2,1,0:T(8,128)(2,1)S(1)}, bf16[8,128,128]{2,1,0:T(8,128)(2,1)S(1)}, u32[]{:S(2)}, u32[]{:S(2)}) collective-permute-start(bf16[8,128,128]{2,1,0:T(8,128)(2,1)S(1)} %collective-permute-done.13), channel_id=1, source_target_pairs={{0,120},{8,0},{16,8},{24,16},{32,24},{40,32},{48,40},{56,48},{64,5... | collective-permute-start | bytes 786440 | tf_op jit(solution)/shard_map/ppermute | solution.py:159
  92.7 9.5 %collective-permute-start.7 = (bf16[8,128,128]{2,1,0:T(8,128)(2,1)S(1)}, bf16[8,128,128]{2,1,0:T(8,128)(2,1)S(1)}, u32[]{:S(2)}, u32[]{:S(2)}) collective-permute-start(bf16[8,128,128]{2,1,0:T(8,128)(2,1)S(1)} %collective-permute-done.6), channel_id=1, source_target_pairs={{0,8},{8,16},{16,24},{24,32},{32,40},{40,48},{48,56},{56,64},{64,7... | collective-permute-start | bytes 786440 | tf_op jit(solution)/shard_map/ppermute | solution.py:148
  102.9 1.7 copy-start.3
  102.9 1.7 copy-start.13
  102.9 1.9 copy-start.1
  105.3 29.2 %copy-start.8 = (s32[128,10]{0,1:T(8,128)S(1)}, s32[128,10]{0,1:T(8,128)}, u32[]{:S(2)}) copy-start(s32[128,10]{0,1:T(8,128)} %param.27) | copy-start | bytes 15364
  106.1 22.3 %all-to-all-start = ((bf16[8,128,256]{2,1,0:T(8,128)(2,1)}), bf16[8,128,256]{2,1,0:T(8,128)(2,1)S(1)}, u32[]{:S(2)}, u32[]{:S(2)}) async-start(bf16[8,128,256]{2,1,0:T(8,128)(2,1)} %bitcast.165), calls=%async_computation | async-start | bytes 1048576 | tf_op jit(solution)/shard_map/all_to_all | solution.py:180
  128.5 16.0 %copy-start.12 = (f32[2048]{0:T(1024)S(1)}, f32[2048]{0:T(1024)}, u32[]{:S(2)}) copy-start(f32[2048]{0:T(1024)} %param.26) | copy-start | bytes 24580
  130.2 13.8 %all-to-all-start.1 = ((bf16[8,128,256]{2,1,0:T(8,128)(2,1)}), bf16[8,128,256]{2,1,0:T(8,128)(2,1)S(1)}, u32[]{:S(2)}, u32[]{:S(2)}) async-start(bf16[8,128,256]{2,1,0:T(8,128)(2,1)} %broadcast_in_dim.37), calls=%async_computation.1 | async-start | bytes 1048576 | tf_op jit(solution)/shard_map/all_to_all | solution.py:187
  145.5 74.0 %copy-start.14 = (bf16[1,2048,512]{2,1,0:T(8,128)(2,1)S(1)}, bf16[1,2048,512]{2,1,0:T(8,128)(2,1)}, u32[]{:S(2)}) copy-start(bf16[1,2048,512]{2,1,0:T(8,128)(2,1)} %param.29) | copy-start | bytes 6291460
  218.4 1.1 copy-start.2
  225.7 12.3 %copy-start.9 = (f32[128,10]{0,1:T(8,128)S(1)}, f32[128,10]{0,1:T(8,128)}, u32[]{:S(2)}) copy-start(f32[128,10]{0,1:T(8,128)} %param.28) | copy-start | bytes 15364
  225.7 81.3 %all-to-all-start.3 = ((bf16[16,20,2048]{2,1,0:T(8,128)(2,1)}), bf16[16,20,2048]{2,1,0:T(8,128)(2,1)}, u32[]{:S(2)}, u32[]{:S(2)}) async-start(bf16[16,20,2048]{2,1,0:T(8,128)(2,1)} %convolution_convert_fusion), calls=%async_computation.3 | async-start | bytes 3145728 | tf_op jit(solution)/shard_map/all_to_all | solution.py:225
  (1 other events, 0.6 us)

commit v5 on v4

--- a/solution.py
+++ b/solution.py
@@ -201,7 +201,10 @@
     expert_count = peer_count * column_count
     pick_count = expert_ids.shape[1]
     slot_count = min(length, length * pick_count * 2 // expert_count)
-    targets = jnp.arange(peer_count, dtype=jnp.int32) * column_count + lax.axis_index("head")
+    offsets = jnp.arange(peer_count, dtype=jnp.int32)
+    targets = ((lax.axis_index("seq") + offsets) % peer_count) * column_count + lax.axis_index(
+        "head"
+    )
     hits = expert_ids[:, :, None] == targets[None, None, :]
     weights = (route_scores / jnp.sum(route_scores, axis=1, keepdims=True)).astype(jnp.bfloat16)
     weights = lax.optimization_barrier(weights).astype(jnp.float32)
@@ -215,19 +218,33 @@
     outgoing = jnp.einsum(
         "tps,td->psd", placement_map, normed, preferred_element_type=jnp.float32
     ).astype(jnp.bfloat16)
-    incoming = lax.all_to_all(outgoing, "seq", split_axis=0, concat_axis=0, tiled=True)
+    incoming = jnp.stack(
+        [outgoing[0]]
+        + [
+            lax.ppermute(
+                outgoing[shift],
+                "seq",
+                [(j, (j + shift) % peer_count) for j in range(peer_count)],
+            )
+            for shift in range(1, peer_count)
+        ]
+    )
     gate_e = jnp.einsum("psd,dh->psh", incoming, w_gate[0], preferred_element_type=jnp.float32)
     up_e = jnp.einsum("psd,dh->psh", incoming, w_up[0], preferred_element_type=jnp.float32)
     hidden = (jax.nn.silu(gate_e) * up_e).astype(jnp.bfloat16)
     result = jnp.einsum(
         "psh,hd->psd", hidden, w_down[0], preferred_element_type=jnp.float32
     ).astype(jnp.bfloat16)
-    returned = lax.all_to_all(
-        result,
-        "seq",
-        split_axis=0,
-        concat_axis=0,
-        tiled=True,
+    returned = jnp.stack(
+        [result[0]]
+        + [
+            lax.ppermute(
+                result[shift],
+                "seq",
+                [((j + shift) % peer_count, j) for j in range(peer_count)],
+            )
+            for shift in range(1, peer_count)
+        ]
     )
     combine_map = (placement_map.astype(jnp.float32) * share_weight[:, :, None]).astype(
         jnp.bfloat16

time: 329 us -> 389 us (1.18)
  starting transfers between devices: 91.3 us -> 235 us
  blocking collectives: 90.9 us -> 12.3 us
  waiting for transfers between devices: 102 us -> 95.3 us
    ppermute x0 -> x30, starting transfers between devices: none -> 155 us  [the longest x15 82.4 us: on_device(): lax.ppermute(result[shift], 'seq', [((j + shift) % peer_count, j) for j i...]
    all_to_all x1 -> x0, blocking collectives: 72.9 us -> none  [on_device(): lax.all_to_all(outgoing, 'seq', split_axis=0, concat_axis=0, tiled=True)]
    all_to_all x1 -> x0, waiting for transfers between devices: 68.9 us -> none  [on_device(): lax.all_to_all(result, 'seq', split_axis=0, concat_axis=0, tiled=True)]
    ppermute x0 -> x30, waiting for transfers between devices: none -> 62.6 us  [the longest x15 33.3 us: on_device(): lax.ppermute(outgoing[shift], 'seq', [(j, (j + shift) % peer_count) for j...]
    all_to_all x1 -> x0, starting transfers between devices: 12.3 us -> none  [on_device(): lax.all_to_all(result, 'seq', split_axis=0, concat_axis=0, tiled=True)]
    all_to_all x1, blocking collectives: 18 us -> 12.3 us  [on_device(): lax.all_to_all(moe_pieces.transpose(1, 0, 2), 'head', split_axis=0, conca...]
  transfers between devices with their start and end apart: 18 -> 47, of which waited for: 10 -> 20; matrix products, arithmetic and copies ran while one was open for 4% -> 3% of each run, Pallas kernels for 0% -> 0%
where the time goes in v5:
time: 389 us; the launch traced here: 388 us
  starting transfers between devices  235 us (60%)
  waiting for transfers between devices  95.3 us (24%)
  matrix products  26.4 us (7%)
  blocking collectives  12.3 us (3%)
  local copies, waits for them, and re-layouts  12 us (3%)
  other arithmetic  5.39 us (1%)
    ppermute x15, starting transfers between devices, on_device(): lax.ppermute(result[shift], 'seq', [((j + shift) % peer_count, j) for j i...  82.4 us
    ppermute x15, starting transfers between devices, on_device(): lax.ppermute(outgoing[shift], 'seq', [(j, (j + shift) % peer_count) for j...  73 us
    ppermute x7, starting transfers between devices, on_device(): going_down = lax.ppermute(going_down, 'seq', backward_pairs)  43.7 us
    ppermute x15, waiting for transfers between devices, on_device(): lax.ppermute(outgoing[shift], 'seq', [(j, (j + shift) % peer_count) for j...  33.3 us
    ppermute x15, waiting for transfers between devices, on_device(): lax.ppermute(result[shift], 'seq', [((j + shift) % peer_count, j) for j i...  29.3 us
    ppermute x8, starting transfers between devices, on_device(): going_up = lax.ppermute(going_up, 'seq', forward_pairs)  18.3 us
    ppermute x8, waiting for transfers between devices, on_device(): going_up = lax.ppermute(going_up, 'seq', forward_pairs)  14.1 us
    all_to_all x1, starting transfers between devices, on_device(): lax.all_to_all(attn_pieces.transpose(1, 0, 2), 'head', split_axis=0, conc...  13 us
  transfers between devices with their start and end apart: 47, of which 20 were waited for; matrix products, arithmetic and copies ran while one was open for 3% of the time, Pallas kernels for 0%

profile of v5, /device:TPU:1, one launch (start us, length us, event | category | flops | bytes accessed | tf_op | source)
XLA Modules:
  0.0 387.5 jit_solution(16945757635989364918)
XLA Ops:
  12.9 4.8 %collective-permute-start = (bf16[8,128,128]{2,1,0:T(8,128)(2,1)}, bf16[8,128,128]{2,1,0:T(8,128)(2,1)S(1)}, u32[]{:S(2)}, u32[]{:S(2)}) collective-permute-start(bf16[8,128,128]{2,1,0:T(8,128)(2,1)} %pad_maximum_fusion), channel_id=1, source_target_pairs={{0,8},{8,16},{16,24},{24,32},{32,40},{40,48},{48,56},{56,64},{64,7... | collective-permute-start | bytes 786440 | tf_op jit(solution)/shard_map/ppermute | solution.py:148
  17.7 15.9 %collective-permute-start.8 = (bf16[8,128,128]{2,1,0:T(8,128)(2,1)}, bf16[8,128,128]{2,1,0:T(8,128)(2,1)}, u32[]{:S(2)}, u32[]{:S(2)}) collective-permute-start(bf16[8,128,128]{2,1,0:T(8,128)(2,1)} %pad_maximum_fusion), channel_id=1, source_target_pairs={{0,120},{8,0},{16,8},{24,16},{32,24},{40,32},{48,40},{56,48},{64,5... | collective-permute-start | bytes 786440 | tf_op jit(solution)/shard_map/ppermute | solution.py:159
  51.2 4.8 %collective-permute-start.10 = (bf16[8,128,128]{2,1,0:T(8,128)(2,1)S(1)}, bf16[8,128,128]{2,1,0:T(8,128)(2,1)S(1)}, u32[]{:S(2)}, u32[]{:S(2)}) collective-permute-start(bf16[8,128,128]{2,1,0:T(8,128)(2,1)S(1)} %collective-permute-done.9), channel_id=1, source_target_pairs={{0,120},{8,0},{16,8},{24,16},{32,24},{40,32},{48,40},{56,48},{64,5... | collective-permute-start | bytes 786440 | tf_op jit(solution)/shard_map/ppermute | solution.py:159
  68.8 4.8 %collective-permute-start.12 = (bf16[8,128,128]{2,1,0:T(8,128)(2,1)S(1)}, bf16[8,128,128]{2,1,0:T(8,128)(2,1)S(1)}, u32[]{:S(2)}, u32[]{:S(2)}) collective-permute-start(bf16[8,128,128]{2,1,0:T(8,128)(2,1)S(1)} %collective-permute-done.11), channel_id=1, source_target_pairs={{0,120},{8,0},{16,8},{24,16},{32,24},{40,32},{48,40},{56,48},{64,5... | collective-permute-start | bytes 786440 | tf_op jit(solution)/shard_map/ppermute | solution.py:159
  94.4 6.7 %collective-permute-done.7 = bf16[8,128,128]{2,1,0:T(8,128)(2,1)S(1)} collective-permute-done((bf16[8,128,128]{2,1,0:T(8,128)(2,1)S(1)}, bf16[8,128,128]{2,1,0:T(8,128)(2,1)S(1)}, u32[]{:S(2)}, u32[]{:S(2)}) %collective-permute-start.7) | collective-permute-done | bytes 262176 | tf_op jit(solution)/shard_map/ppermute | solution.py:148
  105.2 13.0 %all-to-all-start = ((bf16[8,128,256]{2,1,0:T(8,128)(2,1)}), bf16[8,128,256]{2,1,0:T(8,128)(2,1)S(1)}, u32[]{:S(2)}, u32[]{:S(2)}) async-start(bf16[8,128,256]{2,1,0:T(8,128)(2,1)} %bitcast.283), calls=%async_computation | async-start | bytes 1048576 | tf_op jit(solution)/shard_map/all_to_all | solution.py:180
  118.1 9.5 %all-to-all-done = bf16[8,128,256]{2,1,0:T(8,128)(2,1)S(1)} async-done(((bf16[8,128,256]{2,1,0:T(8,128)(2,1)}), bf16[8,128,256]{2,1,0:T(8,128)(2,1)S(1)}, u32[]{:S(2)}, u32[]{:S(2)}) %all-to-all-start) | async-done | bytes 524320 | tf_op jit(solution)/shard_map/all_to_all | solution.py:180
  134.3 9.0 %all-to-all-done.1 = bf16[8,128,256]{2,1,0:T(8,128)(2,1)S(1)} async-done(((bf16[8,128,256]{2,1,0:T(8,128)(2,1)}), bf16[8,128,256]{2,1,0:T(8,128)(2,1)S(1)}, u32[]{:S(2)}, u32[]{:S(2)}) %all-to-all-start.1) | async-done | bytes 524320 | tf_op jit(solution)/shard_map/all_to_all | solution.py:187
  150.9 6.1 %collective-permute-start.18 = (bf16[20,2048]{1,0:T(8,128)(2,1)S(1)}, bf16[20,2048]{1,0:T(8,128)(2,1)S(1)}, u32[]{:S(2)}, u32[]{:S(2)}) collective-permute-start(bf16[20,2048]{1,0:T(8,128)(2,1)S(1)} %get-tuple-element.32), channel_id=1, source_target_pairs={{0,32},{8,40},{16,48},{24,56},{32,64},{40,72},{48,80},{56,88},{64,... | collective-permute-start | bytes 245768 | tf_op jit(solution)/shard_map/ppermute | solution.py:224
  157.1 5.8 %collective-permute-start.19 = (bf16[20,2048]{1,0:T(8,128)(2,1)S(1)}, bf16[20,2048]{1,0:T(8,128)(2,1)S(1)}, u32[]{:S(2)}, u32[]{:S(2)}) collective-permute-start(bf16[20,2048]{1,0:T(8,128)(2,1)S(1)} %get-tuple-element.31), channel_id=1, source_target_pairs={{0,40},{8,48},{16,56},{24,64},{32,72},{40,80},{48,88},{56,96},{64,... | collective-permute-start | bytes 245768 | tf_op jit(solution)/shard_map/ppermute | solution.py:224
  162.9 4.8 %collective-permute-start.20 = (bf16[20,2048]{1,0:T(8,128)(2,1)S(1)}, bf16[20,2048]{1,0:T(8,128)(2,1)S(1)}, u32[]{:S(2)}, u32[]{:S(2)}) collective-permute-start(bf16[20,2048]{1,0:T(8,128)(2,1)S(1)} %get-tuple-element.30), channel_id=1, source_target_pairs={{0,48},{8,56},{16,64},{24,72},{32,80},{40,88},{48,96},{56,104},{64... | collective-permute-start | bytes 245768 | tf_op jit(solution)/shard_map/ppermute | solution.py:224
  167.7 9.5 %collective-permute-start.21 = (bf16[20,2048]{1,0:T(8,128)(2,1)S(1)}, bf16[20,2048]{1,0:T(8,128)(2,1)S(1)}, u32[]{:S(2)}, u32[]{:S(2)}) collective-permute-start(bf16[20,2048]{1,0:T(8,128)(2,1)S(1)} %get-tuple-element.29), channel_id=1, source_target_pairs={{0,56},{8,64},{16,72},{24,80},{32,88},{40,96},{48,104},{56,112},{6... | collective-permute-start | bytes 245768 | tf_op jit(solution)/shard_map/ppermute | solution.py:224
  181.8 8.3 %collective-permute-start.23 = (bf16[20,2048]{1,0:T(8,128)(2,1)S(1)}, bf16[20,2048]{1,0:T(8,128)(2,1)S(1)}, u32[]{:S(2)}, u32[]{:S(2)}) collective-permute-start(bf16[20,2048]{1,0:T(8,128)(2,1)S(1)} %get-tuple-element.27), channel_id=1, source_target_pairs={{0,72},{8,80},{16,88},{24,96},{32,104},{40,112},{48,120},{56,0},{6... | collective-permute-start | bytes 245768 | tf_op jit(solution)/shard_map/ppermute | solution.py:224
  193.7 9.1 %collective-permute-done.20 = bf16[20,2048]{1,0:T(8,128)(2,1)S(1)} collective-permute-done((bf16[20,2048]{1,0:T(8,128)(2,1)S(1)}, bf16[20,2048]{1,0:T(8,128)(2,1)S(1)}, u32[]{:S(2)}, u32[]{:S(2)}) %collective-permute-start.20) | collective-permute-done | bytes 81952 | tf_op jit(solution)/shard_map/ppermute | solution.py:224
  210.2 6.2 %collective-permute-start.27 = (bf16[20,2048]{1,0:T(8,128)(2,1)S(1)}, bf16[20,2048]{1,0:T(8,128)(2,1)S(1)}, u32[]{:S(2)}, u32[]{:S(2)}) collective-permute-start(bf16[20,2048]{1,0:T(8,128)(2,1)S(1)} %get-tuple-element.23), channel_id=1, source_target_pairs={{0,104},{8,112},{16,120},{24,0},{32,8},{40,16},{48,24},{56,32},{64... | collective-permute-start | bytes 245768 | tf_op jit(solution)/shard_map/ppermute | solution.py:224
  216.4 12.6 %collective-permute-start.28 = (bf16[20,2048]{1,0:T(8,128)(2,1)S(1)}, bf16[20,2048]{1,0:T(8,128)(2,1)S(1)}, u32[]{:S(2)}, u32[]{:S(2)}) collective-permute-start(bf16[20,2048]{1,0:T(8,128)(2,1)S(1)} %get-tuple-element.22), channel_id=1, source_target_pairs={{0,112},{8,120},{16,0},{24,8},{32,16},{40,24},{48,32},{56,40},{64,... | collective-permute-start | bytes 245768 | tf_op jit(solution)/shard_map/ppermute | solution.py:224
  231.0 10.9 %collective-permute-done.26 = bf16[20,2048]{1,0:T(8,128)(2,1)S(1)} collective-permute-done((bf16[20,2048]{1,0:T(8,128)(2,1)S(1)}, bf16[20,2048]{1,0:T(8,128)(2,1)S(1)}, u32[]{:S(2)}, u32[]{:S(2)}) %collective-permute-start.26) | collective-permute-done | bytes 81952 | tf_op jit(solution)/shard_map/ppermute | solution.py:224
  244.9 6.8 %collective-permute-done.28 = bf16[20,2048]{1,0:T(8,128)(2,1)S(1)} collective-permute-done((bf16[20,2048]{1,0:T(8,128)(2,1)S(1)}, bf16[20,2048]{1,0:T(8,128)(2,1)S(1)}, u32[]{:S(2)}, u32[]{:S(2)}) %collective-permute-start.28) | collective-permute-done | bytes 81952 | tf_op jit(solution)/shard_map/ppermute | solution.py:224
  254.8 5.4 %convolution_convert_fusion = bf16[16,20,2048]{2,1,0:T(8,128)(2,1)} fusion(bf16[1,512,2048]{2,1,0:T(8,128)(2,1)S(1)} %copy-done, f32[16,20,512]{2,1,0:T(8,128)} %fusion.2, bf16[16,20,2048]{2,1,0:T(8,128)(2,1)} %copy-done.14, bf16[1,2048,512]{2,1,0:T(8,128)(2,1)} %param.29), kind=kOutput, calls=%fused_computation | convolution fusion | flops 1343815680 | bytes 7471104 | tf_op jit(solution)/shard_map/psh,hd->psd/dot_general | solution.py:235
  269.2 4.8 %collective-permute-start.32 = (bf16[20,2048]{1,0:T(8,128)(2,1)S(1)}, bf16[20,2048]{1,0:T(8,128)(2,1)S(1)}, u32[]{:S(2)}, u32[]{:S(2)}) collective-permute-start(bf16[20,2048]{1,0:T(8,128)(2,1)S(1)} %get-tuple-element.17), channel_id=1, source_target_pairs={{24,0},{32,8},{40,16},{48,24},{56,32},{64,40},{72,48},{80,56},{88,... | collective-permute-start | bytes 245768 | tf_op jit(solution)/shard_map/ppermute | solution.py:241
  274.0 5.2 %collective-permute-start.33 = (bf16[20,2048]{1,0:T(8,128)(2,1)S(1)}, bf16[20,2048]{1,0:T(8,128)(2,1)S(1)}, u32[]{:S(2)}, u32[]{:S(2)}) collective-permute-start(bf16[20,2048]{1,0:T(8,128)(2,1)S(1)} %get-tuple-element.16), channel_id=1, source_target_pairs={{32,0},{40,8},{48,16},{56,24},{64,32},{72,40},{80,48},{88,56},{96,... | collective-permute-start | bytes 245768 | tf_op jit(solution)/shard_map/ppermute | solution.py:241
  283.8 6.7 %collective-permute-start.35 = (bf16[20,2048]{1,0:T(8,128)(2,1)S(1)}, bf16[20,2048]{1,0:T(8,128)(2,1)S(1)}, u32[]{:S(2)}, u32[]{:S(2)}) collective-permute-start(bf16[20,2048]{1,0:T(8,128)(2,1)S(1)} %get-tuple-element.14), channel_id=1, source_target_pairs={{48,0},{56,8},{64,16},{72,24},{80,32},{88,40},{96,48},{104,56},{11... | collective-permute-start | bytes 245768 | tf_op jit(solution)/shard_map/ppermute | solution.py:241
  290.5 4.9 %collective-permute-start.36 = (bf16[20,2048]{1,0:T(8,128)(2,1)S(1)}, bf16[20,2048]{1,0:T(8,128)(2,1)S(1)}, u32[]{:S(2)}, u32[]{:S(2)}) collective-permute-start(bf16[20,2048]{1,0:T(8,128)(2,1)S(1)} %get-tuple-element.13), channel_id=1, source_target_pairs={{56,0},{64,8},{72,16},{80,24},{88,32},{96,40},{104,48},{112,56},{1... | collective-permute-start | bytes 245768 | tf_op jit(solution)/shard_map/ppermute | solution.py:241
  295.5 7.0 %collective-permute-start.37 = (bf16[20,2048]{1,0:T(8,128)(2,1)S(1)}, bf16[20,2048]{1,0:T(8,128)(2,1)S(1)}, u32[]{:S(2)}, u32[]{:S(2)}) collective-permute-start(bf16[20,2048]{1,0:T(8,128)(2,1)S(1)} %get-tuple-element.12), channel_id=1, source_target_pairs={{64,0},{72,8},{80,16},{88,24},{96,32},{104,40},{112,48},{120,56},{... | collective-permute-start | bytes 245768 | tf_op jit(solution)/shard_map/ppermute | solution.py:241
  302.6 6.4 %collective-permute-start.38 = (bf16[20,2048]{1,0:T(8,128)(2,1)S(1)}, bf16[20,2048]{1,0:T(8,128)(2,1)S(1)}, u32[]{:S(2)}, u32[]{:S(2)}) collective-permute-start(bf16[20,2048]{1,0:T(8,128)(2,1)S(1)} %get-tuple-element.11), channel_id=1, source_target_pairs={{72,0},{80,8},{88,16},{96,24},{104,32},{112,40},{120,48},{0,56},{8... | collective-permute-start | bytes 245768 | tf_op jit(solution)/shard_map/ppermute | solution.py:241
  309.0 6.6 %collective-permute-start.39 = (bf16[20,2048]{1,0:T(8,128)(2,1)S(1)}, bf16[20,2048]{1,0:T(8,128)(2,1)S(1)}, u32[]{:S(2)}, u32[]{:S(2)}) collective-permute-start(bf16[20,2048]{1,0:T(8,128)(2,1)S(1)} %get-tuple-element.10), channel_id=1, source_target_pairs={{80,0},{88,8},{96,16},{104,24},{112,32},{120,40},{0,48},{8,56},{16... | collective-permute-start | bytes 245768 | tf_op jit(solution)/shard_map/ppermute | solution.py:241
  318.4 5.9 %collective-permute-done.36 = bf16[20,2048]{1,0:T(8,128)(2,1)S(1)} collective-permute-done((bf16[20,2048]{1,0:T(8,128)(2,1)S(1)}, bf16[20,2048]{1,0:T(8,128)(2,1)S(1)}, u32[]{:S(2)}, u32[]{:S(2)}) %collective-permute-start.36) | collective-permute-done | bytes 81952 | tf_op jit(solution)/shard_map/ppermute | solution.py:241
  324.3 6.1 %collective-permute-start.41 = (bf16[20,2048]{1,0:T(8,128)(2,1)S(1)}, bf16[20,2048]{1,0:T(8,128)(2,1)S(1)}, u32[]{:S(2)}, u32[]{:S(2)}) collective-permute-start(bf16[20,2048]{1,0:T(8,128)(2,1)S(1)} %get-tuple-element.8), channel_id=1, source_target_pairs={{96,0},{104,8},{112,16},{120,24},{0,32},{8,40},{16,48},{24,56},{32... | collective-permute-start | bytes 245768 | tf_op jit(solution)/shard_map/ppermute | solution.py:241
  330.4 12.6 %collective-permute-start.42 = (bf16[20,2048]{1,0:T(8,128)(2,1)S(1)}, bf16[20,2048]{1,0:T(8,128)(2,1)S(1)}, u32[]{:S(2)}, u32[]{:S(2)}) collective-permute-start(bf16[20,2048]{1,0:T(8,128)(2,1)S(1)} %get-tuple-element.7), channel_id=1, source_target_pairs={{104,0},{112,8},{120,16},{0,24},{8,32},{16,40},{24,48},{32,56},{40... | collective-permute-start | bytes 245768 | tf_op jit(solution)/shard_map/ppermute | solution.py:241
  345.0 5.5 %collective-permute-start.44 = (bf16[20,2048]{1,0:T(8,128)(2,1)S(1)}, bf16[20,2048]{1,0:T(8,128)(2,1)S(1)}, u32[]{:S(2)}, u32[]{:S(2)}) collective-permute-start(bf16[20,2048]{1,0:T(8,128)(2,1)S(1)} %get-tuple-element.5), channel_id=1, source_target_pairs={{120,0},{0,8},{8,16},{16,24},{24,32},{32,40},{40,48},{48,56},{56,6... | collective-permute-start | bytes 245768 | tf_op jit(solution)/shard_map/ppermute | solution.py:241
  355.5 13.3 %collective-permute-done.42 = bf16[20,2048]{1,0:T(8,128)(2,1)S(1)} collective-permute-done((bf16[20,2048]{1,0:T(8,128)(2,1)S(1)}, bf16[20,2048]{1,0:T(8,128)(2,1)S(1)}, u32[]{:S(2)}, u32[]{:S(2)}) %collective-permute-start.42) | collective-permute-done | bytes 81952 | tf_op jit(solution)/shard_map/ppermute | solution.py:241
  374.5 12.3 %all_to_all.15 = bf16[8,128,256]{2,1,0:T(8,128)(2,1)S(1)} all-to-all(bf16[8,128,256]{2,1,0:T(8,128)(2,1)S(1)} %bitcast.289), channel_id=1, replica_groups=mesh['dp'=8,'seq'=16,'head'=8] {'head'}, dimensions={0} | all-to-all | bytes 1048576 | tf_op jit(solution)/shard_map/all_to_all | solution.py:254
  (247 shorter events, 134.8 us)
Async XLA Ops:
  12.9 25.0 %collective-permute-start = (bf16[8,128,128]{2,1,0:T(8,128)(2,1)}, bf16[8,128,128]{2,1,0:T(8,128)(2,1)S(1)}, u32[]{:S(2)}, u32[]{:S(2)}) collective-permute-start(bf16[8,128,128]{2,1,0:T(8,128)(2,1)} %pad_maximum_fusion), channel_id=1, source_target_pairs={{0,8},{8,16},{16,24},{24,32},{32,40},{40,48},{48,56},{56,64},{64,7... | collective-permute-start | bytes 786440 | tf_op jit(solution)/shard_map/ppermute | solution.py:148
  17.7 24.1 %collective-permute-start.8 = (bf16[8,128,128]{2,1,0:T(8,128)(2,1)}, bf16[8,128,128]{2,1,0:T(8,128)(2,1)}, u32[]{:S(2)}, u32[]{:S(2)}) collective-permute-start(bf16[8,128,128]{2,1,0:T(8,128)(2,1)} %pad_maximum_fusion), channel_id=1, source_target_pairs={{0,120},{8,0},{16,8},{24,16},{32,24},{40,32},{48,40},{56,48},{64,5... | collective-permute-start | bytes 786440 | tf_op jit(solution)/shard_map/ppermute | solution.py:159
  105.2 22.5 %all-to-all-start = ((bf16[8,128,256]{2,1,0:T(8,128)(2,1)}), bf16[8,128,256]{2,1,0:T(8,128)(2,1)S(1)}, u32[]{:S(2)}, u32[]{:S(2)}) async-start(bf16[8,128,256]{2,1,0:T(8,128)(2,1)} %bitcast.283), calls=%async_computation | async-start | bytes 1048576 | tf_op jit(solution)/shard_map/all_to_all | solution.py:180
  147.1 20.6 %collective-permute-start.16 = (bf16[20,2048]{1,0:T(8,128)(2,1)S(1)}, bf16[20,2048]{1,0:T(8,128)(2,1)S(1)}, u32[]{:S(2)}, u32[]{:S(2)}) collective-permute-start(bf16[20,2048]{1,0:T(8,128)(2,1)S(1)} %get-tuple-element.34), channel_id=1, source_target_pairs={{0,16},{8,24},{16,32},{24,40},{32,48},{40,56},{48,64},{56,72},{64,... | collective-permute-start | bytes 245768 | tf_op jit(solution)/shard_map/ppermute | solution.py:224
  149.0 28.2 %collective-permute-start.17 = (bf16[20,2048]{1,0:T(8,128)(2,1)S(1)}, bf16[20,2048]{1,0:T(8,128)(2,1)S(1)}, u32[]{:S(2)}, u32[]{:S(2)}) collective-permute-start(bf16[20,2048]{1,0:T(8,128)(2,1)S(1)} %get-tuple-element.33), channel_id=1, source_target_pairs={{0,24},{8,32},{16,40},{24,48},{32,56},{40,64},{48,72},{56,80},{64,... | collective-permute-start | bytes 245768 | tf_op jit(solution)/shard_map/ppermute | solution.py:224
  150.9 30.9 %collective-permute-start.18 = (bf16[20,2048]{1,0:T(8,128)(2,1)S(1)}, bf16[20,2048]{1,0:T(8,128)(2,1)S(1)}, u32[]{:S(2)}, u32[]{:S(2)}) collective-permute-start(bf16[20,2048]{1,0:T(8,128)(2,1)S(1)} %get-tuple-element.32), channel_id=1, source_target_pairs={{0,32},{8,40},{16,48},{24,56},{32,64},{40,72},{48,80},{56,88},{64,... | collective-permute-start | bytes 245768 | tf_op jit(solution)/shard_map/ppermute | solution.py:224
  157.1 33.1 %collective-permute-start.19 = (bf16[20,2048]{1,0:T(8,128)(2,1)S(1)}, bf16[20,2048]{1,0:T(8,128)(2,1)S(1)}, u32[]{:S(2)}, u32[]{:S(2)}) collective-permute-start(bf16[20,2048]{1,0:T(8,128)(2,1)S(1)} %get-tuple-element.31), channel_id=1, source_target_pairs={{0,40},{8,48},{16,56},{24,64},{32,72},{40,80},{48,88},{56,96},{64,... | collective-permute-start | bytes 245768 | tf_op jit(solution)/shard_map/ppermute | solution.py:224
  162.9 39.8 %collective-permute-start.20 = (bf16[20,2048]{1,0:T(8,128)(2,1)S(1)}, bf16[20,2048]{1,0:T(8,128)(2,1)S(1)}, u32[]{:S(2)}, u32[]{:S(2)}) collective-permute-start(bf16[20,2048]{1,0:T(8,128)(2,1)S(1)} %get-tuple-element.30), channel_id=1, source_target_pairs={{0,48},{8,56},{16,64},{24,72},{32,80},{40,88},{48,96},{56,104},{64... | collective-permute-start | bytes 245768 | tf_op jit(solution)/shard_map/ppermute | solution.py:224
  167.7 36.9 %collective-permute-start.21 = (bf16[20,2048]{1,0:T(8,128)(2,1)S(1)}, bf16[20,2048]{1,0:T(8,128)(2,1)S(1)}, u32[]{:S(2)}, u32[]{:S(2)}) collective-permute-start(bf16[20,2048]{1,0:T(8,128)(2,1)S(1)} %get-tuple-element.29), channel_id=1, source_target_pairs={{0,56},{8,64},{16,72},{24,80},{32,88},{40,96},{48,104},{56,112},{6... | collective-permute-start | bytes 245768 | tf_op jit(solution)/shard_map/ppermute | solution.py:224
  177.2 33.0 %collective-permute-start.22 = (bf16[20,2048]{1,0:T(8,128)(2,1)S(1)}, bf16[20,2048]{1,0:T(8,128)(2,1)S(1)}, u32[]{:S(2)}, u32[]{:S(2)}) collective-permute-start(bf16[20,2048]{1,0:T(8,128)(2,1)S(1)} %get-tuple-element.28), channel_id=1, source_target_pairs={{0,64},{8,72},{16,80},{24,88},{32,96},{40,104},{48,112},{56,120},{... | collective-permute-start | bytes 245768 | tf_op jit(solution)/shard_map/ppermute | solution.py:224
  181.8 34.6 %collective-permute-start.23 = (bf16[20,2048]{1,0:T(8,128)(2,1)S(1)}, bf16[20,2048]{1,0:T(8,128)(2,1)S(1)}, u32[]{:S(2)}, u32[]{:S(2)}) collective-permute-start(bf16[20,2048]{1,0:T(8,128)(2,1)S(1)} %get-tuple-element.27), channel_id=1, source_target_pairs={{0,72},{8,80},{16,88},{24,96},{32,104},{40,112},{48,120},{56,0},{6... | collective-permute-start | bytes 245768 | tf_op jit(solution)/shard_map/ppermute | solution.py:224
  190.1 38.9 %collective-permute-start.24 = (bf16[20,2048]{1,0:T(8,128)(2,1)S(1)}, bf16[20,2048]{1,0:T(8,128)(2,1)S(1)}, u32[]{:S(2)}, u32[]{:S(2)}) collective-permute-start(bf16[20,2048]{1,0:T(8,128)(2,1)S(1)} %get-tuple-element.26), channel_id=1, source_target_pairs={{0,80},{8,88},{16,96},{24,104},{32,112},{40,120},{48,0},{56,8},{64... | collective-permute-start | bytes 245768 | tf_op jit(solution)/shard_map/ppermute | solution.py:224
  202.7 28.2 %collective-permute-start.25 = (bf16[20,2048]{1,0:T(8,128)(2,1)S(1)}, bf16[20,2048]{1,0:T(8,128)(2,1)S(1)}, u32[]{:S(2)}, u32[]{:S(2)}) collective-permute-start(bf16[20,2048]{1,0:T(8,128)(2,1)S(1)} %get-tuple-element.25), channel_id=1, source_target_pairs={{0,88},{8,96},{16,104},{24,112},{32,120},{40,0},{48,8},{56,16},{64... | collective-permute-start | bytes 245768 | tf_op jit(solution)/shard_map/ppermute | solution.py:224
  204.7 37.2 %collective-permute-start.26 = (bf16[20,2048]{1,0:T(8,128)(2,1)S(1)}, bf16[20,2048]{1,0:T(8,128)(2,1)S(1)}, u32[]{:S(2)}, u32[]{:S(2)}) collective-permute-start(bf16[20,2048]{1,0:T(8,128)(2,1)S(1)} %get-tuple-element.24), channel_id=1, source_target_pairs={{0,96},{8,104},{16,112},{24,120},{32,0},{40,8},{48,16},{56,24},{64... | collective-permute-start | bytes 245768 | tf_op jit(solution)/shard_map/ppermute | solution.py:224
  210.2 34.7 %collective-permute-start.27 = (bf16[20,2048]{1,0:T(8,128)(2,1)S(1)}, bf16[20,2048]{1,0:T(8,128)(2,1)S(1)}, u32[]{:S(2)}, u32[]{:S(2)}) collective-permute-start(bf16[20,2048]{1,0:T(8,128)(2,1)S(1)} %get-tuple-element.23), channel_id=1, source_target_pairs={{0,104},{8,112},{16,120},{24,0},{32,8},{40,16},{48,24},{56,32},{64... | collective-permute-start | bytes 245768 | tf_op jit(solution)/shard_map/ppermute | solution.py:224
  216.4 35.3 %collective-permute-start.28 = (bf16[20,2048]{1,0:T(8,128)(2,1)S(1)}, bf16[20,2048]{1,0:T(8,128)(2,1)S(1)}, u32[]{:S(2)}, u32[]{:S(2)}) collective-permute-start(bf16[20,2048]{1,0:T(8,128)(2,1)S(1)} %get-tuple-element.22), channel_id=1, source_target_pairs={{0,112},{8,120},{16,0},{24,8},{32,16},{40,24},{48,32},{56,40},{64,... | collective-permute-start | bytes 245768 | tf_op jit(solution)/shard_map/ppermute | solution.py:224
  229.0 22.7 %collective-permute-start.29 = (bf16[20,2048]{1,0:T(8,128)(2,1)S(1)}, bf16[20,2048]{1,0:T(8,128)(2,1)S(1)}, u32[]{:S(2)}, u32[]{:S(2)}) collective-permute-start(bf16[20,2048]{1,0:T(8,128)(2,1)S(1)} %get-tuple-element.21), channel_id=1, source_target_pairs={{0,120},{8,0},{16,8},{24,16},{32,24},{40,32},{48,40},{56,48},{64,5... | collective-permute-start | bytes 245768 | tf_op jit(solution)/shard_map/ppermute | solution.py:224
  261.8 22.0 %collective-permute-start.30 = (bf16[20,2048]{1,0:T(8,128)(2,1)S(1)}, bf16[20,2048]{1,0:T(8,128)(2,1)S(1)}, u32[]{:S(2)}, u32[]{:S(2)}) collective-permute-start(bf16[20,2048]{1,0:T(8,128)(2,1)S(1)} %get-tuple-element.19), channel_id=1, source_target_pairs={{8,0},{16,8},{24,16},{32,24},{40,32},{48,40},{56,48},{64,56},{72,6... | collective-permute-start | bytes 245768 | tf_op jit(solution)/shard_map/ppermute | solution.py:241
  265.9 24.7 %collective-permute-start.31 = (bf16[20,2048]{1,0:T(8,128)(2,1)S(1)}, bf16[20,2048]{1,0:T(8,128)(2,1)S(1)}, u32[]{:S(2)}, u32[]{:S(2)}) collective-permute-start(bf16[20,2048]{1,0:T(8,128)(2,1)S(1)} %get-tuple-element.18), channel_id=1, source_target_pairs={{16,0},{24,8},{32,16},{40,24},{48,32},{56,40},{64,48},{72,56},{80,... | collective-permute-start | bytes 245768 | tf_op jit(solution)/shard_map/ppermute | solution.py:241
  269.2 26.3 %collective-permute-start.32 = (bf16[20,2048]{1,0:T(8,128)(2,1)S(1)}, bf16[20,2048]{1,0:T(8,128)(2,1)S(1)}, u32[]{:S(2)}, u32[]{:S(2)}) collective-permute-start(bf16[20,2048]{1,0:T(8,128)(2,1)S(1)} %get-tuple-element.17), channel_id=1, source_target_pairs={{24,0},{32,8},{40,16},{48,24},{56,32},{64,40},{72,48},{80,56},{88,... | collective-permute-start | bytes 245768 | tf_op jit(solution)/shard_map/ppermute | solution.py:241
  274.0 28.5 %collective-permute-start.33 = (bf16[20,2048]{1,0:T(8,128)(2,1)S(1)}, bf16[20,2048]{1,0:T(8,128)(2,1)S(1)}, u32[]{:S(2)}, u32[]{:S(2)}) collective-permute-start(bf16[20,2048]{1,0:T(8,128)(2,1)S(1)} %get-tuple-element.16), channel_id=1, source_target_pairs={{32,0},{40,8},{48,16},{56,24},{64,32},{72,40},{80,48},{88,56},{96,... | collective-permute-start | bytes 245768 | tf_op jit(solution)/shard_map/ppermute | solution.py:241
  279.2 29.8 %collective-permute-start.34 = (bf16[20,2048]{1,0:T(8,128)(2,1)S(1)}, bf16[20,2048]{1,0:T(8,128)(2,1)S(1)}, u32[]{:S(2)}, u32[]{:S(2)}) collective-permute-start(bf16[20,2048]{1,0:T(8,128)(2,1)S(1)} %get-tuple-element.15), channel_id=1, source_target_pairs={{40,0},{48,8},{56,16},{64,24},{72,32},{80,40},{88,48},{96,56},{104... | collective-permute-start | bytes 245768 | tf_op jit(solution)/shard_map/ppermute | solution.py:241
  283.8 31.9 %collective-permute-start.35 = (bf16[20,2048]{1,0:T(8,128)(2,1)S(1)}, bf16[20,2048]{1,0:T(8,128)(2,1)S(1)}, u32[]{:S(2)}, u32[]{:S(2)}) collective-permute-start(bf16[20,2048]{1,0:T(8,128)(2,1)S(1)} %get-tuple-element.14), channel_id=1, source_target_pairs={{48,0},{56,8},{64,16},{72,24},{80,32},{88,40},{96,48},{104,56},{11... | collective-permute-start | bytes 245768 | tf_op jit(solution)/shard_map/ppermute | solution.py:241
  290.5 33.8 %collective-permute-start.36 = (bf16[20,2048]{1,0:T(8,128)(2,1)S(1)}, bf16[20,2048]{1,0:T(8,128)(2,1)S(1)}, u32[]{:S(2)}, u32[]{:S(2)}) collective-permute-start(bf16[20,2048]{1,0:T(8,128)(2,1)S(1)} %get-tuple-element.13), channel_id=1, source_target_pairs={{56,0},{64,8},{72,16},{80,24},{88,32},{96,40},{104,48},{112,56},{1... | collective-permute-start | bytes 245768 | tf_op jit(solution)/shard_map/ppermute | solution.py:241
  295.5 34.9 %collective-permute-start.37 = (bf16[20,2048]{1,0:T(8,128)(2,1)S(1)}, bf16[20,2048]{1,0:T(8,128)(2,1)S(1)}, u32[]{:S(2)}, u32[]{:S(2)}) collective-permute-start(bf16[20,2048]{1,0:T(8,128)(2,1)S(1)} %get-tuple-element.12), channel_id=1, source_target_pairs={{64,0},{72,8},{80,16},{88,24},{96,32},{104,40},{112,48},{120,56},{... | collective-permute-start | bytes 245768 | tf_op jit(solution)/shard_map/ppermute | solution.py:241
  302.6 40.5 %collective-permute-start.38 = (bf16[20,2048]{1,0:T(8,128)(2,1)S(1)}, bf16[20,2048]{1,0:T(8,128)(2,1)S(1)}, u32[]{:S(2)}, u32[]{:S(2)}) collective-permute-start(bf16[20,2048]{1,0:T(8,128)(2,1)S(1)} %get-tuple-element.11), channel_id=1, source_target_pairs={{72,0},{80,8},{88,16},{96,24},{104,32},{112,40},{120,48},{0,56},{8... | collective-permute-start | bytes 245768 | tf_op jit(solution)/shard_map/ppermute | solution.py:241
  309.0 36.0 %collective-permute-start.39 = (bf16[20,2048]{1,0:T(8,128)(2,1)S(1)}, bf16[20,2048]{1,0:T(8,128)(2,1)S(1)}, u32[]{:S(2)}, u32[]{:S(2)}) collective-permute-start(bf16[20,2048]{1,0:T(8,128)(2,1)S(1)} %get-tuple-element.10), channel_id=1, source_target_pairs={{80,0},{88,8},{96,16},{104,24},{112,32},{120,40},{0,48},{8,56},{16... | collective-permute-start | bytes 245768 | tf_op jit(solution)/shard_map/ppermute | solution.py:241
  315.7 39.1 %collective-permute-start.40 = (bf16[20,2048]{1,0:T(8,128)(2,1)S(1)}, bf16[20,2048]{1,0:T(8,128)(2,1)S(1)}, u32[]{:S(2)}, u32[]{:S(2)}) collective-permute-start(bf16[20,2048]{1,0:T(8,128)(2,1)S(1)} %get-tuple-element.9), channel_id=1, source_target_pairs={{88,0},{96,8},{104,16},{112,24},{120,32},{0,40},{8,48},{16,56},{24... | collective-permute-start | bytes 245768 | tf_op jit(solution)/shard_map/ppermute | solution.py:241
  324.3 31.1 %collective-permute-start.41 = (bf16[20,2048]{1,0:T(8,128)(2,1)S(1)}, bf16[20,2048]{1,0:T(8,128)(2,1)S(1)}, u32[]{:S(2)}, u32[]{:S(2)}) collective-permute-start(bf16[20,2048]{1,0:T(8,128)(2,1)S(1)} %get-tuple-element.8), channel_id=1, source_target_pairs={{96,0},{104,8},{112,16},{120,24},{0,32},{8,40},{16,48},{24,56},{32... | collective-permute-start | bytes 245768 | tf_op jit(solution)/shard_map/ppermute | solution.py:241
  330.4 38.3 %collective-permute-start.42 = (bf16[20,2048]{1,0:T(8,128)(2,1)S(1)}, bf16[20,2048]{1,0:T(8,128)(2,1)S(1)}, u32[]{:S(2)}, u32[]{:S(2)}) collective-permute-start(bf16[20,2048]{1,0:T(8,128)(2,1)S(1)} %get-tuple-element.7), channel_id=1, source_target_pairs={{104,0},{112,8},{120,16},{0,24},{8,32},{16,40},{24,48},{32,56},{40... | collective-permute-start | bytes 245768 | tf_op jit(solution)/shard_map/ppermute | solution.py:241
  343.1 26.7 %collective-permute-start.43 = (bf16[20,2048]{1,0:T(8,128)(2,1)S(1)}, bf16[20,2048]{1,0:T(8,128)(2,1)S(1)}, u32[]{:S(2)}, u32[]{:S(2)}) collective-permute-start(bf16[20,2048]{1,0:T(8,128)(2,1)S(1)} %get-tuple-element.6), channel_id=1, source_target_pairs={{112,0},{120,8},{0,16},{8,24},{16,32},{24,40},{32,48},{40,56},{48,... | collective-permute-start | bytes 245768 | tf_op jit(solution)/shard_map/ppermute | solution.py:241
  345.0 28.9 %collective-permute-start.44 = (bf16[20,2048]{1,0:T(8,128)(2,1)S(1)}, bf16[20,2048]{1,0:T(8,128)(2,1)S(1)}, u32[]{:S(2)}, u32[]{:S(2)}) collective-permute-start(bf16[20,2048]{1,0:T(8,128)(2,1)S(1)} %get-tuple-element.5), channel_id=1, source_target_pairs={{120,0},{0,8},{8,16},{16,24},{24,32},{32,40},{40,48},{48,56},{56,6... | collective-permute-start | bytes 245768 | tf_op jit(solution)/shard_map/ppermute | solution.py:241
  (32 other events, 614.8 us)

commit v6 on v4

--- a/solution.py
+++ b/solution.py
@@ -222,22 +222,22 @@
     result = jnp.einsum(
         "psh,hd->psd", hidden, w_down[0], preferred_element_type=jnp.float32
     ).astype(jnp.bfloat16)
-    returned = lax.all_to_all(
-        result,
-        "seq",
-        split_axis=0,
-        concat_axis=0,
-        tiled=True,
-    )
-    combine_map = (placement_map.astype(jnp.float32) * share_weight[:, :, None]).astype(
-        jnp.bfloat16
-    )
-    moe = jnp.einsum("tps,psd->td", combine_map, returned, preferred_element_type=jnp.float32)
-    moe_pieces = moe.astype(jnp.bfloat16).reshape(length, column_total, share_width)
-    moe_pieces = lax.all_to_all(
-        moe_pieces.transpose(1, 0, 2), "head", split_axis=0, concat_axis=0, tiled=True
-    )
-    moe_share = jnp.sum(moe_pieces.astype(jnp.float32), axis=0)
+    sliced = result.reshape(peer_count, slot_count, column_count, share_width)
+    sliced = sliced.transpose(0, 2, 1, 3).reshape(expert_count, slot_count, share_width)
+    returned = lax.all_to_all(sliced, ("seq", "head"), split_axis=0, concat_axis=0, tiled=True)
+    every_expert = jnp.arange(expert_count, dtype=jnp.int32)
+    hits_all = expert_ids[:, :, None] == every_expert[None, None, :]
+    chosen_all = jnp.sum(hits_all.astype(jnp.int32), axis=1)
+    weight_all = jnp.sum(jnp.where(hits_all, weights[:, :, None], 0.0), axis=1)
+    rank_all = jnp.cumsum(chosen_all, axis=0) - chosen_all
+    combine_all = jnp.where(
+        (chosen_all[:, :, None] == 1) & (rank_all[:, :, None] == slot_index[None, None, :]),
+        weight_all[:, :, None],
+        0.0,
+    ).astype(jnp.bfloat16)
+    moe_share = jnp.einsum(
+        "tes,esc->tc", combine_all, returned, preferred_element_type=jnp.float32
+    )
     return (resid_share.astype(jnp.float32) + moe_share).astype(jnp.bfloat16)
 
 

time: 329 us -> 324 us (0.985)
  blocking collectives: 90.9 us -> 72.9 us
  local copies, waits for them, and re-layouts: 8.94 us -> 13.7 us
  starting transfers between devices: 91.3 us -> 95.3 us
    all_to_all x1 -> x0, blocking collectives: 18 us -> none  [on_device(): lax.all_to_all(moe_pieces.transpose(1, 0, 2), 'head', split_axis=0, conca...]
    reshape x1 -> x3, local copies, waits for them, and re-layouts: 0.04 us -> 4.64 us  [the longest x2 2.73 us: on_device(): sliced = result.reshape(peer_count, slot_count, column_count, share_width)]
    all_to_all x1, starting transfers between devices: 12.3 us -> 16 us  [on_device(): lax.all_to_all(sliced, ('seq', 'head'), split_axis=0, concat_axis=0, tile...]
    all_to_all x1, waiting for transfers between devices: 68.9 us -> 72.5 us  [on_device(): lax.all_to_all(sliced, ('seq', 'head'), split_axis=0, concat_axis=0, tile...]
where the time goes in v6:
time: 324 us; the launch traced here: 321 us
  waiting for transfers between devices  105 us (32%)
  starting transfers between devices  95.3 us (29%)
  blocking collectives  72.9 us (23%)
  matrix products  27.3 us (8%)
  local copies, waits for them, and re-layouts  13.7 us (4%)
  other arithmetic  5.42 us (2%)
    all_to_all x1, blocking collectives, on_device(): lax.all_to_all(outgoing, 'seq', split_axis=0, concat_axis=0, tiled=True)  72.9 us
    all_to_all x1, waiting for transfers between devices, on_device(): lax.all_to_all(sliced, ('seq', 'head'), split_axis=0, concat_axis=0, tile...  72.5 us
    ppermute x7, starting transfers between devices, on_device(): going_down = lax.ppermute(going_down, 'seq', backward_pairs)  43.7 us
    ppermute x8, starting transfers between devices, on_device(): going_up = lax.ppermute(going_up, 'seq', forward_pairs)  18.3 us
    all_to_all x1, starting transfers between devices, on_device(): lax.all_to_all(sliced, ('seq', 'head'), split_axis=0, concat_axis=0, tile...  16 us
    ppermute x8, waiting for transfers between devices, on_device(): going_up = lax.ppermute(going_up, 'seq', forward_pairs)  14.1 us
    all_to_all x1, starting transfers between devices, on_device(): lax.all_to_all(attn_pieces.transpose(1, 0, 2), 'head', split_axis=0, conc...  13 us
    all_to_all x1, waiting for transfers between devices, on_device(): lax.all_to_all(attn_pieces.transpose(1, 0, 2), 'head', split_axis=0, conc...  9.48 us
  transfers between devices with their start and end apart: 18, of which 10 were waited for; matrix products, arithmetic and copies ran while one was open for 4% of the time, Pallas kernels for 0%

profile of v6, /device:TPU:1, one launch (start us, length us, event | category | flops | bytes accessed | tf_op | source)
XLA Modules:
  0.0 320.7 jit_solution(3292083498247781444)
XLA Ops:
  12.0 4.8 %collective-permute-start = (bf16[8,128,128]{2,1,0:T(8,128)(2,1)}, bf16[8,128,128]{2,1,0:T(8,128)(2,1)S(1)}, u32[]{:S(2)}, u32[]{:S(2)}) collective-permute-start(bf16[8,128,128]{2,1,0:T(8,128)(2,1)} %pad_maximum_fusion), channel_id=1, source_target_pairs={{0,8},{8,16},{16,24},{24,32},{32,40},{40,48},{48,56},{56,64},{64,7... | collective-permute-start | bytes 786440 | tf_op jit(solution)/shard_map/ppermute | solution.py:148
  16.8 15.9 %collective-permute-start.8 = (bf16[8,128,128]{2,1,0:T(8,128)(2,1)}, bf16[8,128,128]{2,1,0:T(8,128)(2,1)}, u32[]{:S(2)}, u32[]{:S(2)}) collective-permute-start(bf16[8,128,128]{2,1,0:T(8,128)(2,1)} %pad_maximum_fusion), channel_id=1, source_target_pairs={{0,120},{8,0},{16,8},{24,16},{32,24},{40,32},{48,40},{56,48},{64,5... | collective-permute-start | bytes 786440 | tf_op jit(solution)/shard_map/ppermute | solution.py:159
  33.3 1.4 convolution_multiply_fusion.1
  34.7 2.3 collective-permute-done
  37.0 1.9 collective-permute-start.1
  40.9 4.6 %collective-permute-start.9 = (bf16[8,128,128]{2,1,0:T(8,128)(2,1)}, bf16[8,128,128]{2,1,0:T(8,128)(2,1)S(1)}, u32[]{:S(2)}, u32[]{:S(2)}) collective-permute-start(bf16[8,128,128]{2,1,0:T(8,128)(2,1)} %collective-permute-done.8), channel_id=1, source_target_pairs={{0,120},{8,0},{16,8},{24,16},{32,24},{40,32},{48,40},{56,48},{64,5... | collective-permute-start | bytes 786440 | tf_op jit(solution)/shard_map/ppermute | solution.py:159
  45.5 1.4 fusion.20
  47.9 1.9 collective-permute-start.2
  50.3 4.8 %collective-permute-start.10 = (bf16[8,128,128]{2,1,0:T(8,128)(2,1)S(1)}, bf16[8,128,128]{2,1,0:T(8,128)(2,1)S(1)}, u32[]{:S(2)}, u32[]{:S(2)}) collective-permute-start(bf16[8,128,128]{2,1,0:T(8,128)(2,1)S(1)} %collective-permute-done.9), channel_id=1, source_target_pairs={{0,120},{8,0},{16,8},{24,16},{32,24},{40,32},{48,40},{56,48},{64,5... | collective-permute-start | bytes 786440 | tf_op jit(solution)/shard_map/ppermute | solution.py:159
  55.4 1.7 collective-permute-done.2
  57.1 1.9 collective-permute-start.3
  59.6 4.6 %collective-permute-start.11 = (bf16[8,128,128]{2,1,0:T(8,128)(2,1)S(1)}, bf16[8,128,128]{2,1,0:T(8,128)(2,1)S(1)}, u32[]{:S(2)}, u32[]{:S(2)}) collective-permute-start(bf16[8,128,128]{2,1,0:T(8,128)(2,1)S(1)} %collective-permute-done.10), channel_id=1, source_target_pairs={{0,120},{8,0},{16,8},{24,16},{32,24},{40,32},{48,40},{56,48},{64,5... | collective-permute-start | bytes 786440 | tf_op jit(solution)/shard_map/ppermute | solution.py:159
  65.4 1.9 collective-permute-start.4
  68.0 4.8 %collective-permute-start.12 = (bf16[8,128,128]{2,1,0:T(8,128)(2,1)S(1)}, bf16[8,128,128]{2,1,0:T(8,128)(2,1)S(1)}, u32[]{:S(2)}, u32[]{:S(2)}) collective-permute-start(bf16[8,128,128]{2,1,0:T(8,128)(2,1)S(1)} %collective-permute-done.11), channel_id=1, source_target_pairs={{0,120},{8,0},{16,8},{24,16},{32,24},{40,32},{48,40},{56,48},{64,5... | collective-permute-start | bytes 786440 | tf_op jit(solution)/shard_map/ppermute | solution.py:159
  73.8 1.9 collective-permute-start.5
  76.4 4.6 %collective-permute-start.13 = (bf16[8,128,128]{2,1,0:T(8,128)(2,1)S(1)}, bf16[8,128,128]{2,1,0:T(8,128)(2,1)S(1)}, u32[]{:S(2)}, u32[]{:S(2)}) collective-permute-start(bf16[8,128,128]{2,1,0:T(8,128)(2,1)S(1)} %collective-permute-done.12), channel_id=1, source_target_pairs={{0,120},{8,0},{16,8},{24,16},{32,24},{40,32},{48,40},{56,48},{64,5... | collective-permute-start | bytes 786440 | tf_op jit(solution)/shard_map/ppermute | solution.py:159
  82.2 1.9 collective-permute-start.6
  84.7 4.6 %collective-permute-start.14 = (bf16[8,128,128]{2,1,0:T(8,128)(2,1)S(1)}, bf16[8,128,128]{2,1,0:T(8,128)(2,1)S(1)}, u32[]{:S(2)}, u32[]{:S(2)}) collective-permute-start(bf16[8,128,128]{2,1,0:T(8,128)(2,1)S(1)} %collective-permute-done.13), channel_id=1, source_target_pairs={{0,120},{8,0},{16,8},{24,16},{32,24},{40,32},{48,40},{56,48},{64,5... | collective-permute-start | bytes 786440 | tf_op jit(solution)/shard_map/ppermute | solution.py:159
  90.7 1.9 collective-permute-start.7
  93.5 6.7 %collective-permute-done.7 = bf16[8,128,128]{2,1,0:T(8,128)(2,1)S(1)} collective-permute-done((bf16[8,128,128]{2,1,0:T(8,128)(2,1)S(1)}, bf16[8,128,128]{2,1,0:T(8,128)(2,1)S(1)}, u32[]{:S(2)}, u32[]{:S(2)}) %collective-permute-start.7) | collective-permute-done | bytes 262176 | tf_op jit(solution)/shard_map/ppermute | solution.py:148
  104.3 13.0 %all-to-all-start = ((bf16[8,128,256]{2,1,0:T(8,128)(2,1)}), bf16[8,128,256]{2,1,0:T(8,128)(2,1)S(1)}, u32[]{:S(2)}, u32[]{:S(2)}) async-start(bf16[8,128,256]{2,1,0:T(8,128)(2,1)} %bitcast.164), calls=%async_computation | async-start | bytes 1048576 | tf_op jit(solution)/shard_map/all_to_all | solution.py:180
  117.2 9.5 %all-to-all-done = bf16[8,128,256]{2,1,0:T(8,128)(2,1)S(1)} async-done(((bf16[8,128,256]{2,1,0:T(8,128)(2,1)}), bf16[8,128,256]{2,1,0:T(8,128)(2,1)S(1)}, u32[]{:S(2)}, u32[]{:S(2)}) %all-to-all-start) | async-done | bytes 524320 | tf_op jit(solution)/shard_map/all_to_all | solution.py:180
  128.5 4.4 %all-to-all-start.1 = ((bf16[8,128,256]{2,1,0:T(8,128)(2,1)}), bf16[8,128,256]{2,1,0:T(8,128)(2,1)S(1)}, u32[]{:S(2)}, u32[]{:S(2)}) async-start(bf16[8,128,256]{2,1,0:T(8,128)(2,1)} %broadcast_in_dim.51), calls=%async_computation.1 | async-start | bytes 1048576 | tf_op jit(solution)/shard_map/all_to_all | solution.py:187
  133.3 9.1 %all-to-all-done.1 = bf16[8,128,256]{2,1,0:T(8,128)(2,1)S(1)} async-done(((bf16[8,128,256]{2,1,0:T(8,128)(2,1)}), bf16[8,128,256]{2,1,0:T(8,128)(2,1)S(1)}, u32[]{:S(2)}, u32[]{:S(2)}) %all-to-all-start.1) | async-done | bytes 524320 | tf_op jit(solution)/shard_map/all_to_all | solution.py:187
  143.9 72.9 %all_to_all.20 = bf16[16,20,2048]{2,1,0:T(8,128)(2,1)S(1)} all-to-all(bf16[16,20,2048]{2,1,0:T(8,128)(2,1)S(1)} %convolution_convert_fusion.1), channel_id=1, replica_groups=mesh['dp'=8,'seq'=16,'head'=8] {'seq'}, dimensions={0} | all-to-all | bytes 2621440 | tf_op jit(solution)/shard_map/all_to_all | solution.py:218
  216.8 1.2 copy-done.2
  219.0 5.1 %convolution_convert_fusion = bf16[16,20,2048]{2,1,0:T(8,128)(2,1)} fusion(bf16[1,512,2048]{2,1,0:T(8,128)(2,1)S(1)} %copy-done, bf16[16,20,2048]{2,1,0:T(8,128)(2,1)} %copy-done.2, bf16[1,2048,512]{2,1,0:T(8,128)(2,1)} %param.30, f32[16,20,512]{2,1,0:T(8,128)S(1)} %fusion.3), kind=kOutput, calls=%fused_computation | convolution fusion | flops 1343815680 | bytes 7471104 | tf_op jit(solution)/shard_map/psh,hd->psd/dot_general | solution.py:222
  224.1 2.6 reshape.173
  226.8 1.9 copy.249
  228.8 16.0 %all-to-all-start.3 = ((bf16[128,20,256]{2,1,0:T(8,128)(2,1)}), bf16[128,20,256]{2,1,0:T(8,128)(2,1)}, u32[]{:S(2)}, u32[]{:S(2)}) async-start(bf16[128,20,256]{2,1,0:T(8,128)(2,1)} %copy.249), calls=%async_computation.3 | async-start | bytes 3145728 | tf_op jit(solution)/shard_map/all_to_all | solution.py:227
  245.7 72.5 %all-to-all-done.3 = bf16[128,20,256]{2,1,0:T(8,128)(2,1)} async-done(((bf16[128,20,256]{2,1,0:T(8,128)(2,1)}), bf16[128,20,256]{2,1,0:T(8,128)(2,1)}, u32[]{:S(2)}, u32[]{:S(2)}) %all-to-all-start.3) | async-done | bytes 1310752 | tf_op jit(solution)/shard_map/all_to_all | solution.py:227
  318.2 2.6 fusion.34
  (161 shorter events, 33.7 us)
Async XLA Ops:
  0.0 218.9 %copy-start = (bf16[1,512,2048]{2,1,0:T(8,128)(2,1)S(1)}, bf16[1,512,2048]{2,1,0:T(8,128)(2,1)}, u32[]{:S(2)}) copy-start(bf16[1,512,2048]{2,1,0:T(8,128)(2,1)} %param.31) | copy-start | bytes 6291460
  0.0 2.7 copy-start.10
  2.6 6.0 %copy-start.6 = (f32[128,4]{0,1:T(4,128)}, f32[128,4]{0,1:T(4,128)S(1)}, u32[]{:S(2)}) copy-start(f32[128,4]{0,1:T(4,128)S(1)} %copy.221) | copy-start | bytes 6148
  7.2 1.5 copy-start.5
  7.5 1.7 copy-start.12
  9.4 23.3 %copy-start.8 = (bf16[128,256]{1,0:T(8,128)(2,1)S(1)}, bf16[128,256]{1,0:T(8,128)(2,1)}, u32[]{:S(2)}) copy-start(bf16[128,256]{1,0:T(8,128)(2,1)} %param.17) | copy-start | bytes 196612
  12.0 25.0 %collective-permute-start = (bf16[8,128,128]{2,1,0:T(8,128)(2,1)}, bf16[8,128,128]{2,1,0:T(8,128)(2,1)S(1)}, u32[]{:S(2)}, u32[]{:S(2)}) collective-permute-start(bf16[8,128,128]{2,1,0:T(8,128)(2,1)} %pad_maximum_fusion), channel_id=1, source_target_pairs={{0,8},{8,16},{16,24},{24,32},{32,40},{40,48},{48,56},{56,64},{64,7... | collective-permute-start | bytes 786440 | tf_op jit(solution)/shard_map/ppermute | solution.py:148
  16.8 24.1 %collective-permute-start.8 = (bf16[8,128,128]{2,1,0:T(8,128)(2,1)}, bf16[8,128,128]{2,1,0:T(8,128)(2,1)}, u32[]{:S(2)}, u32[]{:S(2)}) collective-permute-start(bf16[8,128,128]{2,1,0:T(8,128)(2,1)} %pad_maximum_fusion), channel_id=1, source_target_pairs={{0,120},{8,0},{16,8},{24,16},{32,24},{40,32},{48,40},{56,48},{64,5... | collective-permute-start | bytes 786440 | tf_op jit(solution)/shard_map/ppermute | solution.py:159
  32.8 7.3 %copy-start.4 = (bf16[128,512]{1,0:T(8,128)(2,1)S(1)}, bf16[128,512]{1,0:T(8,128)(2,1)}, u32[]{:S(2)}) copy-start(bf16[128,512]{1,0:T(8,128)(2,1)} %param.20) | copy-start | bytes 393220
  37.0 9.9 %collective-permute-start.1 = (bf16[8,128,128]{2,1,0:T(8,128)(2,1)S(1)}, bf16[8,128,128]{2,1,0:T(8,128)(2,1)}, u32[]{:S(2)}, u32[]{:S(2)}) collective-permute-start(bf16[8,128,128]{2,1,0:T(8,128)(2,1)S(1)} %collective-permute-done), channel_id=1, source_target_pairs={{0,8},{8,16},{16,24},{24,32},{32,40},{40,48},{48,56},{56,64},{64,7... | collective-permute-start | bytes 786440 | tf_op jit(solution)/shard_map/ppermute | solution.py:148
  40.9 9.4 %collective-permute-start.9 = (bf16[8,128,128]{2,1,0:T(8,128)(2,1)}, bf16[8,128,128]{2,1,0:T(8,128)(2,1)S(1)}, u32[]{:S(2)}, u32[]{:S(2)}) collective-permute-start(bf16[8,128,128]{2,1,0:T(8,128)(2,1)} %collective-permute-done.8), channel_id=1, source_target_pairs={{0,120},{8,0},{16,8},{24,16},{32,24},{40,32},{48,40},{56,48},{64,5... | collective-permute-start | bytes 786440 | tf_op jit(solution)/shard_map/ppermute | solution.py:159
  47.9 9.1 %collective-permute-start.2 = (bf16[8,128,128]{2,1,0:T(8,128)(2,1)}, bf16[8,128,128]{2,1,0:T(8,128)(2,1)S(1)}, u32[]{:S(2)}, u32[]{:S(2)}) collective-permute-start(bf16[8,128,128]{2,1,0:T(8,128)(2,1)} %collective-permute-done.1), channel_id=1, source_target_pairs={{0,8},{8,16},{16,24},{24,32},{32,40},{40,48},{48,56},{56,64},{64,7... | collective-permute-start | bytes 786440 | tf_op jit(solution)/shard_map/ppermute | solution.py:148
  50.3 9.3 %collective-permute-start.10 = (bf16[8,128,128]{2,1,0:T(8,128)(2,1)S(1)}, bf16[8,128,128]{2,1,0:T(8,128)(2,1)S(1)}, u32[]{:S(2)}, u32[]{:S(2)}) collective-permute-start(bf16[8,128,128]{2,1,0:T(8,128)(2,1)S(1)} %collective-permute-done.9), channel_id=1, source_target_pairs={{0,120},{8,0},{16,8},{24,16},{32,24},{40,32},{48,40},{56,48},{64,5... | collective-permute-start | bytes 786440 | tf_op jit(solution)/shard_map/ppermute | solution.py:159
  57.1 8.3 %collective-permute-start.3 = (bf16[8,128,128]{2,1,0:T(8,128)(2,1)S(1)}, bf16[8,128,128]{2,1,0:T(8,128)(2,1)S(1)}, u32[]{:S(2)}, u32[]{:S(2)}) collective-permute-start(bf16[8,128,128]{2,1,0:T(8,128)(2,1)S(1)} %collective-permute-done.2), channel_id=1, source_target_pairs={{0,8},{8,16},{16,24},{24,32},{32,40},{40,48},{48,56},{56,64},{64,7... | collective-permute-start | bytes 786440 | tf_op jit(solution)/shard_map/ppermute | solution.py:148
  59.6 8.4 %collective-permute-start.11 = (bf16[8,128,128]{2,1,0:T(8,128)(2,1)S(1)}, bf16[8,128,128]{2,1,0:T(8,128)(2,1)S(1)}, u32[]{:S(2)}, u32[]{:S(2)}) collective-permute-start(bf16[8,128,128]{2,1,0:T(8,128)(2,1)S(1)} %collective-permute-done.10), channel_id=1, source_target_pairs={{0,120},{8,0},{16,8},{24,16},{32,24},{40,32},{48,40},{56,48},{64,5... | collective-permute-start | bytes 786440 | tf_op jit(solution)/shard_map/ppermute | solution.py:159
  65.4 8.3 %collective-permute-start.4 = (bf16[8,128,128]{2,1,0:T(8,128)(2,1)S(1)}, bf16[8,128,128]{2,1,0:T(8,128)(2,1)S(1)}, u32[]{:S(2)}, u32[]{:S(2)}) collective-permute-start(bf16[8,128,128]{2,1,0:T(8,128)(2,1)S(1)} %collective-permute-done.3), channel_id=1, source_target_pairs={{0,8},{8,16},{16,24},{24,32},{32,40},{40,48},{48,56},{56,64},{64,7... | collective-permute-start | bytes 786440 | tf_op jit(solution)/shard_map/ppermute | solution.py:148
  68.0 8.3 %collective-permute-start.12 = (bf16[8,128,128]{2,1,0:T(8,128)(2,1)S(1)}, bf16[8,128,128]{2,1,0:T(8,128)(2,1)S(1)}, u32[]{:S(2)}, u32[]{:S(2)}) collective-permute-start(bf16[8,128,128]{2,1,0:T(8,128)(2,1)S(1)} %collective-permute-done.11), channel_id=1, source_target_pairs={{0,120},{8,0},{16,8},{24,16},{32,24},{40,32},{48,40},{56,48},{64,5... | collective-permute-start | bytes 786440 | tf_op jit(solution)/shard_map/ppermute | solution.py:159
  73.8 8.3 %collective-permute-start.5 = (bf16[8,128,128]{2,1,0:T(8,128)(2,1)S(1)}, bf16[8,128,128]{2,1,0:T(8,128)(2,1)S(1)}, u32[]{:S(2)}, u32[]{:S(2)}) collective-permute-start(bf16[8,128,128]{2,1,0:T(8,128)(2,1)S(1)} %collective-permute-done.4), channel_id=1, source_target_pairs={{0,8},{8,16},{16,24},{24,32},{32,40},{40,48},{48,56},{56,64},{64,7... | collective-permute-start | bytes 786440 | tf_op jit(solution)/shard_map/ppermute | solution.py:148
  76.4 8.4 %collective-permute-start.13 = (bf16[8,128,128]{2,1,0:T(8,128)(2,1)S(1)}, bf16[8,128,128]{2,1,0:T(8,128)(2,1)S(1)}, u32[]{:S(2)}, u32[]{:S(2)}) collective-permute-start(bf16[8,128,128]{2,1,0:T(8,128)(2,1)S(1)} %collective-permute-done.12), channel_id=1, source_target_pairs={{0,120},{8,0},{16,8},{24,16},{32,24},{40,32},{48,40},{56,48},{64,5... | collective-permute-start | bytes 786440 | tf_op jit(solution)/shard_map/ppermute | solution.py:159
  82.2 8.4 %collective-permute-start.6 = (bf16[8,128,128]{2,1,0:T(8,128)(2,1)S(1)}, bf16[8,128,128]{2,1,0:T(8,128)(2,1)S(1)}, u32[]{:S(2)}, u32[]{:S(2)}) collective-permute-start(bf16[8,128,128]{2,1,0:T(8,128)(2,1)S(1)} %collective-permute-done.5), channel_id=1, source_target_pairs={{0,8},{8,16},{16,24},{24,32},{32,40},{40,48},{48,56},{56,64},{64,7... | collective-permute-start | bytes 786440 | tf_op jit(solution)/shard_map/ppermute | solution.py:148
  84.7 8.5 %collective-permute-start.14 = (bf16[8,128,128]{2,1,0:T(8,128)(2,1)S(1)}, bf16[8,128,128]{2,1,0:T(8,128)(2,1)S(1)}, u32[]{:S(2)}, u32[]{:S(2)}) collective-permute-start(bf16[8,128,128]{2,1,0:T(8,128)(2,1)S(1)} %collective-permute-done.13), channel_id=1, source_target_pairs={{0,120},{8,0},{16,8},{24,16},{32,24},{40,32},{48,40},{56,48},{64,5... | collective-permute-start | bytes 786440 | tf_op jit(solution)/shard_map/ppermute | solution.py:159
  90.7 9.5 %collective-permute-start.7 = (bf16[8,128,128]{2,1,0:T(8,128)(2,1)S(1)}, bf16[8,128,128]{2,1,0:T(8,128)(2,1)S(1)}, u32[]{:S(2)}, u32[]{:S(2)}) collective-permute-start(bf16[8,128,128]{2,1,0:T(8,128)(2,1)S(1)} %collective-permute-done.6), channel_id=1, source_target_pairs={{0,8},{8,16},{16,24},{24,32},{32,40},{40,48},{48,56},{56,64},{64,7... | collective-permute-start | bytes 786440 | tf_op jit(solution)/shard_map/ppermute | solution.py:148
  100.8 1.7 copy-start.3
  100.8 1.7 copy-start.15
  101.3 1.6 copy-start.1
  104.3 28.6 %copy-start.7 = (s32[128,10]{0,1:T(8,128)S(1)}, s32[128,10]{0,1:T(8,128)}, u32[]{:S(2)}) copy-start(s32[128,10]{0,1:T(8,128)} %param.27) | copy-start | bytes 15364
  104.3 22.4 %all-to-all-start = ((bf16[8,128,256]{2,1,0:T(8,128)(2,1)}), bf16[8,128,256]{2,1,0:T(8,128)(2,1)S(1)}, u32[]{:S(2)}, u32[]{:S(2)}) async-start(bf16[8,128,256]{2,1,0:T(8,128)(2,1)} %bitcast.164), calls=%async_computation | async-start | bytes 1048576 | tf_op jit(solution)/shard_map/all_to_all | solution.py:180
  128.5 14.5 %copy-start.14 = (f32[2048]{0:T(1024)S(1)}, f32[2048]{0:T(1024)}, u32[]{:S(2)}) copy-start(f32[2048]{0:T(1024)} %param.26) | copy-start | bytes 24580
  128.5 13.9 %all-to-all-start.1 = ((bf16[8,128,256]{2,1,0:T(8,128)(2,1)}), bf16[8,128,256]{2,1,0:T(8,128)(2,1)S(1)}, u32[]{:S(2)}, u32[]{:S(2)}) async-start(bf16[8,128,256]{2,1,0:T(8,128)(2,1)} %broadcast_in_dim.51), calls=%async_computation.1 | async-start | bytes 1048576 | tf_op jit(solution)/shard_map/all_to_all | solution.py:187
  143.9 74.1 %copy-start.16 = (bf16[1,2048,512]{2,1,0:T(8,128)(2,1)S(1)}, bf16[1,2048,512]{2,1,0:T(8,128)(2,1)}, u32[]{:S(2)}) copy-start(bf16[1,2048,512]{2,1,0:T(8,128)(2,1)} %param.29) | copy-start | bytes 6291460
  228.8 16.4 %copy-start.9 = (f32[128,10]{0,1:T(8,128)S(1)}, f32[128,10]{0,1:T(8,128)}, u32[]{:S(2)}) copy-start(f32[128,10]{0,1:T(8,128)} %param.28) | copy-start | bytes 15364
  228.8 89.4 %all-to-all-start.3 = ((bf16[128,20,256]{2,1,0:T(8,128)(2,1)}), bf16[128,20,256]{2,1,0:T(8,128)(2,1)}, u32[]{:S(2)}, u32[]{:S(2)}) async-start(bf16[128,20,256]{2,1,0:T(8,128)(2,1)} %copy.249), calls=%async_computation.3 | async-start | bytes 3145728 | tf_op jit(solution)/shard_map/all_to_all | solution.py:227
  (3 other events, 3.3 us)

commit v7 on v6

--- a/solution.py
+++ b/solution.py
@@ -184,38 +184,46 @@
     stream_share = lax.dynamic_slice_in_dim(stream, share_start, share_width, 1)
     resid_share = (stream_share.astype(jnp.float32) + attn_share).astype(jnp.bfloat16)
     resid_share = lax.optimization_barrier(resid_share)
-    resid_rows = lax.all_to_all(
-        jnp.broadcast_to(resid_share[None], (column_total, length, share_width)),
+    resid_f = resid_share.astype(jnp.float32)
+    square_part = jnp.sum(resid_f * resid_f, axis=-1)
+    square_parts = lax.all_to_all(
+        jnp.broadcast_to(square_part[None], (column_total, length)),
         "head",
         split_axis=0,
         concat_axis=0,
         tiled=True,
     )
-    resid = resid_rows.transpose(1, 0, 2).reshape(length, model_width)
-    resid_f = resid.astype(jnp.float32)
-    normed = (
-        resid_f * lax.rsqrt(jnp.mean(resid_f * resid_f, axis=-1, keepdims=True) + 1e-06) * post_gain
+    square_mean = jnp.sum(square_parts, axis=0) / model_width
+    gain_share = lax.dynamic_slice_in_dim(post_gain, share_start, share_width, 0)
+    normed_share = (
+        resid_f * lax.rsqrt(square_mean[:, None] + 1e-06) * gain_share
     ).astype(jnp.bfloat16)
     peer_count = lax.axis_size("seq")
     column_count = lax.axis_size("head")
     expert_count = peer_count * column_count
     pick_count = expert_ids.shape[1]
     slot_count = min(length, length * pick_count * 2 // expert_count)
-    targets = jnp.arange(peer_count, dtype=jnp.int32) * column_count + lax.axis_index("head")
-    hits = expert_ids[:, :, None] == targets[None, None, :]
     weights = (route_scores / jnp.sum(route_scores, axis=1, keepdims=True)).astype(jnp.bfloat16)
     weights = lax.optimization_barrier(weights).astype(jnp.float32)
-    chosen = jnp.sum(hits.astype(jnp.int32), axis=1)
-    share_weight = jnp.sum(jnp.where(hits, weights[:, :, None], 0.0), axis=1)
-    rank = jnp.cumsum(chosen, axis=0) - chosen
     slot_index = jnp.arange(slot_count, dtype=jnp.int32)
-    placement_map = (
-        (chosen[:, :, None] == 1) & (rank[:, :, None] == slot_index[None, None, :])
+    every_expert = jnp.arange(expert_count, dtype=jnp.int32)
+    hits_all = expert_ids[:, :, None] == every_expert[None, None, :]
+    chosen_all = jnp.sum(hits_all.astype(jnp.int32), axis=1)
+    weight_all = jnp.sum(jnp.where(hits_all, weights[:, :, None], 0.0), axis=1)
+    rank_all = jnp.cumsum(chosen_all, axis=0) - chosen_all
+    placed_all = (chosen_all[:, :, None] == 1) & (rank_all[:, :, None] == slot_index[None, None, :])
+    outgoing = jnp.einsum(
+        "tes,tc->esc",
+        placed_all.astype(jnp.bfloat16),
+        normed_share,
+        preferred_element_type=jnp.float32,
     ).astype(jnp.bfloat16)
-    outgoing = jnp.einsum(
-        "tps,td->psd", placement_map, normed, preferred_element_type=jnp.float32
-    ).astype(jnp.bfloat16)
-    incoming = lax.all_to_all(outgoing, "seq", split_axis=0, concat_axis=0, tiled=True)
+    gathered = lax.all_to_all(outgoing, ("seq", "head"), split_axis=0, concat_axis=0, tiled=True)
+    incoming = (
+        gathered.reshape(peer_count, column_count, slot_count, share_width)
+        .transpose(0, 2, 1, 3)
+        .reshape(peer_count, slot_count, model_width)
+    )
     gate_e = jnp.einsum("psd,dh->psh", incoming, w_gate[0], preferred_element_type=jnp.float32)
     up_e = jnp.einsum("psd,dh->psh", incoming, w_up[0], preferred_element_type=jnp.float32)
     hidden = (jax.nn.silu(gate_e) * up_e).astype(jnp.bfloat16)
@@ -225,16 +233,7 @@
     sliced = result.reshape(peer_count, slot_count, column_count, share_width)
     sliced = sliced.transpose(0, 2, 1, 3).reshape(expert_count, slot_count, share_width)
     returned = lax.all_to_all(sliced, ("seq", "head"), split_axis=0, concat_axis=0, tiled=True)
-    every_expert = jnp.arange(expert_count, dtype=jnp.int32)
-    hits_all = expert_ids[:, :, None] == every_expert[None, None, :]
-    chosen_all = jnp.sum(hits_all.astype(jnp.int32), axis=1)
-    weight_all = jnp.sum(jnp.where(hits_all, weights[:, :, None], 0.0), axis=1)
-    rank_all = jnp.cumsum(chosen_all, axis=0) - chosen_all
-    combine_all = jnp.where(
-        (chosen_all[:, :, None] == 1) & (rank_all[:, :, None] == slot_index[None, None, :]),
-        weight_all[:, :, None],
-        0.0,
-    ).astype(jnp.bfloat16)
+    combine_all = jnp.where(placed_all, weight_all[:, :, None], 0.0).astype(jnp.bfloat16)
     moe_share = jnp.einsum(
         "tes,esc->tc", combine_all, returned, preferred_element_type=jnp.float32
     )

time: 324 us -> 326 us (level)
  blocking collectives: 72.9 us -> 81.4 us
  waiting for transfers between devices: 105 us -> 99.8 us
  starting transfers between devices: 95.3 us -> 90.2 us
  matrix products: 27.3 us -> 30.6 us
    all_to_all x1, blocking collectives: 72.9 us -> 81.4 us  [on_device(): lax.all_to_all(outgoing, ('seq', 'head'), split_axis=0, concat_axis=0, ti...]
    all_to_all x1, waiting for transfers between devices: 9.06 us -> 3.56 us  [on_device(): lax.all_to_all(jnp.broadcast_to(square_part[None], (column_total, length)...]
    all_to_all x1, starting transfers between devices: 16 us -> 11.4 us  [on_device(): lax.all_to_all(sliced, ('seq', 'head'), split_axis=0, concat_axis=0, tile...]
where the time goes in v7:
time: 326 us; the launch traced here: 323 us
  waiting for transfers between devices  99.8 us (31%)
  starting transfers between devices  90.2 us (28%)
  blocking collectives  81.4 us (25%)
  matrix products  30.6 us (9%)
  local copies, waits for them, and re-layouts  15.2 us (5%)
  other arithmetic  4.63 us (1%)
    all_to_all x1, blocking collectives, on_device(): lax.all_to_all(outgoing, ('seq', 'head'), split_axis=0, concat_axis=0, ti...  81.4 us
    all_to_all x1, waiting for transfers between devices, on_device(): lax.all_to_all(sliced, ('seq', 'head'), split_axis=0, concat_axis=0, tile...  72.9 us
    ppermute x7, starting transfers between devices, on_device(): going_down = lax.ppermute(going_down, 'seq', backward_pairs)  43.7 us
    ppermute x8, starting transfers between devices, on_device(): going_up = lax.ppermute(going_up, 'seq', forward_pairs)  18.3 us
    ppermute x8, waiting for transfers between devices, on_device(): going_up = lax.ppermute(going_up, 'seq', forward_pairs)  14.1 us
    all_to_all x1, starting transfers between devices, on_device(): lax.all_to_all(attn_pieces.transpose(1, 0, 2), 'head', split_axis=0, conc...  12.8 us
    all_to_all x1, starting transfers between devices, on_device(): lax.all_to_all(sliced, ('seq', 'head'), split_axis=0, concat_axis=0, tile...  11.4 us
    all_to_all x1, waiting for transfers between devices, on_device(): lax.all_to_all(attn_pieces.transpose(1, 0, 2), 'head', split_axis=0, conc...  9.24 us
  transfers between devices with their start and end apart: 18, of which 10 were waited for; matrix products, arithmetic and copies ran while one was open for 4% of the time, Pallas kernels for 0%

profile of v7, /device:TPU:1, one launch (start us, length us, event | category | flops | bytes accessed | tf_op | source)
XLA Modules:
  0.0 322.8 jit_solution(5345206905424033773)
XLA Ops:
  12.0 4.8 %collective-permute-start = (bf16[8,128,128]{2,1,0:T(8,128)(2,1)}, bf16[8,128,128]{2,1,0:T(8,128)(2,1)S(1)}, u32[]{:S(2)}, u32[]{:S(2)}) collective-permute-start(bf16[8,128,128]{2,1,0:T(8,128)(2,1)} %pad_maximum_fusion), channel_id=1, source_target_pairs={{0,8},{8,16},{16,24},{24,32},{32,40},{40,48},{48,56},{56,64},{64,7... | collective-permute-start | bytes 786440 | tf_op jit(solution)/shard_map/ppermute | solution.py:148
  16.8 15.9 %collective-permute-start.8 = (bf16[8,128,128]{2,1,0:T(8,128)(2,1)}, bf16[8,128,128]{2,1,0:T(8,128)(2,1)}, u32[]{:S(2)}, u32[]{:S(2)}) collective-permute-start(bf16[8,128,128]{2,1,0:T(8,128)(2,1)} %pad_maximum_fusion), channel_id=1, source_target_pairs={{0,120},{8,0},{16,8},{24,16},{32,24},{40,32},{48,40},{56,48},{64,5... | collective-permute-start | bytes 786440 | tf_op jit(solution)/shard_map/ppermute | solution.py:159
  33.3 1.4 convolution_multiply_fusion.1
  34.7 2.3 collective-permute-done
  37.0 1.9 collective-permute-start.1
  40.9 4.6 %collective-permute-start.9 = (bf16[8,128,128]{2,1,0:T(8,128)(2,1)}, bf16[8,128,128]{2,1,0:T(8,128)(2,1)S(1)}, u32[]{:S(2)}, u32[]{:S(2)}) collective-permute-start(bf16[8,128,128]{2,1,0:T(8,128)(2,1)} %collective-permute-done.8), channel_id=1, source_target_pairs={{0,120},{8,0},{16,8},{24,16},{32,24},{40,32},{48,40},{56,48},{64,5... | collective-permute-start | bytes 786440 | tf_op jit(solution)/shard_map/ppermute | solution.py:159
  47.9 1.9 collective-permute-start.2
  50.3 4.8 %collective-permute-start.10 = (bf16[8,128,128]{2,1,0:T(8,128)(2,1)S(1)}, bf16[8,128,128]{2,1,0:T(8,128)(2,1)S(1)}, u32[]{:S(2)}, u32[]{:S(2)}) collective-permute-start(bf16[8,128,128]{2,1,0:T(8,128)(2,1)S(1)} %collective-permute-done.9), channel_id=1, source_target_pairs={{0,120},{8,0},{16,8},{24,16},{32,24},{40,32},{48,40},{56,48},{64,5... | collective-permute-start | bytes 786440 | tf_op jit(solution)/shard_map/ppermute | solution.py:159
  55.4 1.7 collective-permute-done.2
  57.1 1.9 collective-permute-start.3
  59.6 4.6 %collective-permute-start.11 = (bf16[8,128,128]{2,1,0:T(8,128)(2,1)S(1)}, bf16[8,128,128]{2,1,0:T(8,128)(2,1)S(1)}, u32[]{:S(2)}, u32[]{:S(2)}) collective-permute-start(bf16[8,128,128]{2,1,0:T(8,128)(2,1)S(1)} %collective-permute-done.10), channel_id=1, source_target_pairs={{0,120},{8,0},{16,8},{24,16},{32,24},{40,32},{48,40},{56,48},{64,5... | collective-permute-start | bytes 786440 | tf_op jit(solution)/shard_map/ppermute | solution.py:159
  65.4 1.9 collective-permute-start.4
  68.0 4.8 %collective-permute-start.12 = (bf16[8,128,128]{2,1,0:T(8,128)(2,1)S(1)}, bf16[8,128,128]{2,1,0:T(8,128)(2,1)S(1)}, u32[]{:S(2)}, u32[]{:S(2)}) collective-permute-start(bf16[8,128,128]{2,1,0:T(8,128)(2,1)S(1)} %collective-permute-done.11), channel_id=1, source_target_pairs={{0,120},{8,0},{16,8},{24,16},{32,24},{40,32},{48,40},{56,48},{64,5... | collective-permute-start | bytes 786440 | tf_op jit(solution)/shard_map/ppermute | solution.py:159
  73.8 1.9 collective-permute-start.5
  76.3 4.6 %collective-permute-start.13 = (bf16[8,128,128]{2,1,0:T(8,128)(2,1)S(1)}, bf16[8,128,128]{2,1,0:T(8,128)(2,1)S(1)}, u32[]{:S(2)}, u32[]{:S(2)}) collective-permute-start(bf16[8,128,128]{2,1,0:T(8,128)(2,1)S(1)} %collective-permute-done.12), channel_id=1, source_target_pairs={{0,120},{8,0},{16,8},{24,16},{32,24},{40,32},{48,40},{56,48},{64,5... | collective-permute-start | bytes 786440 | tf_op jit(solution)/shard_map/ppermute | solution.py:159
  82.2 1.9 collective-permute-start.6
  84.7 4.6 %collective-permute-start.14 = (bf16[8,128,128]{2,1,0:T(8,128)(2,1)S(1)}, bf16[8,128,128]{2,1,0:T(8,128)(2,1)S(1)}, u32[]{:S(2)}, u32[]{:S(2)}) collective-permute-start(bf16[8,128,128]{2,1,0:T(8,128)(2,1)S(1)} %collective-permute-done.13), channel_id=1, source_target_pairs={{0,120},{8,0},{16,8},{24,16},{32,24},{40,32},{48,40},{56,48},{64,5... | collective-permute-start | bytes 786440 | tf_op jit(solution)/shard_map/ppermute | solution.py:159
  90.6 1.9 collective-permute-start.7
  93.5 6.7 %collective-permute-done.7 = bf16[8,128,128]{2,1,0:T(8,128)(2,1)S(1)} collective-permute-done((bf16[8,128,128]{2,1,0:T(8,128)(2,1)S(1)}, bf16[8,128,128]{2,1,0:T(8,128)(2,1)S(1)}, u32[]{:S(2)}, u32[]{:S(2)}) %collective-permute-start.7) | collective-permute-done | bytes 262176 | tf_op jit(solution)/shard_map/ppermute | solution.py:148
  104.3 12.8 %all-to-all-start = ((bf16[8,128,256]{2,1,0:T(8,128)(2,1)}), bf16[8,128,256]{2,1,0:T(8,128)(2,1)S(1)}, u32[]{:S(2)}, u32[]{:S(2)}) async-start(bf16[8,128,256]{2,1,0:T(8,128)(2,1)} %bitcast.163), calls=%async_computation | async-start | bytes 1048576 | tf_op jit(solution)/shard_map/all_to_all | solution.py:180
  117.3 9.2 %all-to-all-done = bf16[8,128,256]{2,1,0:T(8,128)(2,1)S(1)} async-done(((bf16[8,128,256]{2,1,0:T(8,128)(2,1)}), bf16[8,128,256]{2,1,0:T(8,128)(2,1)S(1)}, u32[]{:S(2)}, u32[]{:S(2)}) %all-to-all-start) | async-done | bytes 524320 | tf_op jit(solution)/shard_map/all_to_all | solution.py:180
  128.2 4.1 %all-to-all-start.1 = ((f32[8,1,128]{2,1,0:T(1,128)}), f32[8,1,128]{2,1,0:T(1,128)S(1)}, u32[]{:S(2)}, u32[]{:S(2)}) async-start(f32[8,1,128]{2,1,0:T(1,128)} %broadcast_in_dim.51), calls=%async_computation.1 | async-start | bytes 8192 | tf_op jit(solution)/shard_map/all_to_all | solution.py:189
  133.3 3.6 %all-to-all-done.1 = f32[8,1,128]{2,1,0:T(1,128)S(1)} async-done(((f32[8,1,128]{2,1,0:T(1,128)}), f32[8,1,128]{2,1,0:T(1,128)S(1)}, u32[]{:S(2)}, u32[]{:S(2)}) %all-to-all-start.1) | async-done | bytes 4128 | tf_op jit(solution)/shard_map/all_to_all | solution.py:189
  138.2 81.4 %all_to_all.21 = bf16[128,20,256]{2,1,0:T(8,128)(2,1)S(1)} all-to-all(bf16[128,20,256]{2,1,0:T(8,128)(2,1)S(1)} %copy.245), channel_id=1, replica_groups=mesh['dp'=8,'seq'=16,'head'=8] {'seq','head'}, dimensions={0} | all-to-all | bytes 2621440 | tf_op jit(solution)/shard_map/all_to_all | solution.py:221
  219.9 1.5 reshape.148
  221.4 4.2 %fusion.3 = f32[16,20,512]{2,1,0:T(8,128)} fusion(bf16[1,2048,512]{2,1,0:T(8,128)(2,1)} %param.29, bf16[16,20,2048]{2,0,1:T(8,128)(2,1)} %reshape.148), kind=kOutput, calls=%fused_computation.5 | convolution fusion | flops 671088640 | bytes 4063232 | tf_op jit(solution)/shard_map/psd,dh->psh/dot_general | solution.py:227
  225.6 5.2 %convolution_convert_fusion = bf16[16,20,2048]{2,1,0:T(8,128)(2,1)} fusion(bf16[1,512,2048]{2,1,0:T(8,128)(2,1)S(1)} %copy-done, bf16[1,2048,512]{2,1,0:T(8,128)(2,1)} %param.30, bf16[16,20,2048]{2,0,1:T(8,128)(2,1)S(1)} %copy-done.2, f32[16,20,512]{2,1,0:T(8,128)} %fusion.3), kind=kOutput, calls=%fused_computation | convolution fusion | flops 1343815680 | bytes 7471104 | tf_op jit(solution)/shard_map/psh,hd->psd/dot_general | solution.py:230
  230.8 2.6 reshape.163
  233.6 1.9 copy.250
  235.5 11.4 %all-to-all-start.3 = ((bf16[128,20,256]{2,1,0:T(8,128)(2,1)}), bf16[128,20,256]{2,1,0:T(8,128)(2,1)}, u32[]{:S(2)}, u32[]{:S(2)}) async-start(bf16[128,20,256]{2,1,0:T(8,128)(2,1)} %copy.250), calls=%async_computation.3 | async-start | bytes 3145728 | tf_op jit(solution)/shard_map/all_to_all | solution.py:235
  247.4 72.9 %all-to-all-done.3 = bf16[128,20,256]{2,1,0:T(8,128)(2,1)} async-done(((bf16[128,20,256]{2,1,0:T(8,128)(2,1)}), bf16[128,20,256]{2,1,0:T(8,128)(2,1)}, u32[]{:S(2)}, u32[]{:S(2)}) %all-to-all-start.3) | async-done | bytes 1310752 | tf_op jit(solution)/shard_map/all_to_all | solution.py:235
  320.3 2.6 fusion.41
  (155 shorter events, 34.5 us)
Async XLA Ops:
  0.0 225.6 %copy-start = (bf16[1,512,2048]{2,1,0:T(8,128)(2,1)S(1)}, bf16[1,512,2048]{2,1,0:T(8,128)(2,1)}, u32[]{:S(2)}) copy-start(bf16[1,512,2048]{2,1,0:T(8,128)(2,1)} %param.31) | copy-start | bytes 6291460
  0.0 2.7 copy-start.11
  2.6 6.0 %copy-start.6 = (f32[128,4]{0,1:T(4,128)}, f32[128,4]{0,1:T(4,128)S(1)}, u32[]{:S(2)}) copy-start(f32[128,4]{0,1:T(4,128)S(1)} %copy.221) | copy-start | bytes 6148
  7.2 1.5 copy-start.5
  7.5 1.7 copy-start.13
  9.4 23.3 %copy-start.7 = (bf16[128,256]{1,0:T(8,128)(2,1)S(1)}, bf16[128,256]{1,0:T(8,128)(2,1)}, u32[]{:S(2)}) copy-start(bf16[128,256]{1,0:T(8,128)(2,1)} %param.17) | copy-start | bytes 196612
  12.0 25.0 %collective-permute-start = (bf16[8,128,128]{2,1,0:T(8,128)(2,1)}, bf16[8,128,128]{2,1,0:T(8,128)(2,1)S(1)}, u32[]{:S(2)}, u32[]{:S(2)}) collective-permute-start(bf16[8,128,128]{2,1,0:T(8,128)(2,1)} %pad_maximum_fusion), channel_id=1, source_target_pairs={{0,8},{8,16},{16,24},{24,32},{32,40},{40,48},{48,56},{56,64},{64,7... | collective-permute-start | bytes 786440 | tf_op jit(solution)/shard_map/ppermute | solution.py:148
  16.8 24.1 %collective-permute-start.8 = (bf16[8,128,128]{2,1,0:T(8,128)(2,1)}, bf16[8,128,128]{2,1,0:T(8,128)(2,1)}, u32[]{:S(2)}, u32[]{:S(2)}) collective-permute-start(bf16[8,128,128]{2,1,0:T(8,128)(2,1)} %pad_maximum_fusion), channel_id=1, source_target_pairs={{0,120},{8,0},{16,8},{24,16},{32,24},{40,32},{48,40},{56,48},{64,5... | collective-permute-start | bytes 786440 | tf_op jit(solution)/shard_map/ppermute | solution.py:159
  32.8 7.3 %copy-start.4 = (bf16[128,512]{1,0:T(8,128)(2,1)S(1)}, bf16[128,512]{1,0:T(8,128)(2,1)}, u32[]{:S(2)}) copy-start(bf16[128,512]{1,0:T(8,128)(2,1)} %param.20) | copy-start | bytes 393220
  37.0 9.9 %collective-permute-start.1 = (bf16[8,128,128]{2,1,0:T(8,128)(2,1)S(1)}, bf16[8,128,128]{2,1,0:T(8,128)(2,1)}, u32[]{:S(2)}, u32[]{:S(2)}) collective-permute-start(bf16[8,128,128]{2,1,0:T(8,128)(2,1)S(1)} %collective-permute-done), channel_id=1, source_target_pairs={{0,8},{8,16},{16,24},{24,32},{32,40},{40,48},{48,56},{56,64},{64,7... | collective-permute-start | bytes 786440 | tf_op jit(solution)/shard_map/ppermute | solution.py:148
  40.9 9.4 %collective-permute-start.9 = (bf16[8,128,128]{2,1,0:T(8,128)(2,1)}, bf16[8,128,128]{2,1,0:T(8,128)(2,1)S(1)}, u32[]{:S(2)}, u32[]{:S(2)}) collective-permute-start(bf16[8,128,128]{2,1,0:T(8,128)(2,1)} %collective-permute-done.8), channel_id=1, source_target_pairs={{0,120},{8,0},{16,8},{24,16},{32,24},{40,32},{48,40},{56,48},{64,5... | collective-permute-start | bytes 786440 | tf_op jit(solution)/shard_map/ppermute | solution.py:159
  47.9 9.1 %collective-permute-start.2 = (bf16[8,128,128]{2,1,0:T(8,128)(2,1)}, bf16[8,128,128]{2,1,0:T(8,128)(2,1)S(1)}, u32[]{:S(2)}, u32[]{:S(2)}) collective-permute-start(bf16[8,128,128]{2,1,0:T(8,128)(2,1)} %collective-permute-done.1), channel_id=1, source_target_pairs={{0,8},{8,16},{16,24},{24,32},{32,40},{40,48},{48,56},{56,64},{64,7... | collective-permute-start | bytes 786440 | tf_op jit(solution)/shard_map/ppermute | solution.py:148
  50.3 9.3 %collective-permute-start.10 = (bf16[8,128,128]{2,1,0:T(8,128)(2,1)S(1)}, bf16[8,128,128]{2,1,0:T(8,128)(2,1)S(1)}, u32[]{:S(2)}, u32[]{:S(2)}) collective-permute-start(bf16[8,128,128]{2,1,0:T(8,128)(2,1)S(1)} %collective-permute-done.9), channel_id=1, source_target_pairs={{0,120},{8,0},{16,8},{24,16},{32,24},{40,32},{48,40},{56,48},{64,5... | collective-permute-start | bytes 786440 | tf_op jit(solution)/shard_map/ppermute | solution.py:159
  57.1 8.3 %collective-permute-start.3 = (bf16[8,128,128]{2,1,0:T(8,128)(2,1)S(1)}, bf16[8,128,128]{2,1,0:T(8,128)(2,1)S(1)}, u32[]{:S(2)}, u32[]{:S(2)}) collective-permute-start(bf16[8,128,128]{2,1,0:T(8,128)(2,1)S(1)} %collective-permute-done.2), channel_id=1, source_target_pairs={{0,8},{8,16},{16,24},{24,32},{32,40},{40,48},{48,56},{56,64},{64,7... | collective-permute-start | bytes 786440 | tf_op jit(solution)/shard_map/ppermute | solution.py:148
  59.6 8.4 %collective-permute-start.11 = (bf16[8,128,128]{2,1,0:T(8,128)(2,1)S(1)}, bf16[8,128,128]{2,1,0:T(8,128)(2,1)S(1)}, u32[]{:S(2)}, u32[]{:S(2)}) collective-permute-start(bf16[8,128,128]{2,1,0:T(8,128)(2,1)S(1)} %collective-permute-done.10), channel_id=1, source_target_pairs={{0,120},{8,0},{16,8},{24,16},{32,24},{40,32},{48,40},{56,48},{64,5... | collective-permute-start | bytes 786440 | tf_op jit(solution)/shard_map/ppermute | solution.py:159
  65.4 8.3 %collective-permute-start.4 = (bf16[8,128,128]{2,1,0:T(8,128)(2,1)S(1)}, bf16[8,128,128]{2,1,0:T(8,128)(2,1)S(1)}, u32[]{:S(2)}, u32[]{:S(2)}) collective-permute-start(bf16[8,128,128]{2,1,0:T(8,128)(2,1)S(1)} %collective-permute-done.3), channel_id=1, source_target_pairs={{0,8},{8,16},{16,24},{24,32},{32,40},{40,48},{48,56},{56,64},{64,7... | collective-permute-start | bytes 786440 | tf_op jit(solution)/shard_map/ppermute | solution.py:148
  68.0 8.3 %collective-permute-start.12 = (bf16[8,128,128]{2,1,0:T(8,128)(2,1)S(1)}, bf16[8,128,128]{2,1,0:T(8,128)(2,1)S(1)}, u32[]{:S(2)}, u32[]{:S(2)}) collective-permute-start(bf16[8,128,128]{2,1,0:T(8,128)(2,1)S(1)} %collective-permute-done.11), channel_id=1, source_target_pairs={{0,120},{8,0},{16,8},{24,16},{32,24},{40,32},{48,40},{56,48},{64,5... | collective-permute-start | bytes 786440 | tf_op jit(solution)/shard_map/ppermute | solution.py:159
  73.8 8.3 %collective-permute-start.5 = (bf16[8,128,128]{2,1,0:T(8,128)(2,1)S(1)}, bf16[8,128,128]{2,1,0:T(8,128)(2,1)S(1)}, u32[]{:S(2)}, u32[]{:S(2)}) collective-permute-start(bf16[8,128,128]{2,1,0:T(8,128)(2,1)S(1)} %collective-permute-done.4), channel_id=1, source_target_pairs={{0,8},{8,16},{16,24},{24,32},{32,40},{40,48},{48,56},{56,64},{64,7... | collective-permute-start | bytes 786440 | tf_op jit(solution)/shard_map/ppermute | solution.py:148
  76.3 8.4 %collective-permute-start.13 = (bf16[8,128,128]{2,1,0:T(8,128)(2,1)S(1)}, bf16[8,128,128]{2,1,0:T(8,128)(2,1)S(1)}, u32[]{:S(2)}, u32[]{:S(2)}) collective-permute-start(bf16[8,128,128]{2,1,0:T(8,128)(2,1)S(1)} %collective-permute-done.12), channel_id=1, source_target_pairs={{0,120},{8,0},{16,8},{24,16},{32,24},{40,32},{48,40},{56,48},{64,5... | collective-permute-start | bytes 786440 | tf_op jit(solution)/shard_map/ppermute | solution.py:159
  82.2 8.4 %collective-permute-start.6 = (bf16[8,128,128]{2,1,0:T(8,128)(2,1)S(1)}, bf16[8,128,128]{2,1,0:T(8,128)(2,1)S(1)}, u32[]{:S(2)}, u32[]{:S(2)}) collective-permute-start(bf16[8,128,128]{2,1,0:T(8,128)(2,1)S(1)} %collective-permute-done.5), channel_id=1, source_target_pairs={{0,8},{8,16},{16,24},{24,32},{32,40},{40,48},{48,56},{56,64},{64,7... | collective-permute-start | bytes 786440 | tf_op jit(solution)/shard_map/ppermute | solution.py:148
  84.7 8.5 %collective-permute-start.14 = (bf16[8,128,128]{2,1,0:T(8,128)(2,1)S(1)}, bf16[8,128,128]{2,1,0:T(8,128)(2,1)S(1)}, u32[]{:S(2)}, u32[]{:S(2)}) collective-permute-start(bf16[8,128,128]{2,1,0:T(8,128)(2,1)S(1)} %collective-permute-done.13), channel_id=1, source_target_pairs={{0,120},{8,0},{16,8},{24,16},{32,24},{40,32},{48,40},{56,48},{64,5... | collective-permute-start | bytes 786440 | tf_op jit(solution)/shard_map/ppermute | solution.py:159
  90.6 9.5 %collective-permute-start.7 = (bf16[8,128,128]{2,1,0:T(8,128)(2,1)S(1)}, bf16[8,128,128]{2,1,0:T(8,128)(2,1)S(1)}, u32[]{:S(2)}, u32[]{:S(2)}) collective-permute-start(bf16[8,128,128]{2,1,0:T(8,128)(2,1)S(1)} %collective-permute-done.6), channel_id=1, source_target_pairs={{0,8},{8,16},{16,24},{24,32},{32,40},{40,48},{48,56},{56,64},{64,7... | collective-permute-start | bytes 786440 | tf_op jit(solution)/shard_map/ppermute | solution.py:148
  100.8 1.7 copy-start.3
  100.8 1.7 copy-start.15
  101.3 1.6 copy-start.1
  103.4 13.7 %copy-start.9 = (s32[128,10]{0,1:T(8,128)S(1)}, s32[128,10]{0,1:T(8,128)}, u32[]{:S(2)}) copy-start(s32[128,10]{0,1:T(8,128)} %param.27) | copy-start | bytes 15364
  104.3 22.3 %all-to-all-start = ((bf16[8,128,256]{2,1,0:T(8,128)(2,1)}), bf16[8,128,256]{2,1,0:T(8,128)(2,1)S(1)}, u32[]{:S(2)}, u32[]{:S(2)}) async-start(bf16[8,128,256]{2,1,0:T(8,128)(2,1)} %bitcast.163), calls=%async_computation | async-start | bytes 1048576 | tf_op jit(solution)/shard_map/all_to_all | solution.py:180
  128.2 8.6 %all-to-all-start.1 = ((f32[8,1,128]{2,1,0:T(1,128)}), f32[8,1,128]{2,1,0:T(1,128)S(1)}, u32[]{:S(2)}, u32[]{:S(2)}) async-start(f32[8,1,128]{2,1,0:T(1,128)} %broadcast_in_dim.51), calls=%async_computation.1 | async-start | bytes 8192 | tf_op jit(solution)/shard_map/all_to_all | solution.py:189
  221.4 4.2 %copy-start.2 = (bf16[16,20,2048]{2,0,1:T(8,128)(2,1)S(1)}, bf16[16,20,2048]{2,0,1:T(8,128)(2,1)}, u32[]{:S(2)}) copy-start(bf16[16,20,2048]{2,0,1:T(8,128)(2,1)} %reshape.148) | copy-start | bytes 3932164
  235.5 11.4 %copy-start.8 = (f32[128,10]{0,1:T(8,128)S(1)}, f32[128,10]{0,1:T(8,128)}, u32[]{:S(2)}) copy-start(f32[128,10]{0,1:T(8,128)} %param.28) | copy-start | bytes 15364
  235.5 11.5 %copy-start.10 = (s32[128,10]{0,1:T(8,128)S(1)}, s32[128,10]{0,1:T(8,128)}, u32[]{:S(2)}) copy-start(s32[128,10]{0,1:T(8,128)} %param.27) | copy-start | bytes 15364
  235.5 84.8 %all-to-all-start.3 = ((bf16[128,20,256]{2,1,0:T(8,128)(2,1)}), bf16[128,20,256]{2,1,0:T(8,128)(2,1)}, u32[]{:S(2)}, u32[]{:S(2)}) async-start(bf16[128,20,256]{2,1,0:T(8,128)(2,1)} %copy.250), calls=%async_computation.3 | async-start | bytes 3145728 | tf_op jit(solution)/shard_map/all_to_all | solution.py:235
  (2 other events, 2.2 us)

commit v8 on v6

--- a/solution.py
+++ b/solution.py
@@ -219,11 +219,11 @@
     gate_e = jnp.einsum("psd,dh->psh", incoming, w_gate[0], preferred_element_type=jnp.float32)
     up_e = jnp.einsum("psd,dh->psh", incoming, w_up[0], preferred_element_type=jnp.float32)
     hidden = (jax.nn.silu(gate_e) * up_e).astype(jnp.bfloat16)
-    result = jnp.einsum(
-        "psh,hd->psd", hidden, w_down[0], preferred_element_type=jnp.float32
-    ).astype(jnp.bfloat16)
-    sliced = result.reshape(peer_count, slot_count, column_count, share_width)
-    sliced = sliced.transpose(0, 2, 1, 3).reshape(expert_count, slot_count, share_width)
+    down_pieces = w_down[0].reshape(w_down.shape[1], column_count, share_width)
+    sliced = jnp.einsum(
+        "psh,hcd->pcsd", hidden, down_pieces, preferred_element_type=jnp.float32
+    ).astype(jnp.bfloat16)
+    sliced = sliced.reshape(expert_count, slot_count, share_width)
     returned = lax.all_to_all(sliced, ("seq", "head"), split_axis=0, concat_axis=0, tiled=True)
     every_expert = jnp.arange(expert_count, dtype=jnp.int32)
     hits_all = expert_ids[:, :, None] == every_expert[None, None, :]

time: 324 us -> 324 us (level)
  blocking collectives: 72.9 us -> 0 us
  waiting for transfers between devices: 105 us -> 170 us
  starting transfers between devices: 95.3 us -> 98.9 us
  matrix products: 27.3 us -> 30.7 us
    all_to_all x1 -> x0, blocking collectives: 72.9 us -> none  [on_device(): lax.all_to_all(outgoing, 'seq', split_axis=0, concat_axis=0, tiled=True)]
    all_to_all x0 -> x1, waiting for transfers between devices: none -> 65.4 us  [on_device(): lax.all_to_all(outgoing, 'seq', split_axis=0, concat_axis=0, tiled=True)]
    all_to_all x0 -> x1, starting transfers between devices: none -> 5.31 us  [on_device(): lax.all_to_all(outgoing, 'seq', split_axis=0, concat_axis=0, tiled=True)]
    reshape x3 -> x0, local copies, waits for them, and re-layouts: 4.64 us -> none  [the longest x2 2.73 us: on_device(): sliced = result.reshape(peer_count, slot_count, column_count, share_width)]
  transfers between devices with their start and end apart: 18 -> 19, of which waited for: 10 -> 11; matrix products, arithmetic and copies ran while one was open for 4% -> 5% of each run, Pallas kernels for 0% -> 0%
where the time goes in v8:
time: 324 us; the launch traced here: 321 us
  waiting for transfers between devices  170 us (52%)
  starting transfers between devices  98.9 us (31%)
  matrix products  30.7 us (9%)
  local copies, waits for them, and re-layouts  14.5 us (4%)
  other arithmetic  5.41 us (2%)
    all_to_all x1, waiting for transfers between devices, on_device(): lax.all_to_all(sliced, ('seq', 'head'), split_axis=0, concat_axis=0, tile...  72.5 us
    all_to_all x1, waiting for transfers between devices, on_device(): lax.all_to_all(outgoing, 'seq', split_axis=0, concat_axis=0, tiled=True)  65.4 us
    ppermute x7, starting transfers between devices, on_device(): going_down = lax.ppermute(going_down, 'seq', backward_pairs)  43.7 us
    ppermute x8, starting transfers between devices, on_device(): going_up = lax.ppermute(going_up, 'seq', forward_pairs)  18.2 us
    all_to_all x1, starting transfers between devices, on_device(): lax.all_to_all(sliced, ('seq', 'head'), split_axis=0, concat_axis=0, tile...  14.7 us
    ppermute x8, waiting for transfers between devices, on_device(): going_up = lax.ppermute(going_up, 'seq', forward_pairs)  14 us
    all_to_all x1, starting transfers between devices, on_device(): lax.all_to_all(attn_pieces.transpose(1, 0, 2), 'head', split_axis=0, conc...  12.7 us
    all_to_all x1, waiting for transfers between devices, on_device(): lax.all_to_all(attn_pieces.transpose(1, 0, 2), 'head', split_axis=0, conc...  9.48 us
  transfers between devices with their start and end apart: 19, of which 11 were waited for; matrix products, arithmetic and copies ran while one was open for 5% of the time, Pallas kernels for 0%

profile of v8, /device:TPU:1, one launch (start us, length us, event | category | flops | bytes accessed | tf_op | source)
XLA Modules:
  0.0 320.8 jit_solution(11575718596932204821)
XLA Ops:
  15.0 4.8 %collective-permute-start = (bf16[8,128,128]{2,1,0:T(8,128)(2,1)}, bf16[8,128,128]{2,1,0:T(8,128)(2,1)S(1)}, u32[]{:S(2)}, u32[]{:S(2)}) collective-permute-start(bf16[8,128,128]{2,1,0:T(8,128)(2,1)} %pad_maximum_fusion), channel_id=1, source_target_pairs={{0,8},{8,16},{16,24},{24,32},{32,40},{40,48},{48,56},{56,64},{64,7... | collective-permute-start | bytes 786440 | tf_op jit(solution)/shard_map/ppermute | solution.py:148
  19.9 15.9 %collective-permute-start.8 = (bf16[8,128,128]{2,1,0:T(8,128)(2,1)}, bf16[8,128,128]{2,1,0:T(8,128)(2,1)}, u32[]{:S(2)}, u32[]{:S(2)}) collective-permute-start(bf16[8,128,128]{2,1,0:T(8,128)(2,1)} %pad_maximum_fusion), channel_id=1, source_target_pairs={{0,120},{8,0},{16,8},{24,16},{32,24},{40,32},{48,40},{56,48},{64,5... | collective-permute-start | bytes 786440 | tf_op jit(solution)/shard_map/ppermute | solution.py:159
  37.8 2.2 collective-permute-done
  40.0 1.9 collective-permute-start.1
  42.4 1.7 copy.239
  44.2 4.6 %collective-permute-start.9 = (bf16[8,128,128]{2,1,0:T(8,128)(2,1)}, bf16[8,128,128]{2,1,0:T(8,128)(2,1)S(1)}, u32[]{:S(2)}, u32[]{:S(2)}) collective-permute-start(bf16[8,128,128]{2,1,0:T(8,128)(2,1)} %collective-permute-done.8), channel_id=1, source_target_pairs={{0,120},{8,0},{16,8},{24,16},{32,24},{40,32},{48,40},{56,48},{64,5... | collective-permute-start | bytes 786440 | tf_op jit(solution)/shard_map/ppermute | solution.py:159
  51.2 1.9 collective-permute-start.2
  53.6 4.7 %collective-permute-start.10 = (bf16[8,128,128]{2,1,0:T(8,128)(2,1)S(1)}, bf16[8,128,128]{2,1,0:T(8,128)(2,1)S(1)}, u32[]{:S(2)}, u32[]{:S(2)}) collective-permute-start(bf16[8,128,128]{2,1,0:T(8,128)(2,1)S(1)} %collective-permute-done.9), channel_id=1, source_target_pairs={{0,120},{8,0},{16,8},{24,16},{32,24},{40,32},{48,40},{56,48},{64,5... | collective-permute-start | bytes 786440 | tf_op jit(solution)/shard_map/ppermute | solution.py:159
  58.6 1.9 collective-permute-done.2
  60.6 1.9 collective-permute-start.3
  63.1 4.6 %collective-permute-start.11 = (bf16[8,128,128]{2,1,0:T(8,128)(2,1)S(1)}, bf16[8,128,128]{2,1,0:T(8,128)(2,1)S(1)}, u32[]{:S(2)}, u32[]{:S(2)}) collective-permute-start(bf16[8,128,128]{2,1,0:T(8,128)(2,1)S(1)} %collective-permute-done.10), channel_id=1, source_target_pairs={{0,120},{8,0},{16,8},{24,16},{32,24},{40,32},{48,40},{56,48},{64,5... | collective-permute-start | bytes 786440 | tf_op jit(solution)/shard_map/ppermute | solution.py:159
  68.9 1.9 collective-permute-start.4
  71.5 4.8 %collective-permute-start.12 = (bf16[8,128,128]{2,1,0:T(8,128)(2,1)S(1)}, bf16[8,128,128]{2,1,0:T(8,128)(2,1)S(1)}, u32[]{:S(2)}, u32[]{:S(2)}) collective-permute-start(bf16[8,128,128]{2,1,0:T(8,128)(2,1)S(1)} %collective-permute-done.11), channel_id=1, source_target_pairs={{0,120},{8,0},{16,8},{24,16},{32,24},{40,32},{48,40},{56,48},{64,5... | collective-permute-start | bytes 786440 | tf_op jit(solution)/shard_map/ppermute | solution.py:159
  77.3 1.9 collective-permute-start.5
  79.8 4.6 %collective-permute-start.13 = (bf16[8,128,128]{2,1,0:T(8,128)(2,1)S(1)}, bf16[8,128,128]{2,1,0:T(8,128)(2,1)S(1)}, u32[]{:S(2)}, u32[]{:S(2)}) collective-permute-start(bf16[8,128,128]{2,1,0:T(8,128)(2,1)S(1)} %collective-permute-done.12), channel_id=1, source_target_pairs={{0,120},{8,0},{16,8},{24,16},{32,24},{40,32},{48,40},{56,48},{64,5... | collective-permute-start | bytes 786440 | tf_op jit(solution)/shard_map/ppermute | solution.py:159
  85.7 1.9 collective-permute-start.6
  88.2 4.6 %collective-permute-start.14 = (bf16[8,128,128]{2,1,0:T(8,128)(2,1)S(1)}, bf16[8,128,128]{2,1,0:T(8,128)(2,1)S(1)}, u32[]{:S(2)}, u32[]{:S(2)}) collective-permute-start(bf16[8,128,128]{2,1,0:T(8,128)(2,1)S(1)} %collective-permute-done.13), channel_id=1, source_target_pairs={{0,120},{8,0},{16,8},{24,16},{32,24},{40,32},{48,40},{56,48},{64,5... | collective-permute-start | bytes 786440 | tf_op jit(solution)/shard_map/ppermute | solution.py:159
  94.0 1.9 collective-permute-start.7
  96.9 6.6 %collective-permute-done.7 = bf16[8,128,128]{2,1,0:T(8,128)(2,1)S(1)} collective-permute-done((bf16[8,128,128]{2,1,0:T(8,128)(2,1)S(1)}, bf16[8,128,128]{2,1,0:T(8,128)(2,1)S(1)}, u32[]{:S(2)}, u32[]{:S(2)}) %collective-permute-start.7) | collective-permute-done | bytes 262176 | tf_op jit(solution)/shard_map/ppermute | solution.py:148
  107.3 12.7 %all-to-all-start = ((bf16[8,128,256]{2,1,0:T(8,128)(2,1)}), bf16[8,128,256]{2,1,0:T(8,128)(2,1)S(1)}, u32[]{:S(2)}, u32[]{:S(2)}) async-start(bf16[8,128,256]{2,1,0:T(8,128)(2,1)} %bitcast.174), calls=%async_computation | async-start | bytes 1048576 | tf_op jit(solution)/shard_map/all_to_all | solution.py:180
  120.0 9.5 %all-to-all-done = bf16[8,128,256]{2,1,0:T(8,128)(2,1)S(1)} async-done(((bf16[8,128,256]{2,1,0:T(8,128)(2,1)}), bf16[8,128,256]{2,1,0:T(8,128)(2,1)S(1)}, u32[]{:S(2)}, u32[]{:S(2)}) %all-to-all-start) | async-done | bytes 524320 | tf_op jit(solution)/shard_map/all_to_all | solution.py:180
  131.2 4.3 %all-to-all-start.1 = ((bf16[8,128,256]{2,1,0:T(8,128)(2,1)}), bf16[8,128,256]{2,1,0:T(8,128)(2,1)S(1)}, u32[]{:S(2)}, u32[]{:S(2)}) async-start(bf16[8,128,256]{2,1,0:T(8,128)(2,1)} %broadcast_in_dim.51), calls=%async_computation.1 | async-start | bytes 1048576 | tf_op jit(solution)/shard_map/all_to_all | solution.py:187
  135.9 9.1 %all-to-all-done.1 = bf16[8,128,256]{2,1,0:T(8,128)(2,1)S(1)} async-done(((bf16[8,128,256]{2,1,0:T(8,128)(2,1)}), bf16[8,128,256]{2,1,0:T(8,128)(2,1)S(1)}, u32[]{:S(2)}, u32[]{:S(2)}) %all-to-all-start.1) | async-done | bytes 524320 | tf_op jit(solution)/shard_map/all_to_all | solution.py:187
  145.9 1.7 convolution_convert_fusion
  147.6 5.3 %all-to-all-start.2 = ((bf16[16,20,2048]{2,1,0:T(8,128)(2,1)}), bf16[16,20,2048]{2,1,0:T(8,128)(2,1)}, u32[]{:S(2)}, u32[]{:S(2)}) async-start(bf16[16,20,2048]{2,1,0:T(8,128)(2,1)} %convolution_convert_fusion), calls=%async_computation.2 | async-start | bytes 3145728 | tf_op jit(solution)/shard_map/all_to_all | solution.py:218
  153.0 3.6 %copy.257 = bf16[64,8,8,256]{3,2,1,0:T(8,128)(2,1)} copy(bf16[64,8,8,256]{3,1,2,0:T(8,128)(2,1)} %bitcast.179) | data formatting | bytes 4194304
  156.6 65.4 %all-to-all-done.2 = bf16[16,20,2048]{2,1,0:T(8,128)(2,1)} async-done(((bf16[16,20,2048]{2,1,0:T(8,128)(2,1)}), bf16[16,20,2048]{2,1,0:T(8,128)(2,1)}, u32[]{:S(2)}, u32[]{:S(2)}) %all-to-all-start.2) | async-done | bytes 1310752 | tf_op jit(solution)/shard_map/all_to_all | solution.py:218
  221.9 3.0 fusion.4
  225.0 5.2 %fusion.7 = bf16[16,20,8,256]{3,1,2,0:T(8,128)(2,1)} fusion(bf16[512,8,256]{2,1,0:T(8,128)(2,1)} %bitcast.180, bf16[16,20,2048]{2,1,0:T(8,128)(2,1)} %all-to-all-done.2, bf16[1,2048,512]{2,1,0:T(8,128)(2,1)S(1)} %copy-done, f32[16,20,512]{2,1,0:T(8,128)S(1)} %fusion.4), kind=kOutput, calls=%fused_computation.9 | convolution fusion | flops 1343815680 | bytes 7471104 | tf_op jit(solution)/shard_map/psh,hcd->pcsd/dot_general | solution.py:223
  230.2 14.7 %all-to-all-start.3 = ((bf16[128,20,256]{2,1,0:T(8,128)(2,1)}), bf16[128,20,256]{2,1,0:T(8,128)(2,1)}, u32[]{:S(2)}, u32[]{:S(2)}) async-start(bf16[128,20,256]{2,1,0:T(8,128)(2,1)} %bitcast.182), calls=%async_computation.3 | async-start | bytes 3145728 | tf_op jit(solution)/shard_map/all_to_all | solution.py:227
  245.8 72.5 %all-to-all-done.3 = bf16[128,20,256]{2,1,0:T(8,128)(2,1)} async-done(((bf16[128,20,256]{2,1,0:T(8,128)(2,1)}), bf16[128,20,256]{2,1,0:T(8,128)(2,1)}, u32[]{:S(2)}, u32[]{:S(2)}) %all-to-all-start.3) | async-done | bytes 1310752 | tf_op jit(solution)/shard_map/all_to_all | solution.py:227
  318.3 2.6 fusion.42
  (142 shorter events, 36.2 us)
Async XLA Ops:
  0.0 225.0 %copy-start = (bf16[1,2048,512]{2,1,0:T(8,128)(2,1)S(1)}, bf16[1,2048,512]{2,1,0:T(8,128)(2,1)}, u32[]{:S(2)}) copy-start(bf16[1,2048,512]{2,1,0:T(8,128)(2,1)} %param.30) | copy-start | bytes 6291460
  7.5 2.4 copy-start.5
  15.0 25.0 %collective-permute-start = (bf16[8,128,128]{2,1,0:T(8,128)(2,1)}, bf16[8,128,128]{2,1,0:T(8,128)(2,1)S(1)}, u32[]{:S(2)}, u32[]{:S(2)}) collective-permute-start(bf16[8,128,128]{2,1,0:T(8,128)(2,1)} %pad_maximum_fusion), channel_id=1, source_target_pairs={{0,8},{8,16},{16,24},{24,32},{32,40},{40,48},{48,56},{56,64},{64,7... | collective-permute-start | bytes 786440 | tf_op jit(solution)/shard_map/ppermute | solution.py:148
  19.9 24.3 %collective-permute-start.8 = (bf16[8,128,128]{2,1,0:T(8,128)(2,1)}, bf16[8,128,128]{2,1,0:T(8,128)(2,1)}, u32[]{:S(2)}, u32[]{:S(2)}) collective-permute-start(bf16[8,128,128]{2,1,0:T(8,128)(2,1)} %pad_maximum_fusion), channel_id=1, source_target_pairs={{0,120},{8,0},{16,8},{24,16},{32,24},{40,32},{48,40},{56,48},{64,5... | collective-permute-start | bytes 786440 | tf_op jit(solution)/shard_map/ppermute | solution.py:159
  40.0 10.1 %collective-permute-start.1 = (bf16[8,128,128]{2,1,0:T(8,128)(2,1)S(1)}, bf16[8,128,128]{2,1,0:T(8,128)(2,1)}, u32[]{:S(2)}, u32[]{:S(2)}) collective-permute-start(bf16[8,128,128]{2,1,0:T(8,128)(2,1)S(1)} %collective-permute-done), channel_id=1, source_target_pairs={{0,8},{8,16},{16,24},{24,32},{32,40},{40,48},{48,56},{56,64},{64,7... | collective-permute-start | bytes 786440 | tf_op jit(solution)/shard_map/ppermute | solution.py:148
  44.2 9.4 %collective-permute-start.9 = (bf16[8,128,128]{2,1,0:T(8,128)(2,1)}, bf16[8,128,128]{2,1,0:T(8,128)(2,1)S(1)}, u32[]{:S(2)}, u32[]{:S(2)}) collective-permute-start(bf16[8,128,128]{2,1,0:T(8,128)(2,1)} %collective-permute-done.8), channel_id=1, source_target_pairs={{0,120},{8,0},{16,8},{24,16},{32,24},{40,32},{48,40},{56,48},{64,5... | collective-permute-start | bytes 786440 | tf_op jit(solution)/shard_map/ppermute | solution.py:159
  51.2 9.3 %collective-permute-start.2 = (bf16[8,128,128]{2,1,0:T(8,128)(2,1)}, bf16[8,128,128]{2,1,0:T(8,128)(2,1)S(1)}, u32[]{:S(2)}, u32[]{:S(2)}) collective-permute-start(bf16[8,128,128]{2,1,0:T(8,128)(2,1)} %collective-permute-done.1), channel_id=1, source_target_pairs={{0,8},{8,16},{16,24},{24,32},{32,40},{40,48},{48,56},{56,64},{64,7... | collective-permute-start | bytes 786440 | tf_op jit(solution)/shard_map/ppermute | solution.py:148
  53.6 9.5 %collective-permute-start.10 = (bf16[8,128,128]{2,1,0:T(8,128)(2,1)S(1)}, bf16[8,128,128]{2,1,0:T(8,128)(2,1)S(1)}, u32[]{:S(2)}, u32[]{:S(2)}) collective-permute-start(bf16[8,128,128]{2,1,0:T(8,128)(2,1)S(1)} %collective-permute-done.9), channel_id=1, source_target_pairs={{0,120},{8,0},{16,8},{24,16},{32,24},{40,32},{48,40},{56,48},{64,5... | collective-permute-start | bytes 786440 | tf_op jit(solution)/shard_map/ppermute | solution.py:159
  60.6 8.3 %collective-permute-start.3 = (bf16[8,128,128]{2,1,0:T(8,128)(2,1)S(1)}, bf16[8,128,128]{2,1,0:T(8,128)(2,1)S(1)}, u32[]{:S(2)}, u32[]{:S(2)}) collective-permute-start(bf16[8,128,128]{2,1,0:T(8,128)(2,1)S(1)} %collective-permute-done.2), channel_id=1, source_target_pairs={{0,8},{8,16},{16,24},{24,32},{32,40},{40,48},{48,56},{56,64},{64,7... | collective-permute-start | bytes 786440 | tf_op jit(solution)/shard_map/ppermute | solution.py:148
  63.1 8.4 %collective-permute-start.11 = (bf16[8,128,128]{2,1,0:T(8,128)(2,1)S(1)}, bf16[8,128,128]{2,1,0:T(8,128)(2,1)S(1)}, u32[]{:S(2)}, u32[]{:S(2)}) collective-permute-start(bf16[8,128,128]{2,1,0:T(8,128)(2,1)S(1)} %collective-permute-done.10), channel_id=1, source_target_pairs={{0,120},{8,0},{16,8},{24,16},{32,24},{40,32},{48,40},{56,48},{64,5... | collective-permute-start | bytes 786440 | tf_op jit(solution)/shard_map/ppermute | solution.py:159
  68.9 8.3 %collective-permute-start.4 = (bf16[8,128,128]{2,1,0:T(8,128)(2,1)S(1)}, bf16[8,128,128]{2,1,0:T(8,128)(2,1)S(1)}, u32[]{:S(2)}, u32[]{:S(2)}) collective-permute-start(bf16[8,128,128]{2,1,0:T(8,128)(2,1)S(1)} %collective-permute-done.3), channel_id=1, source_target_pairs={{0,8},{8,16},{16,24},{24,32},{32,40},{40,48},{48,56},{56,64},{64,7... | collective-permute-start | bytes 786440 | tf_op jit(solution)/shard_map/ppermute | solution.py:148
  71.5 8.3 %collective-permute-start.12 = (bf16[8,128,128]{2,1,0:T(8,128)(2,1)S(1)}, bf16[8,128,128]{2,1,0:T(8,128)(2,1)S(1)}, u32[]{:S(2)}, u32[]{:S(2)}) collective-permute-start(bf16[8,128,128]{2,1,0:T(8,128)(2,1)S(1)} %collective-permute-done.11), channel_id=1, source_target_pairs={{0,120},{8,0},{16,8},{24,16},{32,24},{40,32},{48,40},{56,48},{64,5... | collective-permute-start | bytes 786440 | tf_op jit(solution)/shard_map/ppermute | solution.py:159
  77.3 8.3 %collective-permute-start.5 = (bf16[8,128,128]{2,1,0:T(8,128)(2,1)S(1)}, bf16[8,128,128]{2,1,0:T(8,128)(2,1)S(1)}, u32[]{:S(2)}, u32[]{:S(2)}) collective-permute-start(bf16[8,128,128]{2,1,0:T(8,128)(2,1)S(1)} %collective-permute-done.4), channel_id=1, source_target_pairs={{0,8},{8,16},{16,24},{24,32},{32,40},{40,48},{48,56},{56,64},{64,7... | collective-permute-start | bytes 786440 | tf_op jit(solution)/shard_map/ppermute | solution.py:148
  79.8 8.4 %collective-permute-start.13 = (bf16[8,128,128]{2,1,0:T(8,128)(2,1)S(1)}, bf16[8,128,128]{2,1,0:T(8,128)(2,1)S(1)}, u32[]{:S(2)}, u32[]{:S(2)}) collective-permute-start(bf16[8,128,128]{2,1,0:T(8,128)(2,1)S(1)} %collective-permute-done.12), channel_id=1, source_target_pairs={{0,120},{8,0},{16,8},{24,16},{32,24},{40,32},{48,40},{56,48},{64,5... | collective-permute-start | bytes 786440 | tf_op jit(solution)/shard_map/ppermute | solution.py:159
  85.7 8.3 %collective-permute-start.6 = (bf16[8,128,128]{2,1,0:T(8,128)(2,1)S(1)}, bf16[8,128,128]{2,1,0:T(8,128)(2,1)S(1)}, u32[]{:S(2)}, u32[]{:S(2)}) collective-permute-start(bf16[8,128,128]{2,1,0:T(8,128)(2,1)S(1)} %collective-permute-done.5), channel_id=1, source_target_pairs={{0,8},{8,16},{16,24},{24,32},{32,40},{40,48},{48,56},{56,64},{64,7... | collective-permute-start | bytes 786440 | tf_op jit(solution)/shard_map/ppermute | solution.py:148
  88.2 8.3 %collective-permute-start.14 = (bf16[8,128,128]{2,1,0:T(8,128)(2,1)S(1)}, bf16[8,128,128]{2,1,0:T(8,128)(2,1)S(1)}, u32[]{:S(2)}, u32[]{:S(2)}) collective-permute-start(bf16[8,128,128]{2,1,0:T(8,128)(2,1)S(1)} %collective-permute-done.13), channel_id=1, source_target_pairs={{0,120},{8,0},{16,8},{24,16},{32,24},{40,32},{48,40},{56,48},{64,5... | collective-permute-start | bytes 786440 | tf_op jit(solution)/shard_map/ppermute | solution.py:159
  94.0 9.4 %collective-permute-start.7 = (bf16[8,128,128]{2,1,0:T(8,128)(2,1)S(1)}, bf16[8,128,128]{2,1,0:T(8,128)(2,1)S(1)}, u32[]{:S(2)}, u32[]{:S(2)}) collective-permute-start(bf16[8,128,128]{2,1,0:T(8,128)(2,1)S(1)} %collective-permute-done.6), channel_id=1, source_target_pairs={{0,8},{8,16},{16,24},{24,32},{32,40},{40,48},{48,56},{56,64},{64,7... | collective-permute-start | bytes 786440 | tf_op jit(solution)/shard_map/ppermute | solution.py:148
  104.1 1.7 copy-start.2
  104.1 1.7 copy-start.7
  104.1 1.9 copy-start.1
  106.4 29.1 %copy-start.3 = (s32[128,10]{0,1:T(8,128)S(1)}, s32[128,10]{0,1:T(8,128)}, u32[]{:S(2)}) copy-start(s32[128,10]{0,1:T(8,128)} %param.27) | copy-start | bytes 15364
  107.3 22.2 %all-to-all-start = ((bf16[8,128,256]{2,1,0:T(8,128)(2,1)}), bf16[8,128,256]{2,1,0:T(8,128)(2,1)S(1)}, u32[]{:S(2)}, u32[]{:S(2)}) async-start(bf16[8,128,256]{2,1,0:T(8,128)(2,1)} %bitcast.174), calls=%async_computation | async-start | bytes 1048576 | tf_op jit(solution)/shard_map/all_to_all | solution.py:180
  129.5 16.0 %copy-start.6 = (f32[2048]{0:T(1024)S(1)}, f32[2048]{0:T(1024)}, u32[]{:S(2)}) copy-start(f32[2048]{0:T(1024)} %param.26) | copy-start | bytes 24580
  131.2 13.8 %all-to-all-start.1 = ((bf16[8,128,256]{2,1,0:T(8,128)(2,1)}), bf16[8,128,256]{2,1,0:T(8,128)(2,1)S(1)}, u32[]{:S(2)}, u32[]{:S(2)}) async-start(bf16[8,128,256]{2,1,0:T(8,128)(2,1)} %broadcast_in_dim.51), calls=%async_computation.1 | async-start | bytes 1048576 | tf_op jit(solution)/shard_map/all_to_all | solution.py:187
  147.6 74.3 %all-to-all-start.2 = ((bf16[16,20,2048]{2,1,0:T(8,128)(2,1)}), bf16[16,20,2048]{2,1,0:T(8,128)(2,1)}, u32[]{:S(2)}, u32[]{:S(2)}) async-start(bf16[16,20,2048]{2,1,0:T(8,128)(2,1)} %convolution_convert_fusion), calls=%async_computation.2 | async-start | bytes 3145728 | tf_op jit(solution)/shard_map/all_to_all | solution.py:218
  230.2 15.2 %copy-start.4 = (f32[128,10]{0,1:T(8,128)S(1)}, f32[128,10]{0,1:T(8,128)}, u32[]{:S(2)}) copy-start(f32[128,10]{0,1:T(8,128)} %param.28) | copy-start | bytes 15364
  230.2 88.1 %all-to-all-start.3 = ((bf16[128,20,256]{2,1,0:T(8,128)(2,1)}), bf16[128,20,256]{2,1,0:T(8,128)(2,1)}, u32[]{:S(2)}, u32[]{:S(2)}) async-start(bf16[128,20,256]{2,1,0:T(8,128)(2,1)} %bitcast.182), calls=%async_computation.3 | async-start | bytes 3145728 | tf_op jit(solution)/shard_map/all_to_all | solution.py:227

commit v9 on v8

--- a/solution.py
+++ b/solution.py
@@ -172,14 +172,16 @@
         * jax.nn.silu(gate_rows)
     )
     gated = gated.astype(jnp.bfloat16).reshape(length, head_count * DV)
-    attn_part = jnp.dot(gated, out_proj, preferred_element_type=jnp.float32)
     share_width = model_width // lax.axis_size("head")
     share_start = lax.axis_index("head") * share_width
     column_total = lax.axis_size("head")
-    attn_pieces = attn_part.astype(jnp.bfloat16).reshape(length, column_total, share_width)
-    attn_pieces = lax.all_to_all(
-        attn_pieces.transpose(1, 0, 2), "head", split_axis=0, concat_axis=0, tiled=True
-    )
+    attn_pieces = jnp.einsum(
+        "tk,kcd->ctd",
+        gated,
+        out_proj.reshape(out_proj.shape[0], column_total, share_width),
+        preferred_element_type=jnp.float32,
+    ).astype(jnp.bfloat16)
+    attn_pieces = lax.all_to_all(attn_pieces, "head", split_axis=0, concat_axis=0, tiled=True)
     attn_share = jnp.sum(attn_pieces.astype(jnp.float32), axis=0)
     stream_share = lax.dynamic_slice_in_dim(stream, share_start, share_width, 1)
     resid_share = (stream_share.astype(jnp.float32) + attn_share).astype(jnp.bfloat16)

time: 324 us -> 324 us (level)
  no operation moved by 1% of the time
where the time goes in v9:
time: 324 us; the launch traced here: 321 us
  waiting for transfers between devices  170 us (52%)
  starting transfers between devices  99 us (31%)
  matrix products  31.5 us (10%)
  local copies, waits for them, and re-layouts  13.7 us (4%)
  other arithmetic  5.41 us (2%)
    all_to_all x1, waiting for transfers between devices, on_device(): lax.all_to_all(sliced, ('seq', 'head'), split_axis=0, concat_axis=0, tile...  72.5 us
    all_to_all x1, waiting for transfers between devices, on_device(): lax.all_to_all(outgoing, 'seq', split_axis=0, concat_axis=0, tiled=True)  65.4 us
    ppermute x7, starting transfers between devices, on_device(): going_down = lax.ppermute(going_down, 'seq', backward_pairs)  43.7 us
    ppermute x8, starting transfers between devices, on_device(): going_up = lax.ppermute(going_up, 'seq', forward_pairs)  18.2 us
    all_to_all x1, starting transfers between devices, on_device(): lax.all_to_all(sliced, ('seq', 'head'), split_axis=0, concat_axis=0, tile...  14.7 us
    ppermute x8, waiting for transfers between devices, on_device(): going_up = lax.ppermute(going_up, 'seq', forward_pairs)  14 us
    all_to_all x1, starting transfers between devices, on_device(): lax.all_to_all(attn_pieces, 'head', split_axis=0, concat_axis=0, tiled=True)  12.8 us
    all_to_all x1, waiting for transfers between devices, on_device(): lax.all_to_all(attn_pieces, 'head', split_axis=0, concat_axis=0, tiled=True)  9.48 us
  transfers between devices with their start and end apart: 19, of which 11 were waited for; matrix products, arithmetic and copies ran while one was open for 5% of the time, Pallas kernels for 0%

profile of v9, /device:TPU:1, one launch (start us, length us, event | category | flops | bytes accessed | tf_op | source)
XLA Modules:
  0.0 320.9 jit_solution(15671337906649642976)
XLA Ops:
  15.0 4.8 %collective-permute-start = (bf16[8,128,128]{2,1,0:T(8,128)(2,1)}, bf16[8,128,128]{2,1,0:T(8,128)(2,1)S(1)}, u32[]{:S(2)}, u32[]{:S(2)}) collective-permute-start(bf16[8,128,128]{2,1,0:T(8,128)(2,1)} %pad_maximum_fusion), channel_id=1, source_target_pairs={{0,8},{8,16},{16,24},{24,32},{32,40},{40,48},{48,56},{56,64},{64,7... | collective-permute-start | bytes 786440 | tf_op jit(solution)/shard_map/ppermute | solution.py:148
  19.9 15.9 %collective-permute-start.8 = (bf16[8,128,128]{2,1,0:T(8,128)(2,1)}, bf16[8,128,128]{2,1,0:T(8,128)(2,1)}, u32[]{:S(2)}, u32[]{:S(2)}) collective-permute-start(bf16[8,128,128]{2,1,0:T(8,128)(2,1)} %pad_maximum_fusion), channel_id=1, source_target_pairs={{0,120},{8,0},{16,8},{24,16},{32,24},{40,32},{48,40},{56,48},{64,5... | collective-permute-start | bytes 786440 | tf_op jit(solution)/shard_map/ppermute | solution.py:159
  37.8 2.2 collective-permute-done
  40.0 1.9 collective-permute-start.1
  42.4 1.7 copy.247
  44.2 4.6 %collective-permute-start.9 = (bf16[8,128,128]{2,1,0:T(8,128)(2,1)}, bf16[8,128,128]{2,1,0:T(8,128)(2,1)S(1)}, u32[]{:S(2)}, u32[]{:S(2)}) collective-permute-start(bf16[8,128,128]{2,1,0:T(8,128)(2,1)} %collective-permute-done.8), channel_id=1, source_target_pairs={{0,120},{8,0},{16,8},{24,16},{32,24},{40,32},{48,40},{56,48},{64,5... | collective-permute-start | bytes 786440 | tf_op jit(solution)/shard_map/ppermute | solution.py:159
  51.2 1.9 collective-permute-start.2
  53.6 4.7 %collective-permute-start.10 = (bf16[8,128,128]{2,1,0:T(8,128)(2,1)S(1)}, bf16[8,128,128]{2,1,0:T(8,128)(2,1)S(1)}, u32[]{:S(2)}, u32[]{:S(2)}) collective-permute-start(bf16[8,128,128]{2,1,0:T(8,128)(2,1)S(1)} %collective-permute-done.9), channel_id=1, source_target_pairs={{0,120},{8,0},{16,8},{24,16},{32,24},{40,32},{48,40},{56,48},{64,5... | collective-permute-start | bytes 786440 | tf_op jit(solution)/shard_map/ppermute | solution.py:159
  58.6 1.9 collective-permute-done.2
  60.6 1.9 collective-permute-start.3
  63.1 4.6 %collective-permute-start.11 = (bf16[8,128,128]{2,1,0:T(8,128)(2,1)S(1)}, bf16[8,128,128]{2,1,0:T(8,128)(2,1)S(1)}, u32[]{:S(2)}, u32[]{:S(2)}) collective-permute-start(bf16[8,128,128]{2,1,0:T(8,128)(2,1)S(1)} %collective-permute-done.10), channel_id=1, source_target_pairs={{0,120},{8,0},{16,8},{24,16},{32,24},{40,32},{48,40},{56,48},{64,5... | collective-permute-start | bytes 786440 | tf_op jit(solution)/shard_map/ppermute | solution.py:159
  68.9 1.9 collective-permute-start.4
  71.5 4.8 %collective-permute-start.12 = (bf16[8,128,128]{2,1,0:T(8,128)(2,1)S(1)}, bf16[8,128,128]{2,1,0:T(8,128)(2,1)S(1)}, u32[]{:S(2)}, u32[]{:S(2)}) collective-permute-start(bf16[8,128,128]{2,1,0:T(8,128)(2,1)S(1)} %collective-permute-done.11), channel_id=1, source_target_pairs={{0,120},{8,0},{16,8},{24,16},{32,24},{40,32},{48,40},{56,48},{64,5... | collective-permute-start | bytes 786440 | tf_op jit(solution)/shard_map/ppermute | solution.py:159
  77.3 1.9 collective-permute-start.5
  79.8 4.6 %collective-permute-start.13 = (bf16[8,128,128]{2,1,0:T(8,128)(2,1)S(1)}, bf16[8,128,128]{2,1,0:T(8,128)(2,1)S(1)}, u32[]{:S(2)}, u32[]{:S(2)}) collective-permute-start(bf16[8,128,128]{2,1,0:T(8,128)(2,1)S(1)} %collective-permute-done.12), channel_id=1, source_target_pairs={{0,120},{8,0},{16,8},{24,16},{32,24},{40,32},{48,40},{56,48},{64,5... | collective-permute-start | bytes 786440 | tf_op jit(solution)/shard_map/ppermute | solution.py:159
  85.7 1.9 collective-permute-start.6
  88.2 4.6 %collective-permute-start.14 = (bf16[8,128,128]{2,1,0:T(8,128)(2,1)S(1)}, bf16[8,128,128]{2,1,0:T(8,128)(2,1)S(1)}, u32[]{:S(2)}, u32[]{:S(2)}) collective-permute-start(bf16[8,128,128]{2,1,0:T(8,128)(2,1)S(1)} %collective-permute-done.13), channel_id=1, source_target_pairs={{0,120},{8,0},{16,8},{24,16},{32,24},{40,32},{48,40},{56,48},{64,5... | collective-permute-start | bytes 786440 | tf_op jit(solution)/shard_map/ppermute | solution.py:159
  94.0 1.9 collective-permute-start.7
  96.9 6.6 %collective-permute-done.7 = bf16[8,128,128]{2,1,0:T(8,128)(2,1)S(1)} collective-permute-done((bf16[8,128,128]{2,1,0:T(8,128)(2,1)S(1)}, bf16[8,128,128]{2,1,0:T(8,128)(2,1)S(1)}, u32[]{:S(2)}, u32[]{:S(2)}) %collective-permute-start.7) | collective-permute-done | bytes 262176 | tf_op jit(solution)/shard_map/ppermute | solution.py:148
  107.2 12.8 %all-to-all-start = ((bf16[8,128,256]{2,1,0:T(8,128)(2,1)}), bf16[8,128,256]{2,1,0:T(8,128)(2,1)S(1)}, u32[]{:S(2)}, u32[]{:S(2)}) async-start(bf16[8,128,256]{2,1,0:T(8,128)(2,1)} %fusion.25), calls=%async_computation | async-start | bytes 1048576 | tf_op jit(solution)/shard_map/all_to_all | solution.py:184
  120.0 9.5 %all-to-all-done = bf16[8,128,256]{2,1,0:T(8,128)(2,1)S(1)} async-done(((bf16[8,128,256]{2,1,0:T(8,128)(2,1)}), bf16[8,128,256]{2,1,0:T(8,128)(2,1)S(1)}, u32[]{:S(2)}, u32[]{:S(2)}) %all-to-all-start) | async-done | bytes 524320 | tf_op jit(solution)/shard_map/all_to_all | solution.py:184
  131.3 4.3 %all-to-all-start.1 = ((bf16[8,128,256]{2,1,0:T(8,128)(2,1)}), bf16[8,128,256]{2,1,0:T(8,128)(2,1)S(1)}, u32[]{:S(2)}, u32[]{:S(2)}) async-start(bf16[8,128,256]{2,1,0:T(8,128)(2,1)} %broadcast_in_dim.51), calls=%async_computation.1 | async-start | bytes 1048576 | tf_op jit(solution)/shard_map/all_to_all | solution.py:189
  136.0 9.1 %all-to-all-done.1 = bf16[8,128,256]{2,1,0:T(8,128)(2,1)S(1)} async-done(((bf16[8,128,256]{2,1,0:T(8,128)(2,1)}), bf16[8,128,256]{2,1,0:T(8,128)(2,1)S(1)}, u32[]{:S(2)}, u32[]{:S(2)}) %all-to-all-start.1) | async-done | bytes 524320 | tf_op jit(solution)/shard_map/all_to_all | solution.py:189
  146.0 1.7 convolution_convert_fusion
  147.7 5.3 %all-to-all-start.2 = ((bf16[16,20,2048]{2,1,0:T(8,128)(2,1)}), bf16[16,20,2048]{2,1,0:T(8,128)(2,1)}, u32[]{:S(2)}, u32[]{:S(2)}) async-start(bf16[16,20,2048]{2,1,0:T(8,128)(2,1)} %convolution_convert_fusion), calls=%async_computation.2 | async-start | bytes 3145728 | tf_op jit(solution)/shard_map/all_to_all | solution.py:220
  153.0 3.6 %copy.268 = bf16[64,8,8,256]{3,2,1,0:T(8,128)(2,1)} copy(bf16[64,8,8,256]{3,1,2,0:T(8,128)(2,1)} %bitcast.184) | data formatting | bytes 4194304
  156.7 65.4 %all-to-all-done.2 = bf16[16,20,2048]{2,1,0:T(8,128)(2,1)} async-done(((bf16[16,20,2048]{2,1,0:T(8,128)(2,1)}), bf16[16,20,2048]{2,1,0:T(8,128)(2,1)}, u32[]{:S(2)}, u32[]{:S(2)}) %all-to-all-start.2) | async-done | bytes 1310752 | tf_op jit(solution)/shard_map/all_to_all | solution.py:220
  222.0 3.0 fusion.7
  225.1 5.2 %fusion.10 = bf16[16,20,8,256]{3,1,2,0:T(8,128)(2,1)} fusion(bf16[512,8,256]{2,1,0:T(8,128)(2,1)} %bitcast.185, bf16[16,20,2048]{2,1,0:T(8,128)(2,1)} %all-to-all-done.2, bf16[1,2048,512]{2,1,0:T(8,128)(2,1)S(1)} %copy-done, f32[16,20,512]{2,1,0:T(8,128)S(1)} %fusion.7), kind=kOutput, calls=%fused_computation.11 | convolution fusion | flops 1343815680 | bytes 7471104 | tf_op jit(solution)/shard_map/psh,hcd->pcsd/dot_general | solution.py:225
  230.2 14.7 %all-to-all-start.3 = ((bf16[128,20,256]{2,1,0:T(8,128)(2,1)}), bf16[128,20,256]{2,1,0:T(8,128)(2,1)}, u32[]{:S(2)}, u32[]{:S(2)}) async-start(bf16[128,20,256]{2,1,0:T(8,128)(2,1)} %bitcast.186), calls=%async_computation.3 | async-start | bytes 3145728 | tf_op jit(solution)/shard_map/all_to_all | solution.py:229
  245.9 72.5 %all-to-all-done.3 = bf16[128,20,256]{2,1,0:T(8,128)(2,1)} async-done(((bf16[128,20,256]{2,1,0:T(8,128)(2,1)}), bf16[128,20,256]{2,1,0:T(8,128)(2,1)}, u32[]{:S(2)}, u32[]{:S(2)}) %all-to-all-start.3) | async-done | bytes 1310752 | tf_op jit(solution)/shard_map/all_to_all | solution.py:229
  318.4 2.6 fusion.51
  (141 shorter events, 36.1 us)
Async XLA Ops:
  0.0 225.1 %copy-start = (bf16[1,2048,512]{2,1,0:T(8,128)(2,1)S(1)}, bf16[1,2048,512]{2,1,0:T(8,128)(2,1)}, u32[]{:S(2)}) copy-start(bf16[1,2048,512]{2,1,0:T(8,128)(2,1)} %param.30) | copy-start | bytes 6291460
  7.5 2.4 copy-start.5
  15.0 25.0 %collective-permute-start = (bf16[8,128,128]{2,1,0:T(8,128)(2,1)}, bf16[8,128,128]{2,1,0:T(8,128)(2,1)S(1)}, u32[]{:S(2)}, u32[]{:S(2)}) collective-permute-start(bf16[8,128,128]{2,1,0:T(8,128)(2,1)} %pad_maximum_fusion), channel_id=1, source_target_pairs={{0,8},{8,16},{16,24},{24,32},{32,40},{40,48},{48,56},{56,64},{64,7... | collective-permute-start | bytes 786440 | tf_op jit(solution)/shard_map/ppermute | solution.py:148
  19.9 24.3 %collective-permute-start.8 = (bf16[8,128,128]{2,1,0:T(8,128)(2,1)}, bf16[8,128,128]{2,1,0:T(8,128)(2,1)}, u32[]{:S(2)}, u32[]{:S(2)}) collective-permute-start(bf16[8,128,128]{2,1,0:T(8,128)(2,1)} %pad_maximum_fusion), channel_id=1, source_target_pairs={{0,120},{8,0},{16,8},{24,16},{32,24},{40,32},{48,40},{56,48},{64,5... | collective-permute-start | bytes 786440 | tf_op jit(solution)/shard_map/ppermute | solution.py:159
  40.0 10.1 %collective-permute-start.1 = (bf16[8,128,128]{2,1,0:T(8,128)(2,1)S(1)}, bf16[8,128,128]{2,1,0:T(8,128)(2,1)}, u32[]{:S(2)}, u32[]{:S(2)}) collective-permute-start(bf16[8,128,128]{2,1,0:T(8,128)(2,1)S(1)} %collective-permute-done), channel_id=1, source_target_pairs={{0,8},{8,16},{16,24},{24,32},{32,40},{40,48},{48,56},{56,64},{64,7... | collective-permute-start | bytes 786440 | tf_op jit(solution)/shard_map/ppermute | solution.py:148
  44.2 9.4 %collective-permute-start.9 = (bf16[8,128,128]{2,1,0:T(8,128)(2,1)}, bf16[8,128,128]{2,1,0:T(8,128)(2,1)S(1)}, u32[]{:S(2)}, u32[]{:S(2)}) collective-permute-start(bf16[8,128,128]{2,1,0:T(8,128)(2,1)} %collective-permute-done.8), channel_id=1, source_target_pairs={{0,120},{8,0},{16,8},{24,16},{32,24},{40,32},{48,40},{56,48},{64,5... | collective-permute-start | bytes 786440 | tf_op jit(solution)/shard_map/ppermute | solution.py:159
  51.2 9.3 %collective-permute-start.2 = (bf16[8,128,128]{2,1,0:T(8,128)(2,1)}, bf16[8,128,128]{2,1,0:T(8,128)(2,1)S(1)}, u32[]{:S(2)}, u32[]{:S(2)}) collective-permute-start(bf16[8,128,128]{2,1,0:T(8,128)(2,1)} %collective-permute-done.1), channel_id=1, source_target_pairs={{0,8},{8,16},{16,24},{24,32},{32,40},{40,48},{48,56},{56,64},{64,7... | collective-permute-start | bytes 786440 | tf_op jit(solution)/shard_map/ppermute | solution.py:148
  53.6 9.5 %collective-permute-start.10 = (bf16[8,128,128]{2,1,0:T(8,128)(2,1)S(1)}, bf16[8,128,128]{2,1,0:T(8,128)(2,1)S(1)}, u32[]{:S(2)}, u32[]{:S(2)}) collective-permute-start(bf16[8,128,128]{2,1,0:T(8,128)(2,1)S(1)} %collective-permute-done.9), channel_id=1, source_target_pairs={{0,120},{8,0},{16,8},{24,16},{32,24},{40,32},{48,40},{56,48},{64,5... | collective-permute-start | bytes 786440 | tf_op jit(solution)/shard_map/ppermute | solution.py:159
  60.6 8.3 %collective-permute-start.3 = (bf16[8,128,128]{2,1,0:T(8,128)(2,1)S(1)}, bf16[8,128,128]{2,1,0:T(8,128)(2,1)S(1)}, u32[]{:S(2)}, u32[]{:S(2)}) collective-permute-start(bf16[8,128,128]{2,1,0:T(8,128)(2,1)S(1)} %collective-permute-done.2), channel_id=1, source_target_pairs={{0,8},{8,16},{16,24},{24,32},{32,40},{40,48},{48,56},{56,64},{64,7... | collective-permute-start | bytes 786440 | tf_op jit(solution)/shard_map/ppermute | solution.py:148
  63.1 8.4 %collective-permute-start.11 = (bf16[8,128,128]{2,1,0:T(8,128)(2,1)S(1)}, bf16[8,128,128]{2,1,0:T(8,128)(2,1)S(1)}, u32[]{:S(2)}, u32[]{:S(2)}) collective-permute-start(bf16[8,128,128]{2,1,0:T(8,128)(2,1)S(1)} %collective-permute-done.10), channel_id=1, source_target_pairs={{0,120},{8,0},{16,8},{24,16},{32,24},{40,32},{48,40},{56,48},{64,5... | collective-permute-start | bytes 786440 | tf_op jit(solution)/shard_map/ppermute | solution.py:159
  68.9 8.3 %collective-permute-start.4 = (bf16[8,128,128]{2,1,0:T(8,128)(2,1)S(1)}, bf16[8,128,128]{2,1,0:T(8,128)(2,1)S(1)}, u32[]{:S(2)}, u32[]{:S(2)}) collective-permute-start(bf16[8,128,128]{2,1,0:T(8,128)(2,1)S(1)} %collective-permute-done.3), channel_id=1, source_target_pairs={{0,8},{8,16},{16,24},{24,32},{32,40},{40,48},{48,56},{56,64},{64,7... | collective-permute-start | bytes 786440 | tf_op jit(solution)/shard_map/ppermute | solution.py:148
  71.5 8.3 %collective-permute-start.12 = (bf16[8,128,128]{2,1,0:T(8,128)(2,1)S(1)}, bf16[8,128,128]{2,1,0:T(8,128)(2,1)S(1)}, u32[]{:S(2)}, u32[]{:S(2)}) collective-permute-start(bf16[8,128,128]{2,1,0:T(8,128)(2,1)S(1)} %collective-permute-done.11), channel_id=1, source_target_pairs={{0,120},{8,0},{16,8},{24,16},{32,24},{40,32},{48,40},{56,48},{64,5... | collective-permute-start | bytes 786440 | tf_op jit(solution)/shard_map/ppermute | solution.py:159
  77.3 8.3 %collective-permute-start.5 = (bf16[8,128,128]{2,1,0:T(8,128)(2,1)S(1)}, bf16[8,128,128]{2,1,0:T(8,128)(2,1)S(1)}, u32[]{:S(2)}, u32[]{:S(2)}) collective-permute-start(bf16[8,128,128]{2,1,0:T(8,128)(2,1)S(1)} %collective-permute-done.4), channel_id=1, source_target_pairs={{0,8},{8,16},{16,24},{24,32},{32,40},{40,48},{48,56},{56,64},{64,7... | collective-permute-start | bytes 786440 | tf_op jit(solution)/shard_map/ppermute | solution.py:148
  79.8 8.4 %collective-permute-start.13 = (bf16[8,128,128]{2,1,0:T(8,128)(2,1)S(1)}, bf16[8,128,128]{2,1,0:T(8,128)(2,1)S(1)}, u32[]{:S(2)}, u32[]{:S(2)}) collective-permute-start(bf16[8,128,128]{2,1,0:T(8,128)(2,1)S(1)} %collective-permute-done.12), channel_id=1, source_target_pairs={{0,120},{8,0},{16,8},{24,16},{32,24},{40,32},{48,40},{56,48},{64,5... | collective-permute-start | bytes 786440 | tf_op jit(solution)/shard_map/ppermute | solution.py:159
  85.7 8.3 %collective-permute-start.6 = (bf16[8,128,128]{2,1,0:T(8,128)(2,1)S(1)}, bf16[8,128,128]{2,1,0:T(8,128)(2,1)S(1)}, u32[]{:S(2)}, u32[]{:S(2)}) collective-permute-start(bf16[8,128,128]{2,1,0:T(8,128)(2,1)S(1)} %collective-permute-done.5), channel_id=1, source_target_pairs={{0,8},{8,16},{16,24},{24,32},{32,40},{40,48},{48,56},{56,64},{64,7... | collective-permute-start | bytes 786440 | tf_op jit(solution)/shard_map/ppermute | solution.py:148
  88.2 8.3 %collective-permute-start.14 = (bf16[8,128,128]{2,1,0:T(8,128)(2,1)S(1)}, bf16[8,128,128]{2,1,0:T(8,128)(2,1)S(1)}, u32[]{:S(2)}, u32[]{:S(2)}) collective-permute-start(bf16[8,128,128]{2,1,0:T(8,128)(2,1)S(1)} %collective-permute-done.13), channel_id=1, source_target_pairs={{0,120},{8,0},{16,8},{24,16},{32,24},{40,32},{48,40},{56,48},{64,5... | collective-permute-start | bytes 786440 | tf_op jit(solution)/shard_map/ppermute | solution.py:159
  94.0 9.4 %collective-permute-start.7 = (bf16[8,128,128]{2,1,0:T(8,128)(2,1)S(1)}, bf16[8,128,128]{2,1,0:T(8,128)(2,1)S(1)}, u32[]{:S(2)}, u32[]{:S(2)}) collective-permute-start(bf16[8,128,128]{2,1,0:T(8,128)(2,1)S(1)} %collective-permute-done.6), channel_id=1, source_target_pairs={{0,8},{8,16},{16,24},{24,32},{32,40},{40,48},{48,56},{56,64},{64,7... | collective-permute-start | bytes 786440 | tf_op jit(solution)/shard_map/ppermute | solution.py:148
  104.1 1.7 copy-start.2
  104.1 1.7 copy-start.7
  104.1 1.9 copy-start.1
  107.2 28.3 %copy-start.3 = (s32[128,10]{0,1:T(8,128)S(1)}, s32[128,10]{0,1:T(8,128)}, u32[]{:S(2)}) copy-start(s32[128,10]{0,1:T(8,128)} %param.27) | copy-start | bytes 15364
  107.2 22.3 %all-to-all-start = ((bf16[8,128,256]{2,1,0:T(8,128)(2,1)}), bf16[8,128,256]{2,1,0:T(8,128)(2,1)S(1)}, u32[]{:S(2)}, u32[]{:S(2)}) async-start(bf16[8,128,256]{2,1,0:T(8,128)(2,1)} %fusion.25), calls=%async_computation | async-start | bytes 1048576 | tf_op jit(solution)/shard_map/all_to_all | solution.py:184
  129.6 16.0 %copy-start.6 = (f32[2048]{0:T(1024)S(1)}, f32[2048]{0:T(1024)}, u32[]{:S(2)}) copy-start(f32[2048]{0:T(1024)} %param.26) | copy-start | bytes 24580
  131.3 13.8 %all-to-all-start.1 = ((bf16[8,128,256]{2,1,0:T(8,128)(2,1)}), bf16[8,128,256]{2,1,0:T(8,128)(2,1)S(1)}, u32[]{:S(2)}, u32[]{:S(2)}) async-start(bf16[8,128,256]{2,1,0:T(8,128)(2,1)} %broadcast_in_dim.51), calls=%async_computation.1 | async-start | bytes 1048576 | tf_op jit(solution)/shard_map/all_to_all | solution.py:189
  147.7 74.3 %all-to-all-start.2 = ((bf16[16,20,2048]{2,1,0:T(8,128)(2,1)}), bf16[16,20,2048]{2,1,0:T(8,128)(2,1)}, u32[]{:S(2)}, u32[]{:S(2)}) async-start(bf16[16,20,2048]{2,1,0:T(8,128)(2,1)} %convolution_convert_fusion), calls=%async_computation.2 | async-start | bytes 3145728 | tf_op jit(solution)/shard_map/all_to_all | solution.py:220
  230.2 15.2 %copy-start.4 = (f32[128,10]{0,1:T(8,128)S(1)}, f32[128,10]{0,1:T(8,128)}, u32[]{:S(2)}) copy-start(f32[128,10]{0,1:T(8,128)} %param.28) | copy-start | bytes 15364
  230.2 88.1 %all-to-all-start.3 = ((bf16[128,20,256]{2,1,0:T(8,128)(2,1)}), bf16[128,20,256]{2,1,0:T(8,128)(2,1)}, u32[]{:S(2)}, u32[]{:S(2)}) async-start(bf16[128,20,256]{2,1,0:T(8,128)(2,1)} %bitcast.186), calls=%async_computation.3 | async-start | bytes 3145728 | tf_op jit(solution)/shard_map/all_to_all | solution.py:229
